TPU v7x, 256 devices: a whole 4x4x8 slice. The times are simulated.
256 devices in a mesh: blk: 64 (over y, z, core), lev: 4 (over x).
Axes of the slice: x: 4, y: 4, z: 8, core: 2. Of those that a mesh axis runs over, the one named last changes fastest.
Arguments:
- adjoint_in: float32 [4096, 12, 1024], P('blk', 'lev'), may hold values from -6 to 6
- courant: float32 [2, 4096, 12, 1024], P(None, 'blk', 'lev'), may hold values from 0.05 to 0.45
- mixing: float32 [4096, 12, 1024], P('blk', 'lev'), may hold values from 0.5 to 8
- oh_rate: float32 [4096, 12, 1024], P('blk', 'lev'), may hold values from 0.02 to 0.6
- substeps: int32 [4096], P('blk'), may hold values from 1 to 4
- nest_weight: float32 [4096, 128], P('blk'), may hold values from 0.2 to 0.9
- dest_device: int32 [4096, 1], P('blk'), may hold values from 0 to 63; in each aligned block of 64 rows (0 to 63, 64 to 127, ...) at most 2 rows name the same one
- dest_slot: int32 [4096], P('blk'), may hold values from 0 to 63
- emission_profile: float32 [12], P('lev'), may hold values from 0.05 to 1
- tile_owner: int32 [4096], P('blk'), may hold values from 0 to 1023, as said below
Outputs:
- adjoint_out: float32 [4096, 12, 1024], P('blk', 'lev')
- tile_grad: float32 [1024, 1024], P(('blk', 'lev'))
Inputs may be any that keep to these rules, and one draw needn't show every extreme that they name: Of the 64 blocks of one index of blk, at most 2 have the same dest_device. Tiles form 64 groups of 16 consecutive tiles. Of the 64 blocks of one index of blk, at most 2 have tile_owner in the same group, and some group holds exactly 2 of them.
All inputs are finite; a program needn't handle non-finite values.
Results may differ from a plain program's by a relative error of at most 0.0003.
Values sent between devices are 32-bit elements; how exact they have to be, the bound alone decides.
No kernel may reach another device: no remote copies, remote signals or barrier semaphores. Data moves between devices by JAX's collectives and lax.ppermute only.
A program may use at most 128 MiB of HBM per device.

v0:
```python
import functools

import jax
import jax.numpy as jnp
from jax import lax
from jax.experimental import pallas as pl
from jax.experimental.pallas import tpu as pltpu
from jax.sharding import PartitionSpec as P

RMAX = 4
STEPS = 2
INTERPRET = False
HI = lax.Precision.HIGHEST


def solve_kernel(ep_ref, a_ref, s_ref, k_ref, x_ref, g_ref, r_ref):
    level_count = a_ref.shape[0]
    grad = ep_ref[0] * a_ref[0]
    for level in range(1, level_count):
        grad = grad + ep_ref[level] * a_ref[level]
    g_ref[...] = grad
    prev_ratio = None
    prev_scaled = None
    for level in range(level_count):
        right = a_ref[level] * s_ref[level]
        lower_k = k_ref[level - 1] if level > 0 else None
        upper_k = k_ref[level] if level < level_count - 1 else None
        if level == 0:
            pivot_val = 1.0 + upper_k
            scaled = right / pivot_val
        else:
            diag_term = 1.0 + lower_k if upper_k is None else 1.0 + lower_k + upper_k
            pivot_val = diag_term + lower_k * prev_ratio
            scaled = (right + lower_k * prev_scaled) / pivot_val
        x_ref[level] = scaled
        if upper_k is not None:
            prev_ratio = -upper_k / pivot_val
            r_ref[level] = prev_ratio
        prev_scaled = scaled
    solved = prev_scaled
    for level in range(level_count - 2, -1, -1):
        solved = x_ref[level] - r_ref[level] * solved
        x_ref[level] = solved


def column_solve(ep, adjoint, survive, mixing):
    level_count, blocks, cells = adjoint.shape
    chunk = 256
    spec = pl.BlockSpec((level_count, blocks, chunk), lambda c: (0, 0, c))
    return pl.pallas_call(
        solve_kernel,
        grid=(cells // chunk,),
        in_specs=[pl.BlockSpec(memory_space=pltpu.SMEM), spec, spec, spec],
        out_specs=[spec, pl.BlockSpec((blocks, chunk), lambda c: (0, c))],
        out_shape=[
            jax.ShapeDtypeStruct(adjoint.shape, jnp.float32),
            jax.ShapeDtypeStruct((blocks, cells), jnp.float32),
        ],
        scratch_shapes=[pltpu.VMEM((level_count, blocks, chunk), jnp.float32)],
        interpret=INTERPRET,
    )(ep, adjoint, survive, mixing)


def stencil_kernel(side_len, st_ref, v_ref, e_ref, n_ref, add_ref, o_ref):
    v = v_ref[...]
    east_c = e_ref[...]
    north_c = n_ref[...]
    cells = v.shape[1]
    lane = lax.broadcasted_iota(jnp.int32, v.shape, 1)
    east_ok = lane % side_len != side_len - 1
    north_ok = lane < cells - side_len
    keep = 1.0 - east_c - north_c
    steps = st_ref[...]
    for substep in range(RMAX):
        east_adj = jnp.where(east_ok, pltpu.roll(v, cells - 1, 1), 0.0)
        north_adj = jnp.where(north_ok, pltpu.roll(v, cells - side_len, 1), 0.0)
        moved = keep * v + east_c * east_adj + north_c * north_adj
        v = jnp.where(substep < steps, moved, v)
    o_ref[...] = v + add_ref[...]


def advect(side_len, steps, adjoint, east_c, north_c, added):
    rows, cells = adjoint.shape
    tile = 64
    spec = pl.BlockSpec((tile, cells), lambda r: (r, 0))
    return pl.pallas_call(
        functools.partial(stencil_kernel, side_len),
        grid=(rows // tile,),
        in_specs=[pl.BlockSpec((tile, 1), lambda r: (r, 0)), spec, spec, spec, spec],
        out_specs=spec,
        out_shape=jax.ShapeDtypeStruct(adjoint.shape, jnp.float32),
        interpret=INTERPRET,
    )(steps, adjoint, east_c, north_c, added)


def face_matrix(side_len, cells):
    pos = jnp.arange(side_len, dtype=jnp.int32)
    where = jnp.concatenate([pos, (side_len - 1) * side_len + pos, pos * side_len, pos * side_len + side_len - 1])
    return (jnp.arange(cells, dtype=jnp.int32)[:, None] == where[None, :]).astype(jnp.float32)


def pack_plan(keys, dest_count, cap):
    count = keys.shape[0]
    order = jnp.arange(count, dtype=jnp.int32)
    earlier = (keys[:, None] == keys[None, :]) & (order[None, :] < order[:, None])
    slot = keys * cap + jnp.sum(earlier.astype(jnp.int32), axis=1)
    rows = jnp.arange(dest_count * cap, dtype=jnp.int32)
    return (rows[:, None] == slot[None, :]).astype(jnp.float32)


def to_columns(x):
    return lax.all_to_all(x, "lev", split_axis=x.ndim - 2, concat_axis=x.ndim - 3, tiled=True)


def local(
    adjoint_in,
    courant,
    mixing,
    oh_rate,
    substeps,
    nest_weight,
    dest_device,
    dest_slot,
    emission_profile,
    tile_owner,
):
    blocks, lev_dev, cell_count = adjoint_in.shape
    cycle_len = nest_weight.shape[1]
    side_len = cycle_len // 4
    peer_count = lax.axis_size("blk")
    lev_groups = lax.axis_size("lev")
    lev_index = lax.axis_index("lev")
    own = blocks // lev_groups
    levels = lev_dev * lev_groups
    cap = 2

    state = to_columns(jnp.stack([adjoint_in, jnp.exp(-oh_rate), mixing]).transpose(0, 2, 1, 3))
    adjoint, survive, column_mixing = state[0], state[1], state[2]
    flows = to_columns(courant.transpose(0, 2, 1, 3)).reshape(2, levels * own, cell_count)
    ep = jnp.broadcast_to(emission_profile[:, None], (lev_dev, lev_groups))
    ep = lax.all_to_all(ep, "lev", split_axis=1, concat_axis=0, tiled=True).reshape(levels)

    own_steps = lax.dynamic_slice_in_dim(substeps, lev_index * own, own)
    row_steps = jnp.tile(own_steps, levels)[:, None]
    own_weight = lax.dynamic_slice_in_dim(nest_weight, lev_index * own, own)
    own_owner = lax.dynamic_slice_in_dim(tile_owner, lev_index * own, own)

    face_pack = pack_plan(dest_device[:, 0], peer_count, cap)
    tiles_total = blocks * peer_count // 4
    group_size = tiles_total // peer_count
    tile_pack = pack_plan(own_owner // group_size, peer_count, cap)
    info = jnp.stack(
        [
            jnp.dot(face_pack, (dest_slot + 1).astype(jnp.float32), precision=HI),
            jnp.dot(tile_pack, (own_owner % group_size + 1).astype(jnp.float32), precision=HI),
        ],
        axis=1,
    )
    info = lax.all_to_all(
        info.reshape(peer_count, cap, 2), "blk", split_axis=0, concat_axis=0, tiled=True
    ).reshape(peer_count * cap, 2)
    face_take = (
        info[:, 0][None, :] == (jnp.arange(blocks, dtype=jnp.int32) + 1).astype(jnp.float32)[:, None]
    ).astype(jnp.float32)
    tile_take = (
        info[:, 1][None, :] == (jnp.arange(group_size, dtype=jnp.int32) + 1).astype(jnp.float32)[:, None]
    ).astype(jnp.float32)

    pick = face_matrix(side_len, cell_count)
    grad_sum = jnp.zeros((own, cell_count), jnp.float32)
    for step_index in range(STEPS):
        solved, grad_step = column_solve(ep, adjoint, survive, column_mixing)
        grad_sum = grad_sum + grad_step
        flat = solved.reshape(levels * own, cell_count)
        cycle_out = jnp.dot(flat, pick, precision=HI).reshape(levels, own, cycle_len) * own_weight[None]
        by_level = lax.all_to_all(cycle_out, "lev", split_axis=0, concat_axis=1, tiled=True)
        sent = jnp.einsum("sb,lbk->slk", face_pack, by_level, precision=HI)
        sent = sent.reshape(peer_count, cap, lev_dev, cycle_len)
        got = lax.all_to_all(sent, "blk", split_axis=0, concat_axis=0, tiled=True)
        got = got.reshape(peer_count * cap, lev_dev, cycle_len)
        arrivals = jnp.einsum("ts,slk->ltk", face_take, got, precision=HI)
        arrivals = to_columns(arrivals).reshape(levels * own, cycle_len)
        added = jnp.dot(arrivals, pick.T, precision=HI)
        adjoint = advect(side_len, row_steps, flat, flows[0], flows[1], added).reshape(levels, own, cell_count)

    tile_sent = jnp.dot(tile_pack, grad_sum, precision=HI).reshape(peer_count, cap, cell_count)
    tile_got = lax.all_to_all(tile_sent, "blk", split_axis=0, concat_axis=0, tiled=True)
    tile_parts = jnp.dot(tile_take, tile_got.reshape(peer_count * cap, cell_count), precision=HI)
    tile_parts = lax.all_to_all(
        tile_parts.reshape(lev_groups, group_size // lev_groups, cell_count),
        "lev",
        split_axis=0,
        concat_axis=0,
        tiled=True,
    )
    tile_grad = jnp.sum(tile_parts, axis=0)
    adjoint_out = lax.all_to_all(adjoint, "lev", split_axis=0, concat_axis=1, tiled=True)
    return (adjoint_out.transpose(1, 0, 2), tile_grad)


def solution(mesh):
    placed = (
        P("blk", "lev", None),
        P(None, "blk", "lev", None),
        P("blk", "lev", None),
        P("blk", "lev", None),
        P("blk"),
        P("blk", None),
        P("blk", None),
        P("blk"),
        P("lev"),
        P("blk"),
    )
    return jax.shard_map(
        local,
        mesh=mesh,
        in_specs=placed,
        out_specs=(P("blk", "lev", None), P(("blk", "lev"), None)),
        check_vma=False,
    )
```

profile of v0, /device:TPU:8, one launch (start us, length us, event | category | flops | bytes accessed | tf_op | source)
XLA Modules:
  0.0 240.3 jit_solution(5233013616581540149)
XLA Ops:
  0.7 1.3 broadcast_in_dim.2
  2.0 4.3 %all-to-all-start = ((f32[3,4,1]{0,2,1:T(1,128)}), f32[3,4,1]{0,2,1:T(1,128)S(1)}, u32[]{:S(2)}, u32[]{:S(2)}) async-start(f32[3,4,1]{0,2,1:T(1,128)} %broadcast_in_dim.2), calls=%async_computation | async-start | bytes 4096 | tf_op jit(solution)/shard_map/all_to_all | solution.py:141
  6.3 1.2 negate_exponential_fusion
  7.5 1.7 copy.133
  9.2 1.1 copy_bitcast_fusion.3
  10.3 2.7 %maximum_bitcast_fusion = f32[3,3,64,1024]{3,1,0,2:T(4,128)} fusion(f32[1,64,3,1024]{3,2,0,1:T(4,128)S(1)} %get-tuple-element.20, f32[1,64,3,1024]{3,2,0,1:T(4,128)S(1)} %get-tuple-element.19, f32[1,64,3,1024]{3,2,0,1:T(4,128)S(1)} %bitcast.118), kind=kLoop, calls=%fused_computation | loop fusion | flops 1179648 | bytes 4718592 | tf_op jit(solution)/shard_map/transpose | solution.py:137
  13.0 4.9 %all-to-all-start.1 = ((f32[3,3,64,1024]{3,1,0,2:T(4,128)}), f32[3,3,64,1024]{3,1,0,2:T(4,128)S(1)}, u32[]{:S(2)}, u32[]{:S(2)}) async-start(f32[3,3,64,1024]{3,1,0,2:T(4,128)} %maximum_bitcast_fusion), calls=%async_computation.1 | async-start | bytes 6291456 | tf_op jit(solution)/shard_map/all_to_all | solution.py:112
  19.1 0.7 copy.108
  19.9 0.6 reshape.147.ep_ref
  20.5 34.5 %all-to-all-done.1 = f32[3,3,64,1024]{3,1,0,2:T(4,128)S(1)} async-done(((f32[3,3,64,1024]{3,1,0,2:T(4,128)}), f32[3,3,64,1024]{3,1,0,2:T(4,128)S(1)}, u32[]{:S(2)}, u32[]{:S(2)}) %all-to-all-start.1) | async-done | bytes 2359328 | tf_op jit(solution)/shard_map/all_to_all | solution.py:112
  55.0 12.1 %all-to-all-start.5 = ((f32[64,2,2]{1,2,0:T(2,128)}), f32[64,2,2]{1,2,0:T(2,128)S(1)}, u32[]{:S(2)}, u32[]{:S(2)}) async-start(f32[64,2,2]{1,2,0:T(2,128)} %copy.108), calls=%async_computation.5 | async-start | bytes 131072 | tf_op jit(solution)/shard_map/all_to_all | solution.py:159
  67.1 1.6 copy.130
  68.7 1.5 fusion.53
  70.2 4.0 %shard_map.113 = (f32[12,16,1024]{2,1,0:T(8,128)}, f32[16,1024]{1,0:T(8,128)}) custom-call(f32[12]{0:T(128)} %reshape.147.ep_ref, f32[12,16,1024]{2,1,0:T(8,128)} %bitcast.119, f32[12,16,1024]{2,1,0:T(8,128)} %bitcast.110, f32[12,16,1024]{2,1,0:T(8,128)} %bitcast.108), custom_call_target="tpu_custom_call" | custom-call | tf_op jit(solution)/shard_map/pallas_call | solution.py:50
  74.2 2.3 convolution_multiply_fusion.1
  76.5 3.3 %all-to-all-start.3 = ((f32[12,16,128]{2,1,0:T(8,128)}), f32[12,16,128]{2,1,0:T(8,128)S(1)}, u32[]{:S(2)}, u32[]{:S(2)}) async-start(f32[12,16,128]{2,1,0:T(8,128)} %convolution_multiply_fusion.1), calls=%async_computation.3 | async-start | bytes 196608 | tf_op jit(solution)/shard_map/all_to_all | solution.py:176
  79.8 2.4 copy.132
  82.2 3.4 %all-to-all-done.3 = f32[12,16,128]{2,1,0:T(8,128)S(1)} async-done(((f32[12,16,128]{2,1,0:T(8,128)}), f32[12,16,128]{2,1,0:T(8,128)S(1)}, u32[]{:S(2)}, u32[]{:S(2)}) %all-to-all-start.3) | async-done | bytes 98336 | tf_op jit(solution)/shard_map/all_to_all | solution.py:176
  85.6 3.6 %all-to-all-start.2 = ((f32[2,3,64,1024]{3,0,1,2:T(2,128)}), f32[2,3,64,1024]{3,0,1,2:T(2,128)S(1)}, u32[]{:S(2)}, u32[]{:S(2)}) async-start(f32[2,3,64,1024]{3,0,1,2:T(2,128)} %bitcast.104), calls=%async_computation.2 | async-start | bytes 3145728 | tf_op jit(solution)/shard_map/all_to_all | solution.py:112
  89.5 0.8 copy.106
  90.3 19.0 %all-to-all-done.2 = f32[2,3,64,1024]{3,0,1,2:T(2,128)S(1)} async-done(((f32[2,3,64,1024]{3,0,1,2:T(2,128)}), f32[2,3,64,1024]{3,0,1,2:T(2,128)S(1)}, u32[]{:S(2)}, u32[]{:S(2)}) %all-to-all-start.2) | async-done | bytes 1572896 | tf_op jit(solution)/shard_map/all_to_all | solution.py:112
  109.2 10.3 %all-to-all-start.4 = ((f32[64,2,3,128]{3,1,2,0:T(2,128)}), f32[64,2,3,128]{3,1,2,0:T(2,128)S(1)}, u32[]{:S(2)}, u32[]{:S(2)}) async-start(f32[64,2,3,128]{3,1,2,0:T(2,128)} %copy.106), calls=%async_computation.4 | async-start | bytes 393216 | tf_op jit(solution)/shard_map/all_to_all | solution.py:179
  119.7 0.7 broadcast_in_dim_tile.4.st_ref
  121.1 8.8 %all-to-all-done.4 = f32[64,2,3,128]{3,1,2,0:T(2,128)S(1)} async-done(((f32[64,2,3,128]{3,1,2,0:T(2,128)}), f32[64,2,3,128]{3,1,2,0:T(2,128)S(1)}, u32[]{:S(2)}, u32[]{:S(2)}) %all-to-all-start.4) | async-done | bytes 196640 | tf_op jit(solution)/shard_map/all_to_all | solution.py:179
  130.2 0.7 copy.110
  130.9 3.5 %all-to-all-start.6 = ((f32[3,64,128]{2,0,1:T(4,128)}), f32[3,64,128]{2,0,1:T(4,128)S(1)}, u32[]{:S(2)}, u32[]{:S(2)}) async-start(f32[3,64,128]{2,0,1:T(4,128)} %copy.110), calls=%async_computation.6 | async-start | bytes 262144 | tf_op jit(solution)/shard_map/all_to_all | solution.py:112
  134.5 1.3 fusion.54
  135.7 4.5 %all-to-all-done.6 = f32[3,64,128]{2,0,1:T(4,128)S(1)} async-done(((f32[3,64,128]{2,0,1:T(4,128)}), f32[3,64,128]{2,0,1:T(4,128)S(1)}, u32[]{:S(2)}, u32[]{:S(2)}) %all-to-all-start.6) | async-done | bytes 98336 | tf_op jit(solution)/shard_map/all_to_all | solution.py:112
  140.2 1.4 fusion.1.add_ref
  141.6 5.1 %shard_map.114 = f32[192,1024]{1,0:T(8,128)} custom-call(s32[192,1]{1,0:T(8,128)} %broadcast_in_dim_tile.4.st_ref, f32[192,1024]{1,0:T(8,128)} %bitcast.122, f32[192,1024]{1,0:T(8,128)} %bitcast.114, f32[192,1024]{1,0:T(8,128)} %bitcast.112, f32[192,1024]{1,0:T(8,128)} %fusion.1.add_ref), custom_call_target="tpu_custom_call" | custom-call | tf_op jit(solution)/shard_map/pallas_call | solution.py:86
  146.7 4.0 %shard_map.115 = (f32[12,16,1024]{2,1,0:T(8,128)}, f32[16,1024]{1,0:T(8,128)}) custom-call(f32[12]{0:T(128)} %reshape.147.ep_ref, f32[12,16,1024]{2,1,0:T(8,128)} %bitcast.121, f32[12,16,1024]{2,1,0:T(8,128)} %bitcast.111, f32[12,16,1024]{2,1,0:T(8,128)} %bitcast.109), custom_call_target="tpu_custom_call" | custom-call | tf_op jit(solution)/shard_map/pallas_call | solution.py:50
  150.7 1.7 convolution_multiply_fusion
  152.5 8.2 %all_to_all.152 = f32[12,16,128]{2,1,0:T(8,128)S(1)} all-to-all(f32[12,16,128]{2,1,0:T(8,128)S(1)} %convolution_multiply_fusion), channel_id=1, replica_groups=mesh['blk'=64,'lev'=4] {'lev'}, dimensions={0} | all-to-all | bytes 196608 | tf_op jit(solution)/shard_map/all_to_all | solution.py:176
  161.1 16.4 %all_to_all.153 = f32[64,2,3,128]{3,1,2,0:T(2,128)S(1)} all-to-all(f32[64,2,3,128]{3,1,2,0:T(2,128)S(1)} %copy.115), channel_id=1, replica_groups=mesh['blk'=64,'lev'=4] {'blk'}, dimensions={0} | all-to-all | bytes 393216 | tf_op jit(solution)/shard_map/all_to_all | solution.py:179
  177.8 0.7 copy.117
  178.6 3.3 %all-to-all-start.9 = ((f32[3,64,128]{2,0,1:T(4,128)}), f32[3,64,128]{2,0,1:T(4,128)S(1)}, u32[]{:S(2)}, u32[]{:S(2)}) async-start(f32[3,64,128]{2,0,1:T(4,128)} %copy.117), calls=%async_computation.9 | async-start | bytes 262144 | tf_op jit(solution)/shard_map/all_to_all | solution.py:112
  182.3 1.1 reshape.157
  183.4 4.5 %all-to-all-done.9 = f32[3,64,128]{2,0,1:T(4,128)S(1)} async-done(((f32[3,64,128]{2,0,1:T(4,128)}), f32[3,64,128]{2,0,1:T(4,128)S(1)}, u32[]{:S(2)}, u32[]{:S(2)}) %all-to-all-start.9) | async-done | bytes 98336 | tf_op jit(solution)/shard_map/all_to_all | solution.py:112
  187.8 6.3 %all-to-all-start.11 = ((f32[64,2,1024]{2,1,0:T(2,128)}), f32[64,2,1024]{2,1,0:T(2,128)S(1)}, u32[]{:S(2)}, u32[]{:S(2)}) async-start(f32[64,2,1024]{2,1,0:T(2,128)} %reshape.157), calls=%async_computation.11 | async-start | bytes 1048576 | tf_op jit(solution)/shard_map/all_to_all | solution.py:187
  194.2 16.6 %all-to-all-done.11 = f32[64,2,1024]{2,1,0:T(2,128)S(1)} async-done(((f32[64,2,1024]{2,1,0:T(2,128)}), f32[64,2,1024]{2,1,0:T(2,128)S(1)}, u32[]{:S(2)}, u32[]{:S(2)}) %all-to-all-start.11) | async-done | bytes 524320 | tf_op jit(solution)/shard_map/all_to_all | solution.py:187
  211.1 0.9 fusion.34
  212.1 3.3 %all-to-all-start.12 = ((f32[4,4,1024]{2,1,0:T(4,128)}), f32[4,4,1024]{2,1,0:T(4,128)S(1)}, u32[]{:S(2)}, u32[]{:S(2)}) async-start(f32[4,4,1024]{2,1,0:T(4,128)} %fusion.34), calls=%async_computation.12 | async-start | bytes 131072 | tf_op jit(solution)/shard_map/all_to_all | solution.py:189
  215.3 1.4 fusion.add_ref
  216.7 5.1 %shard_map.116 = f32[192,1024]{1,0:T(8,128)} custom-call(s32[192,1]{1,0:T(8,128)} %broadcast_in_dim_tile.4.st_ref, f32[192,1024]{1,0:T(8,128)} %bitcast.123, f32[192,1024]{1,0:T(8,128)} %bitcast.115, f32[192,1024]{1,0:T(8,128)} %bitcast.113, f32[192,1024]{1,0:T(8,128)} %fusion.add_ref), custom_call_target="tpu_custom_call" | custom-call | tf_op jit(solution)/shard_map/pallas_call | solution.py:86
  221.8 4.8 %all-to-all-start.10 = ((f32[12,16,1024]{2,1,0:T(8,128)}), f32[12,16,1024]{2,1,0:T(8,128)S(1)}, u32[]{:S(2)}, u32[]{:S(2)}) async-start(f32[12,16,1024]{2,1,0:T(8,128)} %bitcast.124), calls=%async_computation.10 | async-start | bytes 1572864 | tf_op jit(solution)/shard_map/all_to_all | solution.py:197
  226.6 0.6 reduce_sum.29
  227.2 12.2 %all-to-all-done.10 = f32[12,16,1024]{2,1,0:T(8,128)S(1)} async-done(((f32[12,16,1024]{2,1,0:T(8,128)}), f32[12,16,1024]{2,1,0:T(8,128)S(1)}, u32[]{:S(2)}, u32[]{:S(2)}) %all-to-all-start.10) | async-done | bytes 786464 | tf_op jit(solution)/shard_map/all_to_all | solution.py:197
  239.4 0.9 copy.121
  (61 shorter events, 4.1 us)
Async XLA Ops:
  0.6 19.3 %copy-start = (f32[64,128]{1,0:T(8,128)S(1)}, f32[64,128]{1,0:T(8,128)}, u32[]{:S(2)}) copy-start(f32[64,128]{1,0:T(8,128)} %param.15) | copy-start | bytes 98308
  0.6 8.5 %copy-start.2 = (f32[64,3,1024]{2,0,1:T(8,128)S(1)}, f32[64,3,1024]{2,0,1:T(8,128)}, u32[]{:S(2)}) copy-start(f32[64,3,1024]{2,0,1:T(8,128)} %param.12) | copy-start | bytes 2359300
  2.0 11.1 %all-to-all-start = ((f32[3,4,1]{0,2,1:T(1,128)}), f32[3,4,1]{0,2,1:T(1,128)S(1)}, u32[]{:S(2)}, u32[]{:S(2)}) async-start(f32[3,4,1]{0,2,1:T(1,128)} %broadcast_in_dim.2), calls=%async_computation | async-start | bytes 4096 | tf_op jit(solution)/shard_map/all_to_all | solution.py:141
  13.0 5.0 %copy-start.5 = (s32[64]{0:T(128)S(1)}, s32[64]{0:T(128)}, u32[]{:S(2)}) copy-start(s32[64]{0:T(128)} %param.19) | copy-start | bytes 772
  13.0 5.6 %copy-start.6 = (s32[64,1]{0,1:T(1,128)S(1)}, s32[64,1]{0,1:T(1,128)}, u32[]{:S(2)}) copy-start(s32[64,1]{0,1:T(1,128)} %param.16) | copy-start | bytes 772
  13.0 5.8 %copy-start.7 = (s32[64]{0:T(128)S(1)}, s32[64]{0:T(128)}, u32[]{:S(2)}) copy-start(s32[64]{0:T(128)} %param.17) | copy-start | bytes 772
  13.0 41.9 %all-to-all-start.1 = ((f32[3,3,64,1024]{3,1,0,2:T(4,128)}), f32[3,3,64,1024]{3,1,0,2:T(4,128)S(1)}, u32[]{:S(2)}, u32[]{:S(2)}) async-start(f32[3,3,64,1024]{3,1,0,2:T(4,128)} %maximum_bitcast_fusion), calls=%async_computation.1 | async-start | bytes 6291456 | tf_op jit(solution)/shard_map/all_to_all | solution.py:112
  55.0 21.5 %all-to-all-start.5 = ((f32[64,2,2]{1,2,0:T(2,128)}), f32[64,2,2]{1,2,0:T(2,128)S(1)}, u32[]{:S(2)}, u32[]{:S(2)}) async-start(f32[64,2,2]{1,2,0:T(2,128)} %copy.108), calls=%async_computation.5 | async-start | bytes 131072 | tf_op jit(solution)/shard_map/all_to_all | solution.py:159
  68.7 11.1 %copy-start.1 = (f32[2,64,3,1024]{3,1,2,0:T(8,128)S(1)}, f32[2,64,3,1024]{3,1,2,0:T(8,128)}, u32[]{:S(2)}) copy-start(f32[2,64,3,1024]{3,1,2,0:T(8,128)} %param.11) | copy-start | bytes 4718596
  76.5 9.1 %all-to-all-start.3 = ((f32[12,16,128]{2,1,0:T(8,128)}), f32[12,16,128]{2,1,0:T(8,128)S(1)}, u32[]{:S(2)}, u32[]{:S(2)}) async-start(f32[12,16,128]{2,1,0:T(8,128)} %convolution_multiply_fusion.1), calls=%async_computation.3 | async-start | bytes 196608 | tf_op jit(solution)/shard_map/all_to_all | solution.py:176
  79.8 39.8 %copy-start.8 = (s32[64]{0:T(128)S(1)}, s32[64]{0:T(128)}, u32[]{:S(2)}) copy-start(s32[64]{0:T(128)} %param.14) | copy-start | bytes 772
  85.6 23.7 %all-to-all-start.2 = ((f32[2,3,64,1024]{3,0,1,2:T(2,128)}), f32[2,3,64,1024]{3,0,1,2:T(2,128)S(1)}, u32[]{:S(2)}, u32[]{:S(2)}) async-start(f32[2,3,64,1024]{3,0,1,2:T(2,128)} %bitcast.104), calls=%async_computation.2 | async-start | bytes 3145728 | tf_op jit(solution)/shard_map/all_to_all | solution.py:112
  109.2 20.7 %all-to-all-start.4 = ((f32[64,2,3,128]{3,1,2,0:T(2,128)}), f32[64,2,3,128]{3,1,2,0:T(2,128)S(1)}, u32[]{:S(2)}, u32[]{:S(2)}) async-start(f32[64,2,3,128]{3,1,2,0:T(2,128)} %copy.106), calls=%async_computation.4 | async-start | bytes 393216 | tf_op jit(solution)/shard_map/all_to_all | solution.py:179
  130.9 9.3 %all-to-all-start.6 = ((f32[3,64,128]{2,0,1:T(4,128)}), f32[3,64,128]{2,0,1:T(4,128)S(1)}, u32[]{:S(2)}, u32[]{:S(2)}) async-start(f32[3,64,128]{2,0,1:T(4,128)} %copy.110), calls=%async_computation.6 | async-start | bytes 262144 | tf_op jit(solution)/shard_map/all_to_all | solution.py:112
  146.7 35.2 %copy-start.3 = (f32[16,1024]{1,0:T(8,128)S(1)}, f32[16,1024]{1,0:T(8,128)}, u32[]{:S(2)}) copy-start(f32[16,1024]{1,0:T(8,128)} %get-tuple-element.8) | copy-start | bytes 196612
  150.7 31.2 %copy-start.4 = (f32[16,1024]{1,0:T(8,128)S(1)}, f32[16,1024]{1,0:T(8,128)}, u32[]{:S(2)}) copy-start(f32[16,1024]{1,0:T(8,128)} %get-tuple-element.9) | copy-start | bytes 196612
  178.6 9.3 %all-to-all-start.9 = ((f32[3,64,128]{2,0,1:T(4,128)}), f32[3,64,128]{2,0,1:T(4,128)S(1)}, u32[]{:S(2)}, u32[]{:S(2)}) async-start(f32[3,64,128]{2,0,1:T(4,128)} %copy.117), calls=%async_computation.9 | async-start | bytes 262144 | tf_op jit(solution)/shard_map/all_to_all | solution.py:112
  187.8 22.9 %all-to-all-start.11 = ((f32[64,2,1024]{2,1,0:T(2,128)}), f32[64,2,1024]{2,1,0:T(2,128)S(1)}, u32[]{:S(2)}, u32[]{:S(2)}) async-start(f32[64,2,1024]{2,1,0:T(2,128)} %reshape.157), calls=%async_computation.11 | async-start | bytes 1048576 | tf_op jit(solution)/shard_map/all_to_all | solution.py:187
  212.1 9.8 %all-to-all-start.12 = ((f32[4,4,1024]{2,1,0:T(4,128)}), f32[4,4,1024]{2,1,0:T(4,128)S(1)}, u32[]{:S(2)}, u32[]{:S(2)}) async-start(f32[4,4,1024]{2,1,0:T(4,128)} %fusion.34), calls=%async_computation.12 | async-start | bytes 131072 | tf_op jit(solution)/shard_map/all_to_all | solution.py:189
  221.8 17.5 %all-to-all-start.10 = ((f32[12,16,1024]{2,1,0:T(8,128)}), f32[12,16,1024]{2,1,0:T(8,128)S(1)}, u32[]{:S(2)}, u32[]{:S(2)}) async-start(f32[12,16,1024]{2,1,0:T(8,128)} %bitcast.124), calls=%async_computation.10 | async-start | bytes 1572864 | tf_op jit(solution)/shard_map/all_to_all | solution.py:197
where the time goes:
time: 242 us; the launch traced here: 240 us
  waiting for transfers between devices  103 us (43%)
  starting transfers between devices  59.7 us (25%)
  blocking collectives  24.6 us (10%)
  local copies, waits for them, and re-layouts  19 us (8%)
  Pallas kernels  18.2 us (8%)
  matrix products  9.38 us (4%)
  other arithmetic  5.16 us (2%)
    all_to_all x4, waiting for transfers between devices, to_columns(): lax.all_to_all(x, 'lev', split_axis=x.ndim - 2, concat_axis=x.ndim - 3, t...  62.3 us
    all_to_all x1, waiting for transfers between devices, local(): lax.all_to_all(tile_sent, 'blk', split_axis=0, concat_axis=0, tiled=True)  16.6 us
    all_to_all x1, blocking collectives, local(): got = lax.all_to_all(sent, 'blk', split_axis=0, concat_axis=0, tiled=True)  16.4 us
    all_to_all x4, starting transfers between devices, to_columns(): lax.all_to_all(x, 'lev', split_axis=x.ndim - 2, concat_axis=x.ndim - 3, t...  15.3 us
    all_to_all x1, waiting for transfers between devices, local(): lax.all_to_all(adjoint, 'lev', split_axis=0, concat_axis=1, tiled=True)  12.2 us
    all_to_all x1, starting transfers between devices, local(): lax.all_to_all(info.reshape(peer_count, cap, 2), 'blk', split_axis=0, con...  12.1 us
    all_to_all x1, starting transfers between devices, local(): got = lax.all_to_all(sent, 'blk', split_axis=0, concat_axis=0, tiled=True)  10.3 us
    pallas_call x2, Pallas kernels, advect(): pl.pallas_call(functools.partial(stencil_kernel, side_len), grid=(rows //...  10.2 us
  transfers between devices with their start and end apart: 11, of which 8 were waited for; matrix products, arithmetic and copies ran while one was open for 10% of the time, Pallas kernels for 4%

commit v1 on v0

--- a/solution.py
+++ b/solution.py
@@ -156,15 +156,8 @@
         ],
         axis=1,
     )
-    info = lax.all_to_all(
-        info.reshape(peer_count, cap, 2), "blk", split_axis=0, concat_axis=0, tiled=True
-    ).reshape(peer_count * cap, 2)
-    face_take = (
-        info[:, 0][None, :] == (jnp.arange(blocks, dtype=jnp.int32) + 1).astype(jnp.float32)[:, None]
-    ).astype(jnp.float32)
-    tile_take = (
-        info[:, 1][None, :] == (jnp.arange(group_size, dtype=jnp.int32) + 1).astype(jnp.float32)[:, None]
-    ).astype(jnp.float32)
+    info = jnp.pad(info, ((0, 0), (0, cycle_len - 2))).reshape(peer_count, cap, cycle_len)
+    face_width = lev_dev * cycle_len
 
     pick = face_matrix(side_len, cell_count)
     grad_sum = jnp.zeros((own, cell_count), jnp.float32)
@@ -175,27 +168,45 @@
         cycle_out = jnp.dot(flat, pick, precision=HI).reshape(levels, own, cycle_len) * own_weight[None]
         by_level = lax.all_to_all(cycle_out, "lev", split_axis=0, concat_axis=1, tiled=True)
         sent = jnp.einsum("sb,lbk->slk", face_pack, by_level, precision=HI)
-        sent = sent.reshape(peer_count, cap, lev_dev, cycle_len)
+        sent = sent.reshape(peer_count, cap, face_width)
+        if step_index == 0:
+            sent = jnp.concatenate([sent, info], axis=2)
+        if step_index == STEPS - 1:
+            tile_sent = jnp.dot(tile_pack, grad_sum, precision=HI).reshape(peer_count, cap, cell_count)
+            sent = jnp.concatenate([sent, tile_sent], axis=2)
         got = lax.all_to_all(sent, "blk", split_axis=0, concat_axis=0, tiled=True)
-        got = got.reshape(peer_count * cap, lev_dev, cycle_len)
+        got = got.reshape(peer_count * cap, -1)
+        if step_index == 0:
+            face_take = (
+                got[:, face_width][None, :]
+                == (jnp.arange(blocks, dtype=jnp.int32) + 1).astype(jnp.float32)[:, None]
+            ).astype(jnp.float32)
+            tile_take = (
+                got[:, face_width + 1][None, :]
+                == (jnp.arange(group_size, dtype=jnp.int32) + 1).astype(jnp.float32)[:, None]
+            ).astype(jnp.float32)
+        if step_index == STEPS - 1:
+            tile_got = got[:, face_width:]
+        got = got[:, :face_width].reshape(peer_count * cap, lev_dev, cycle_len)
         arrivals = jnp.einsum("ts,slk->ltk", face_take, got, precision=HI)
         arrivals = to_columns(arrivals).reshape(levels * own, cycle_len)
         added = jnp.dot(arrivals, pick.T, precision=HI)
         adjoint = advect(side_len, row_steps, flat, flows[0], flows[1], added).reshape(levels, own, cell_count)
 
-    tile_sent = jnp.dot(tile_pack, grad_sum, precision=HI).reshape(peer_count, cap, cell_count)
-    tile_got = lax.all_to_all(tile_sent, "blk", split_axis=0, concat_axis=0, tiled=True)
-    tile_parts = jnp.dot(tile_take, tile_got.reshape(peer_count * cap, cell_count), precision=HI)
-    tile_parts = lax.all_to_all(
-        tile_parts.reshape(lev_groups, group_size // lev_groups, cell_count),
-        "lev",
-        split_axis=0,
-        concat_axis=0,
-        tiled=True,
-    )
-    tile_grad = jnp.sum(tile_parts, axis=0)
-    adjoint_out = lax.all_to_all(adjoint, "lev", split_axis=0, concat_axis=1, tiled=True)
-    return (adjoint_out.transpose(1, 0, 2), tile_grad)
+    tile_parts = jnp.dot(tile_take, tile_got, precision=HI)
+    tile_rows = group_size // lev_groups
+    packed = jnp.concatenate(
+        [
+            adjoint.reshape(lev_groups, lev_dev * own, cell_count),
+            tile_parts.reshape(lev_groups, tile_rows, cell_count),
+        ],
+        axis=1,
+    )
+    packed = lax.all_to_all(packed, "lev", split_axis=0, concat_axis=0, tiled=True)
+    tile_grad = jnp.sum(packed[:, lev_dev * own :], axis=0)
+    adjoint_out = packed[:, : lev_dev * own].reshape(lev_groups, lev_dev, own, cell_count)
+    adjoint_out = adjoint_out.transpose(0, 2, 1, 3).reshape(blocks, lev_dev, cell_count)
+    return (adjoint_out, tile_grad)
 
 
 def solution(mesh):

time: 242 us -> 220 us (0.909)
  starting transfers between devices: 59.7 us -> 44.8 us
  blocking collectives: 24.6 us -> 16.7 us
  waiting for transfers between devices: 103 us -> 99.7 us
  other arithmetic: 5.16 us -> 7.61 us
    all_to_all x4 -> x0, waiting for transfers between devices: 28.8 us -> none  [the longest x1 16.6 us: local(): lax.all_to_all(tile_sent, 'blk', split_axis=0, concat_axis=0, tiled=True)]
    all_to_all x4 -> x0, starting transfers between devices: 26.4 us -> none  [the longest x1 12.1 us: local(): lax.all_to_all(info.reshape(peer_count, cap, 2), 'blk', split_axis=0, con...]
    all_to_all x1 -> x2, waiting for transfers between devices: 8.83 us -> 30.7 us  [local(): got = lax.all_to_all(sent, 'blk', split_axis=0, concat_axis=0, tiled=True)]
    all_to_all x1 -> x2, starting transfers between devices: 10.3 us -> 18.6 us  [local(): got = lax.all_to_all(sent, 'blk', split_axis=0, concat_axis=0, tiled=True)]
    all_to_all x2 -> x1, blocking collectives: 24.6 us -> 16.7 us  [local(): lax.all_to_all(packed, 'lev', split_axis=0, concat_axis=0, tiled=True)]
    all_to_all x1 -> x2, waiting for transfers between devices: 3.35 us -> 9.82 us  [local(): lax.all_to_all(cycle_out, 'lev', split_axis=0, concat_axis=1, tiled=True)]
    all_to_all x1 -> x2, starting transfers between devices: 3.3 us -> 6.74 us  [local(): lax.all_to_all(cycle_out, 'lev', split_axis=0, concat_axis=1, tiled=True)]
    all_to_all x4, waiting for transfers between devices: 62.3 us -> 59.2 us  [to_columns(): lax.all_to_all(x, 'lev', split_axis=x.ndim - 2, concat_axis=x.ndim - 3, t...]
  transfers between devices with their start and end apart: 11 -> 9, of which waited for: 8 -> 8; matrix products, arithmetic and copies ran while one was open for 10% -> 8% of each run, Pallas kernels for 4% -> 0%
where the time goes in v1:
time: 220 us; the launch traced here: 218 us
  waiting for transfers between devices  99.7 us (45%)
  starting transfers between devices  44.8 us (20%)
  local copies, waits for them, and re-layouts  19.6 us (9%)
  Pallas kernels  18.3 us (8%)
  blocking collectives  16.7 us (8%)
  matrix products  10.4 us (5%)
  other arithmetic  7.61 us (3%)
    all_to_all x4, waiting for transfers between devices, to_columns(): lax.all_to_all(x, 'lev', split_axis=x.ndim - 2, concat_axis=x.ndim - 3, t...  59.2 us
    all_to_all x2, waiting for transfers between devices, local(): got = lax.all_to_all(sent, 'blk', split_axis=0, concat_axis=0, tiled=True)  30.7 us
    all_to_all x2, starting transfers between devices, local(): got = lax.all_to_all(sent, 'blk', split_axis=0, concat_axis=0, tiled=True)  18.6 us
    all_to_all x1, blocking collectives, local(): lax.all_to_all(packed, 'lev', split_axis=0, concat_axis=0, tiled=True)  16.7 us
    all_to_all x4, starting transfers between devices, to_columns(): lax.all_to_all(x, 'lev', split_axis=x.ndim - 2, concat_axis=x.ndim - 3, t...  15.2 us
    pallas_call x2, Pallas kernels, advect(): pl.pallas_call(functools.partial(stencil_kernel, side_len), grid=(rows //...  10.3 us
    all_to_all x2, waiting for transfers between devices, local(): lax.all_to_all(cycle_out, 'lev', split_axis=0, concat_axis=1, tiled=True)  9.82 us
    pallas_call x2, Pallas kernels, column_solve(): pl.pallas_call(solve_kernel, grid=(cells // chunk,), in_specs=[pl.BlockSp...  8 us
  transfers between devices with their start and end apart: 9, of which 8 were waited for; matrix products, arithmetic and copies ran while one was open for 8% of the time, Pallas kernels for 0%

profile of v1, /device:TPU:8, one launch (start us, length us, event | category | flops | bytes accessed | tf_op | source)
XLA Modules:
  0.0 218.1 jit_solution(607651391968932711)
XLA Ops:
  0.7 1.3 broadcast_in_dim.2
  2.0 4.3 %all-to-all-start = ((f32[3,4,1]{0,2,1:T(1,128)}), f32[3,4,1]{0,2,1:T(1,128)S(1)}, u32[]{:S(2)}, u32[]{:S(2)}) async-start(f32[3,4,1]{0,2,1:T(1,128)} %broadcast_in_dim.2), calls=%async_computation | async-start | bytes 4096 | tf_op jit(solution)/shard_map/all_to_all | solution.py:141
  6.3 1.2 negate_exponential_fusion
  7.5 1.7 copy.171
  9.2 1.1 copy_bitcast_fusion.3
  10.3 2.7 %maximum_bitcast_fusion = f32[3,3,64,1024]{3,1,0,2:T(4,128)} fusion(f32[1,64,3,1024]{3,2,0,1:T(4,128)S(1)} %get-tuple-element.20, f32[1,64,3,1024]{3,2,0,1:T(4,128)S(1)} %get-tuple-element.19, f32[1,64,3,1024]{3,2,0,1:T(4,128)S(1)} %bitcast.109), kind=kLoop, calls=%fused_computation | loop fusion | flops 1179648 | bytes 4718592 | tf_op jit(solution)/shard_map/transpose | solution.py:137
  13.0 4.8 %all-to-all-start.1 = ((f32[3,3,64,1024]{3,1,0,2:T(4,128)}), f32[3,3,64,1024]{3,1,0,2:T(4,128)S(1)}, u32[]{:S(2)}, u32[]{:S(2)}) async-start(f32[3,3,64,1024]{3,1,0,2:T(4,128)} %maximum_bitcast_fusion), calls=%async_computation.1 | async-start | bytes 6291456 | tf_op jit(solution)/shard_map/all_to_all | solution.py:112
  17.8 3.8 %copy.170 = f32[2,64,3,1024]{3,0,2,1:T(2,128)} copy(f32[2,64,3,1024]{3,1,2,0:T(8,128)} %param.11) | data formatting | bytes 3145728 | tf_op args[1]
  22.0 0.6 reshape.138.ep_ref
  22.6 32.2 %all-to-all-done.1 = f32[3,3,64,1024]{3,1,0,2:T(4,128)S(1)} async-done(((f32[3,3,64,1024]{3,1,0,2:T(4,128)}), f32[3,3,64,1024]{3,1,0,2:T(4,128)S(1)}, u32[]{:S(2)}, u32[]{:S(2)}) %all-to-all-start.1) | async-done | bytes 2359328 | tf_op jit(solution)/shard_map/all_to_all | solution.py:112
  54.8 1.6 copy.168
  56.5 1.5 fusion.52
  57.9 4.0 %shard_map.113 = (f32[12,16,1024]{2,1,0:T(8,128)}, f32[16,1024]{1,0:T(8,128)}) custom-call(f32[12]{0:T(128)} %reshape.138.ep_ref, f32[12,16,1024]{2,1,0:T(8,128)} %bitcast.110, f32[12,16,1024]{2,1,0:T(8,128)} %bitcast.101, f32[12,16,1024]{2,1,0:T(8,128)} %bitcast.99), custom_call_target="tpu_custom_call" | custom-call | tf_op jit(solution)/shard_map/pallas_call | solution.py:50
  61.9 2.3 %convolution_multiply_fusion.1 = f32[12,16,128]{2,1,0:T(8,128)} fusion(f32[12,16,1024]{2,1,0:T(8,128)} %get-tuple-element.6, s32[128]{0:T(128)S(1)} %pad_add_fusion, f32[16,128]{1,0:T(8,128)S(1)} %constant_dynamic-slice_fusion), kind=kOutput, calls=%fused_computation.7 | convolution fusion | flops 302145536 | bytes 893440 | tf_op jit(solution)/shard_map/dot_general | solution.py:168
  64.3 3.4 %all-to-all-start.3 = ((f32[12,16,128]{2,1,0:T(8,128)}), f32[12,16,128]{2,1,0:T(8,128)S(1)}, u32[]{:S(2)}, u32[]{:S(2)}) async-start(f32[12,16,128]{2,1,0:T(8,128)} %convolution_multiply_fusion.1), calls=%async_computation.3 | async-start | bytes 196608 | tf_op jit(solution)/shard_map/all_to_all | solution.py:169
  67.9 5.6 %all-to-all-done.3 = f32[12,16,128]{2,1,0:T(8,128)S(1)} async-done(((f32[12,16,128]{2,1,0:T(8,128)}), f32[12,16,128]{2,1,0:T(8,128)S(1)}, u32[]{:S(2)}, u32[]{:S(2)}) %all-to-all-start.3) | async-done | bytes 98336 | tf_op jit(solution)/shard_map/all_to_all | solution.py:169
  73.5 3.6 %all-to-all-start.2 = ((f32[2,3,64,1024]{3,0,1,2:T(2,128)}), f32[2,3,64,1024]{3,0,1,2:T(2,128)S(1)}, u32[]{:S(2)}, u32[]{:S(2)}) async-start(f32[2,3,64,1024]{3,0,1,2:T(2,128)} %bitcast.95), calls=%async_computation.2 | async-start | bytes 3145728 | tf_op jit(solution)/shard_map/all_to_all | solution.py:112
  78.1 0.9 copy.141
  79.0 16.2 %all-to-all-done.2 = f32[2,3,64,1024]{3,0,1,2:T(2,128)S(1)} async-done(((f32[2,3,64,1024]{3,0,1,2:T(2,128)}), f32[2,3,64,1024]{3,0,1,2:T(2,128)S(1)}, u32[]{:S(2)}, u32[]{:S(2)}) %all-to-all-start.2) | async-done | bytes 1572896 | tf_op jit(solution)/shard_map/all_to_all | solution.py:112
  95.1 12.1 %all-to-all-start.4 = ((f32[64,2,512]{2,1,0:T(2,128)}), f32[64,2,512]{2,1,0:T(2,128)S(1)}, u32[]{:S(2)}, u32[]{:S(2)}) async-start(f32[64,2,512]{2,1,0:T(2,128)} %copy.141), calls=%async_computation.4 | async-start | bytes 524288 | tf_op jit(solution)/shard_map/all_to_all | solution.py:177
  107.4 0.7 broadcast_in_dim_tile.4.st_ref
  108.1 0.5 copy.169
  108.6 10.2 %all-to-all-done.4 = f32[64,2,512]{2,1,0:T(2,128)S(1)} async-done(((f32[64,2,512]{2,1,0:T(2,128)}), f32[64,2,512]{2,1,0:T(2,128)S(1)}, u32[]{:S(2)}, u32[]{:S(2)}) %all-to-all-start.4) | async-done | bytes 262176 | tf_op jit(solution)/shard_map/all_to_all | solution.py:177
  119.6 0.7 copy.144
  120.3 3.5 %all-to-all-start.5 = ((f32[3,64,128]{2,0,1:T(4,128)}), f32[3,64,128]{2,0,1:T(4,128)S(1)}, u32[]{:S(2)}, u32[]{:S(2)}) async-start(f32[3,64,128]{2,0,1:T(4,128)} %copy.144), calls=%async_computation.5 | async-start | bytes 262144 | tf_op jit(solution)/shard_map/all_to_all | solution.py:112
  123.8 1.2 fusion.53
  125.1 4.5 %all-to-all-done.5 = f32[3,64,128]{2,0,1:T(4,128)S(1)} async-done(((f32[3,64,128]{2,0,1:T(4,128)}), f32[3,64,128]{2,0,1:T(4,128)S(1)}, u32[]{:S(2)}, u32[]{:S(2)}) %all-to-all-start.5) | async-done | bytes 98336 | tf_op jit(solution)/shard_map/all_to_all | solution.py:112
  129.6 1.4 fusion.3.add_ref
  131.0 5.2 %shard_map.114 = f32[192,1024]{1,0:T(8,128)} custom-call(s32[192,1]{1,0:T(8,128)} %broadcast_in_dim_tile.4.st_ref, f32[192,1024]{1,0:T(8,128)} %bitcast.114, f32[192,1024]{1,0:T(8,128)} %bitcast.105, f32[192,1024]{1,0:T(8,128)} %bitcast.103, f32[192,1024]{1,0:T(8,128)} %fusion.3.add_ref), custom_call_target="tpu_custom_call" | custom-call | tf_op jit(solution)/shard_map/pallas_call | solution.py:86
  136.2 4.0 %shard_map.115 = (f32[12,16,1024]{2,1,0:T(8,128)}, f32[16,1024]{1,0:T(8,128)}) custom-call(f32[12]{0:T(128)} %reshape.138.ep_ref, f32[12,16,1024]{2,1,0:T(8,128)} %bitcast.112, f32[12,16,1024]{2,1,0:T(8,128)} %bitcast.102, f32[12,16,1024]{2,1,0:T(8,128)} %bitcast.100), custom_call_target="tpu_custom_call" | custom-call | tf_op jit(solution)/shard_map/pallas_call | solution.py:50
  140.2 2.3 %convolution_multiply_fusion = f32[12,16,128]{2,1,0:T(8,128)} fusion(f32[12,16,1024]{2,1,0:T(8,128)} %get-tuple-element.7, s32[128]{0:T(128)S(1)} %pad_add_fusion, f32[16,128]{1,0:T(8,128)S(1)} %constant_dynamic-slice_fusion), kind=kOutput, calls=%fused_computation.5 | convolution fusion | flops 302145536 | bytes 893440 | tf_op jit(solution)/shard_map/dot_general | solution.py:168
  142.5 3.3 %all-to-all-start.6 = ((f32[12,16,128]{2,1,0:T(8,128)}), f32[12,16,128]{2,1,0:T(8,128)S(1)}, u32[]{:S(2)}, u32[]{:S(2)}) async-start(f32[12,16,128]{2,1,0:T(8,128)} %convolution_multiply_fusion), calls=%async_computation.6 | async-start | bytes 196608 | tf_op jit(solution)/shard_map/all_to_all | solution.py:169
  145.8 1.2 fusion.15
  147.0 0.3 reshape.146
  147.3 4.2 %all-to-all-done.6 = f32[12,16,128]{2,1,0:T(8,128)S(1)} async-done(((f32[12,16,128]{2,1,0:T(8,128)}), f32[12,16,128]{2,1,0:T(8,128)S(1)}, u32[]{:S(2)}, u32[]{:S(2)}) %all-to-all-start.6) | async-done | bytes 98336 | tf_op jit(solution)/shard_map/all_to_all | solution.py:169
  152.2 1.2 pad_maximum_fusion.1
  153.4 6.5 %all-to-all-start.7 = ((f32[64,2,1408]{2,1,0:T(2,128)}), f32[64,2,1408]{2,1,0:T(2,128)S(1)}, u32[]{:S(2)}, u32[]{:S(2)}) async-start(f32[64,2,1408]{2,1,0:T(2,128)} %pad_maximum_fusion.1), calls=%async_computation.7 | async-start | bytes 1441792 | tf_op jit(solution)/shard_map/all_to_all | solution.py:177
  159.8 20.5 %all-to-all-done.7 = f32[64,2,1408]{2,1,0:T(2,128)S(1)} async-done(((f32[64,2,1408]{2,1,0:T(2,128)}), f32[64,2,1408]{2,1,0:T(2,128)S(1)}, u32[]{:S(2)}, u32[]{:S(2)}) %all-to-all-start.7) | async-done | bytes 720928 | tf_op jit(solution)/shard_map/all_to_all | solution.py:177
  180.4 0.5 reshape.147
  181.3 0.7 copy.153
  182.0 3.3 %all-to-all-start.8 = ((f32[3,64,128]{2,0,1:T(4,128)}), f32[3,64,128]{2,0,1:T(4,128)S(1)}, u32[]{:S(2)}, u32[]{:S(2)}) async-start(f32[3,64,128]{2,0,1:T(4,128)} %copy.153), calls=%async_computation.8 | async-start | bytes 262144 | tf_op jit(solution)/shard_map/all_to_all | solution.py:112
  185.7 6.3 %all-to-all-done.8 = f32[3,64,128]{2,0,1:T(4,128)S(1)} async-done(((f32[3,64,128]{2,0,1:T(4,128)}), f32[3,64,128]{2,0,1:T(4,128)S(1)}, u32[]{:S(2)}, u32[]{:S(2)}) %all-to-all-start.8) | async-done | bytes 98336 | tf_op jit(solution)/shard_map/all_to_all | solution.py:112
  192.0 1.4 fusion.2.add_ref
  193.4 5.1 %shard_map.116 = f32[192,1024]{1,0:T(8,128)} custom-call(s32[192,1]{1,0:T(8,128)} %broadcast_in_dim_tile.4.st_ref, f32[192,1024]{1,0:T(8,128)} %bitcast.115, f32[192,1024]{1,0:T(8,128)} %bitcast.106, f32[192,1024]{1,0:T(8,128)} %bitcast.104, f32[192,1024]{1,0:T(8,128)} %fusion.2.add_ref), custom_call_target="tpu_custom_call" | custom-call | tf_op jit(solution)/shard_map/pallas_call | solution.py:86
  198.5 1.2 pad_maximum_fusion
  199.8 16.7 %all_to_all.124 = f32[4,52,1024]{2,1,0:T(8,128)S(1)} all-to-all(f32[4,52,1024]{2,1,0:T(8,128)S(1)} %pad_maximum_fusion), channel_id=1, replica_groups=mesh['blk'=64,'lev'=4] {'lev'}, dimensions={0} | all-to-all | bytes 1703936 | tf_op jit(solution)/shard_map/all_to_all | solution.py:205
  216.5 0.9 copy.157
  217.5 0.6 slice_reduce_fusion
  (62 shorter events, 3.8 us)
Async XLA Ops:
  0.6 21.2 %copy-start = (f32[64,128]{1,0:T(8,128)S(1)}, f32[64,128]{1,0:T(8,128)}, u32[]{:S(2)}) copy-start(f32[64,128]{1,0:T(8,128)} %param.15) | copy-start | bytes 98308
  0.6 8.5 %copy-start.1 = (f32[64,3,1024]{2,0,1:T(8,128)S(1)}, f32[64,3,1024]{2,0,1:T(8,128)}, u32[]{:S(2)}) copy-start(f32[64,3,1024]{2,0,1:T(8,128)} %param.12) | copy-start | bytes 2359300
  2.0 11.1 %all-to-all-start = ((f32[3,4,1]{0,2,1:T(1,128)}), f32[3,4,1]{0,2,1:T(1,128)S(1)}, u32[]{:S(2)}, u32[]{:S(2)}) async-start(f32[3,4,1]{0,2,1:T(1,128)} %broadcast_in_dim.2), calls=%async_computation | async-start | bytes 4096 | tf_op jit(solution)/shard_map/all_to_all | solution.py:141
  13.0 41.8 %all-to-all-start.1 = ((f32[3,3,64,1024]{3,1,0,2:T(4,128)}), f32[3,3,64,1024]{3,1,0,2:T(4,128)S(1)}, u32[]{:S(2)}, u32[]{:S(2)}) async-start(f32[3,3,64,1024]{3,1,0,2:T(4,128)} %maximum_bitcast_fusion), calls=%async_computation.1 | async-start | bytes 6291456 | tf_op jit(solution)/shard_map/all_to_all | solution.py:112
  17.8 3.9 %copy-start.3 = (s32[64]{0:T(128)S(1)}, s32[64]{0:T(128)}, u32[]{:S(2)}) copy-start(s32[64]{0:T(128)} %param.19) | copy-start | bytes 772
  56.5 11.2 %copy-start.4 = (s32[64,1]{0,1:T(1,128)S(1)}, s32[64,1]{0,1:T(1,128)}, u32[]{:S(2)}) copy-start(s32[64,1]{0,1:T(1,128)} %param.16) | copy-start | bytes 772
  57.9 19.2 %copy-start.5 = (s32[64]{0:T(128)S(1)}, s32[64]{0:T(128)}, u32[]{:S(2)}) copy-start(s32[64]{0:T(128)} %param.17) | copy-start | bytes 772
  64.3 43.0 %copy-start.6 = (s32[64]{0:T(128)S(1)}, s32[64]{0:T(128)}, u32[]{:S(2)}) copy-start(s32[64]{0:T(128)} %param.14) | copy-start | bytes 772
  64.3 9.2 %all-to-all-start.3 = ((f32[12,16,128]{2,1,0:T(8,128)}), f32[12,16,128]{2,1,0:T(8,128)S(1)}, u32[]{:S(2)}, u32[]{:S(2)}) async-start(f32[12,16,128]{2,1,0:T(8,128)} %convolution_multiply_fusion.1), calls=%async_computation.3 | async-start | bytes 196608 | tf_op jit(solution)/shard_map/all_to_all | solution.py:169
  73.5 21.7 %all-to-all-start.2 = ((f32[2,3,64,1024]{3,0,1,2:T(2,128)}), f32[2,3,64,1024]{3,0,1,2:T(2,128)S(1)}, u32[]{:S(2)}, u32[]{:S(2)}) async-start(f32[2,3,64,1024]{3,0,1,2:T(2,128)} %bitcast.95), calls=%async_computation.2 | async-start | bytes 3145728 | tf_op jit(solution)/shard_map/all_to_all | solution.py:112
  95.1 23.6 %all-to-all-start.4 = ((f32[64,2,512]{2,1,0:T(2,128)}), f32[64,2,512]{2,1,0:T(2,128)S(1)}, u32[]{:S(2)}, u32[]{:S(2)}) async-start(f32[64,2,512]{2,1,0:T(2,128)} %copy.141), calls=%async_computation.4 | async-start | bytes 524288 | tf_op jit(solution)/shard_map/all_to_all | solution.py:177
  120.3 9.3 %all-to-all-start.5 = ((f32[3,64,128]{2,0,1:T(4,128)}), f32[3,64,128]{2,0,1:T(4,128)S(1)}, u32[]{:S(2)}, u32[]{:S(2)}) async-start(f32[3,64,128]{2,0,1:T(4,128)} %copy.144), calls=%async_computation.5 | async-start | bytes 262144 | tf_op jit(solution)/shard_map/all_to_all | solution.py:112
  131.0 14.8 %copy-start.2 = (f32[16,1024]{1,0:T(8,128)S(1)}, f32[16,1024]{1,0:T(8,128)}, u32[]{:S(2)}) copy-start(f32[16,1024]{1,0:T(8,128)} %get-tuple-element.8) | copy-start | bytes 196612
  142.5 9.1 %all-to-all-start.6 = ((f32[12,16,128]{2,1,0:T(8,128)}), f32[12,16,128]{2,1,0:T(8,128)S(1)}, u32[]{:S(2)}, u32[]{:S(2)}) async-start(f32[12,16,128]{2,1,0:T(8,128)} %convolution_multiply_fusion), calls=%async_computation.6 | async-start | bytes 196608 | tf_op jit(solution)/shard_map/all_to_all | solution.py:169
  153.4 27.0 %all-to-all-start.7 = ((f32[64,2,1408]{2,1,0:T(2,128)}), f32[64,2,1408]{2,1,0:T(2,128)S(1)}, u32[]{:S(2)}, u32[]{:S(2)}) async-start(f32[64,2,1408]{2,1,0:T(2,128)} %pad_maximum_fusion.1), calls=%async_computation.7 | async-start | bytes 1441792 | tf_op jit(solution)/shard_map/all_to_all | solution.py:177
  182.0 10.0 %all-to-all-start.8 = ((f32[3,64,128]{2,0,1:T(4,128)}), f32[3,64,128]{2,0,1:T(4,128)S(1)}, u32[]{:S(2)}, u32[]{:S(2)}) async-start(f32[3,64,128]{2,0,1:T(4,128)} %copy.153), calls=%async_computation.8 | async-start | bytes 262144 | tf_op jit(solution)/shard_map/all_to_all | solution.py:112

commit v2 on v1

--- a/solution.py
+++ b/solution.py
@@ -112,6 +112,24 @@
     return lax.all_to_all(x, "lev", split_axis=x.ndim - 2, concat_axis=x.ndim - 3, tiled=True)
 
 
+def ring_columns(x, lev_index, lev_groups):
+    lead = x.shape[:-3]
+    lev_dev, blocks, cells = x.shape[-3:]
+    own = blocks // lev_groups
+    parts = x.reshape(lead + (lev_dev, lev_groups, own, cells))
+    got = []
+    for shift in range(lev_groups):
+        piece = lax.dynamic_index_in_dim(parts, (lev_index + shift) % lev_groups, axis=len(lead) + 1, keepdims=False)
+        if shift:
+            ring = [(src, (src + shift) % lev_groups) for src in range(lev_groups)]
+            piece = lax.ppermute(piece, "lev", ring)
+        got.append(piece)
+    got = jnp.stack(got, axis=len(lead))
+    order = (lev_index - jnp.arange(lev_groups, dtype=jnp.int32)) % lev_groups
+    got = jnp.take(got, order, axis=len(lead))
+    return got.reshape(lead + (lev_groups * lev_dev, own, cells))
+
+
 def local(
     adjoint_in,
     courant,
@@ -136,7 +154,7 @@
 
     state = to_columns(jnp.stack([adjoint_in, jnp.exp(-oh_rate), mixing]).transpose(0, 2, 1, 3))
     adjoint, survive, column_mixing = state[0], state[1], state[2]
-    flows = to_columns(courant.transpose(0, 2, 1, 3)).reshape(2, levels * own, cell_count)
+    flows = courant.transpose(0, 2, 1, 3)
     ep = jnp.broadcast_to(emission_profile[:, None], (lev_dev, lev_groups))
     ep = lax.all_to_all(ep, "lev", split_axis=1, concat_axis=0, tiled=True).reshape(levels)
 
@@ -163,6 +181,9 @@
     grad_sum = jnp.zeros((own, cell_count), jnp.float32)
     for step_index in range(STEPS):
         solved, grad_step = column_solve(ep, adjoint, survive, column_mixing)
+        if step_index == 0:
+            flows, solved = lax.optimization_barrier((flows, solved))
+            flows = ring_columns(flows, lev_index, lev_groups).reshape(2, levels * own, cell_count)
         grad_sum = grad_sum + grad_step
         flat = solved.reshape(levels * own, cell_count)
         cycle_out = jnp.dot(flat, pick, precision=HI).reshape(levels, own, cycle_len) * own_weight[None]

time: 220 us -> 200 us (0.909)
  waiting for transfers between devices: 99.7 us -> 81.8 us
  local copies, waits for them, and re-layouts: 19.6 us -> 15.9 us
    all_to_all x4 -> x3, waiting for transfers between devices: 59.2 us -> 46.7 us  [to_columns(): lax.all_to_all(x, 'lev', split_axis=x.ndim - 2, concat_axis=x.ndim - 3, t...]
    all_to_all x2, waiting for transfers between devices: 9.82 us -> 4.24 us  [local(): lax.all_to_all(cycle_out, 'lev', split_axis=0, concat_axis=1, tiled=True)]
    unnamed x17 -> x20, local copies, waits for them, and re-layouts: 5.61 us -> 0.7 us
    ppermute x0 -> x3, starting transfers between devices: none -> 4.89 us  [ring_columns(): piece = lax.ppermute(piece, 'lev', ring)]
    ppermute x0 -> x3, waiting for transfers between devices: none -> 3.5 us  [ring_columns(): piece = lax.ppermute(piece, 'lev', ring)]
    all_to_all x2, waiting for transfers between devices: 30.7 us -> 27.4 us  [local(): got = lax.all_to_all(sent, 'blk', split_axis=0, concat_axis=0, tiled=True)]
    all_to_all x4 -> x3, starting transfers between devices: 15.2 us -> 11.9 us  [to_columns(): lax.all_to_all(x, 'lev', split_axis=x.ndim - 2, concat_axis=x.ndim - 3, t...]
  transfers between devices with their start and end apart: 9 -> 11, of which waited for: 8 -> 8; matrix products, arithmetic and copies ran while one was open for 8% -> 7% of each run, Pallas kernels for 0% -> 0%
where the time goes in v2:
time: 200 us; the launch traced here: 199 us
  waiting for transfers between devices  81.8 us (41%)
  starting transfers between devices  46.3 us (23%)
  Pallas kernels  18.4 us (9%)
  blocking collectives  16.7 us (8%)
  local copies, waits for them, and re-layouts  15.9 us (8%)
  matrix products  10.4 us (5%)
  other arithmetic  8.11 us (4%)
    all_to_all x3, waiting for transfers between devices, to_columns(): lax.all_to_all(x, 'lev', split_axis=x.ndim - 2, concat_axis=x.ndim - 3, t...  46.7 us
    all_to_all x2, waiting for transfers between devices, local(): got = lax.all_to_all(sent, 'blk', split_axis=0, concat_axis=0, tiled=True)  27.4 us
    all_to_all x2, starting transfers between devices, local(): got = lax.all_to_all(sent, 'blk', split_axis=0, concat_axis=0, tiled=True)  18.6 us
    all_to_all x1, blocking collectives, local(): lax.all_to_all(packed, 'lev', split_axis=0, concat_axis=0, tiled=True)  16.7 us
    all_to_all x3, starting transfers between devices, to_columns(): lax.all_to_all(x, 'lev', split_axis=x.ndim - 2, concat_axis=x.ndim - 3, t...  11.9 us
    pallas_call x2, Pallas kernels, advect(): pl.pallas_call(functools.partial(stencil_kernel, side_len), grid=(rows //...  10.2 us
    pallas_call x2, Pallas kernels, column_solve(): pl.pallas_call(solve_kernel, grid=(cells // chunk,), in_specs=[pl.BlockSp...  8.13 us
    all_to_all x2, starting transfers between devices, local(): lax.all_to_all(cycle_out, 'lev', split_axis=0, concat_axis=1, tiled=True)  6.61 us
  transfers between devices with their start and end apart: 11, of which 8 were waited for; matrix products, arithmetic and copies ran while one was open for 7% of the time, Pallas kernels for 0%

profile of v2, /device:TPU:8, one launch (start us, length us, event | category | flops | bytes accessed | tf_op | source)
XLA Modules:
  0.0 198.6 jit_solution(6149529153929018279)
XLA Ops:
  0.7 1.3 broadcast_in_dim.9
  2.0 4.3 %all-to-all-start = ((f32[3,4,1]{0,2,1:T(1,128)}), f32[3,4,1]{0,2,1:T(1,128)S(1)}, u32[]{:S(2)}, u32[]{:S(2)}) async-start(f32[3,4,1]{0,2,1:T(1,128)} %broadcast_in_dim.9), calls=%async_computation | async-start | bytes 4096 | tf_op jit(solution)/shard_map/all_to_all | solution.py:159
  6.3 1.3 negate_exponential_fusion
  7.6 0.5 copy.155
  8.3 0.7 broadcast_in_dim_tile.4.st_ref
  9.5 1.1 copy_bitcast_fusion.1
  10.6 2.6 %maximum_bitcast_fusion = f32[3,3,64,1024]{3,1,0,2:T(4,128)} fusion(f32[1,64,3,1024]{3,2,0,1:T(4,128)S(1)} %get-tuple-element.28, f32[1,64,3,1024]{3,2,0,1:T(4,128)S(1)} %get-tuple-element.27, f32[1,64,3,1024]{3,2,0,1:T(4,128)S(1)} %bitcast.125), kind=kLoop, calls=%fused_computation.1 | loop fusion | flops 1179648 | bytes 4718592 | tf_op jit(solution)/shard_map/transpose | solution.py:155
  13.2 4.9 %all-to-all-start.1 = ((f32[3,3,64,1024]{3,1,0,2:T(4,128)}), f32[3,3,64,1024]{3,1,0,2:T(4,128)S(1)}, u32[]{:S(2)}, u32[]{:S(2)}) async-start(f32[3,3,64,1024]{3,1,0,2:T(4,128)} %maximum_bitcast_fusion), calls=%async_computation.1 | async-start | bytes 6291456 | tf_op jit(solution)/shard_map/all_to_all | solution.py:112
  18.9 0.6 reshape.194.ep_ref
  19.5 35.6 %all-to-all-done.1 = f32[3,3,64,1024]{3,1,0,2:T(4,128)S(1)} async-done(((f32[3,3,64,1024]{3,1,0,2:T(4,128)}), f32[3,3,64,1024]{3,1,0,2:T(4,128)S(1)}, u32[]{:S(2)}, u32[]{:S(2)}) %all-to-all-start.1) | async-done | bytes 2359328 | tf_op jit(solution)/shard_map/all_to_all | solution.py:112
  55.1 1.6 copy.154
  56.8 1.5 fusion.54
  58.2 4.1 %shard_map.113 = (f32[12,16,1024]{2,1,0:T(8,128)}, f32[16,1024]{1,0:T(8,128)}) custom-call(f32[12]{0:T(128)} %reshape.194.ep_ref, f32[12,16,1024]{2,1,0:T(8,128)} %bitcast.126, f32[12,16,1024]{2,1,0:T(8,128)} %bitcast.119, f32[12,16,1024]{2,1,0:T(8,128)} %bitcast.117), custom_call_target="tpu_custom_call" | custom-call | tf_op jit(solution)/shard_map/pallas_call | solution.py:50
  62.3 2.3 %convolution_multiply_fusion.1 = f32[12,16,128]{2,1,0:T(8,128)} fusion(f32[12,16,1024]{2,1,0:T(8,128)} %get-tuple-element.9, s32[128]{0:T(128)S(1)} %pad_add_fusion, f32[16,128]{1,0:T(8,128)S(1)} %constant_dynamic-slice_fusion), kind=kOutput, calls=%fused_computation.8 | convolution fusion | flops 302145536 | bytes 893440 | tf_op jit(solution)/shard_map/dot_general | solution.py:189
  64.7 3.3 %all-to-all-start.2 = ((f32[12,16,128]{2,1,0:T(8,128)}), f32[12,16,128]{2,1,0:T(8,128)S(1)}, u32[]{:S(2)}, u32[]{:S(2)}) async-start(f32[12,16,128]{2,1,0:T(8,128)} %convolution_multiply_fusion.1), calls=%async_computation.2 | async-start | bytes 196608 | tf_op jit(solution)/shard_map/all_to_all | solution.py:190
  68.0 1.1 dynamic-slice_bitcast_fusion.3
  69.1 3.2 %collective-permute-start.2 = (f32[2,3,16,1024]{3,2,1,0:T(8,128)}, f32[2,3,16,1024]{3,2,1,0:T(8,128)S(1)}, u32[]{:S(2)}, u32[]{:S(2)}) collective-permute-start(f32[2,3,16,1024]{3,2,1,0:T(8,128)} %get-tuple-element.26), channel_id=1, source_target_pairs={{0,3},{1,0},{2,1},{3,2},{4,7},{5,4},{6,5},{7,6},{8,11},{9,8},{10,9... | collective-permute-start | bytes 1179656 | tf_op jit(solution)/shard_map/ppermute | solution.py:125
  72.3 0.9 collective-permute-start.1
  73.1 0.9 collective-permute-start
  74.4 0.9 copy.125
  75.4 12.1 %all-to-all-start.3 = ((f32[64,2,512]{2,1,0:T(2,128)}), f32[64,2,512]{2,1,0:T(2,128)S(1)}, u32[]{:S(2)}, u32[]{:S(2)}) async-start(f32[64,2,512]{2,1,0:T(2,128)} %copy.125), calls=%async_computation.3 | async-start | bytes 524288 | tf_op jit(solution)/shard_map/all_to_all | solution.py:198
  87.7 3.3 %collective-permute-done = f32[2,3,16,1024]{3,2,1,0:T(8,128)S(1)} collective-permute-done((f32[2,3,16,1024]{3,2,1,0:T(8,128)}, f32[2,3,16,1024]{3,2,1,0:T(8,128)S(1)}, u32[]{:S(2)}, u32[]{:S(2)}) %collective-permute-start) | collective-permute-done | bytes 393248 | tf_op jit(solution)/shard_map/ppermute | solution.py:125
  91.2 0.7 gather_fusion
  92.1 6.9 %all-to-all-done.3 = f32[64,2,512]{2,1,0:T(2,128)S(1)} async-done(((f32[64,2,512]{2,1,0:T(2,128)}), f32[64,2,512]{2,1,0:T(2,128)S(1)}, u32[]{:S(2)}, u32[]{:S(2)}) %all-to-all-start.3) | async-done | bytes 262176 | tf_op jit(solution)/shard_map/all_to_all | solution.py:198
  99.8 0.7 copy.128
  100.5 3.6 %all-to-all-start.4 = ((f32[3,64,128]{2,0,1:T(4,128)}), f32[3,64,128]{2,0,1:T(4,128)S(1)}, u32[]{:S(2)}, u32[]{:S(2)}) async-start(f32[3,64,128]{2,0,1:T(4,128)} %copy.128), calls=%async_computation.4 | async-start | bytes 262144 | tf_op jit(solution)/shard_map/all_to_all | solution.py:112
  104.2 1.2 fusion.55
  105.4 4.7 %all-to-all-done.4 = f32[3,64,128]{2,0,1:T(4,128)S(1)} async-done(((f32[3,64,128]{2,0,1:T(4,128)}), f32[3,64,128]{2,0,1:T(4,128)S(1)}, u32[]{:S(2)}, u32[]{:S(2)}) %all-to-all-start.4) | async-done | bytes 98336 | tf_op jit(solution)/shard_map/all_to_all | solution.py:112
  110.2 1.4 fusion.3.add_ref
  111.6 5.1 %shard_map.114 = f32[192,1024]{1,0:T(8,128)} custom-call(s32[192,1]{1,0:T(8,128)} %broadcast_in_dim_tile.4.st_ref, f32[192,1024]{1,0:T(8,128)} %bitcast.130, f32[192,1024]{1,0:T(8,128)} %bitcast.123, f32[192,1024]{1,0:T(8,128)} %bitcast.121, f32[192,1024]{1,0:T(8,128)} %fusion.3.add_ref), custom_call_target="tpu_custom_call" | custom-call | tf_op jit(solution)/shard_map/pallas_call | solution.py:86
  116.7 4.0 %shard_map.115 = (f32[12,16,1024]{2,1,0:T(8,128)}, f32[16,1024]{1,0:T(8,128)}) custom-call(f32[12]{0:T(128)} %reshape.194.ep_ref, f32[12,16,1024]{2,1,0:T(8,128)} %bitcast.128, f32[12,16,1024]{2,1,0:T(8,128)} %bitcast.120, f32[12,16,1024]{2,1,0:T(8,128)} %bitcast.118), custom_call_target="tpu_custom_call" | custom-call | tf_op jit(solution)/shard_map/pallas_call | solution.py:50
  120.7 2.3 %convolution_multiply_fusion = f32[12,16,128]{2,1,0:T(8,128)} fusion(f32[12,16,1024]{2,1,0:T(8,128)} %get-tuple-element.11, s32[128]{0:T(128)S(1)} %pad_add_fusion, f32[16,128]{1,0:T(8,128)S(1)} %constant_dynamic-slice_fusion), kind=kOutput, calls=%fused_computation.6 | convolution fusion | flops 302145536 | bytes 893440 | tf_op jit(solution)/shard_map/dot_general | solution.py:189
  123.1 3.3 %all-to-all-start.5 = ((f32[12,16,128]{2,1,0:T(8,128)}), f32[12,16,128]{2,1,0:T(8,128)S(1)}, u32[]{:S(2)}, u32[]{:S(2)}) async-start(f32[12,16,128]{2,1,0:T(8,128)} %convolution_multiply_fusion), calls=%async_computation.5 | async-start | bytes 196608 | tf_op jit(solution)/shard_map/all_to_all | solution.py:190
  126.4 1.2 fusion.15
  127.9 4.2 %all-to-all-done.5 = f32[12,16,128]{2,1,0:T(8,128)S(1)} async-done(((f32[12,16,128]{2,1,0:T(8,128)}), f32[12,16,128]{2,1,0:T(8,128)S(1)}, u32[]{:S(2)}, u32[]{:S(2)}) %all-to-all-start.5) | async-done | bytes 98336 | tf_op jit(solution)/shard_map/all_to_all | solution.py:190
  132.7 1.2 pad_maximum_fusion.2
  133.9 6.5 %all-to-all-start.6 = ((f32[64,2,1408]{2,1,0:T(2,128)}), f32[64,2,1408]{2,1,0:T(2,128)S(1)}, u32[]{:S(2)}, u32[]{:S(2)}) async-start(f32[64,2,1408]{2,1,0:T(2,128)} %pad_maximum_fusion.2), calls=%async_computation.6 | async-start | bytes 1441792 | tf_op jit(solution)/shard_map/all_to_all | solution.py:198
  140.4 20.5 %all-to-all-done.6 = f32[64,2,1408]{2,1,0:T(2,128)S(1)} async-done(((f32[64,2,1408]{2,1,0:T(2,128)}), f32[64,2,1408]{2,1,0:T(2,128)S(1)}, u32[]{:S(2)}, u32[]{:S(2)}) %all-to-all-start.6) | async-done | bytes 720928 | tf_op jit(solution)/shard_map/all_to_all | solution.py:198
  160.9 0.5 reshape.204
  161.9 0.7 copy.137
  162.6 3.3 %all-to-all-start.7 = ((f32[3,64,128]{2,0,1:T(4,128)}), f32[3,64,128]{2,0,1:T(4,128)S(1)}, u32[]{:S(2)}, u32[]{:S(2)}) async-start(f32[3,64,128]{2,0,1:T(4,128)} %copy.137), calls=%async_computation.7 | async-start | bytes 262144 | tf_op jit(solution)/shard_map/all_to_all | solution.py:112
  166.3 6.3 %all-to-all-done.7 = f32[3,64,128]{2,0,1:T(4,128)S(1)} async-done(((f32[3,64,128]{2,0,1:T(4,128)}), f32[3,64,128]{2,0,1:T(4,128)S(1)}, u32[]{:S(2)}, u32[]{:S(2)}) %all-to-all-start.7) | async-done | bytes 98336 | tf_op jit(solution)/shard_map/all_to_all | solution.py:112
  172.6 1.4 fusion.2.add_ref
  174.0 5.1 %shard_map.116 = f32[192,1024]{1,0:T(8,128)} custom-call(s32[192,1]{1,0:T(8,128)} %broadcast_in_dim_tile.4.st_ref, f32[192,1024]{1,0:T(8,128)} %bitcast.131, f32[192,1024]{1,0:T(8,128)} %bitcast.124, f32[192,1024]{1,0:T(8,128)} %bitcast.122, f32[192,1024]{1,0:T(8,128)} %fusion.2.add_ref), custom_call_target="tpu_custom_call" | custom-call | tf_op jit(solution)/shard_map/pallas_call | solution.py:86
  179.1 1.2 pad_maximum_fusion.1
  180.3 16.7 %all_to_all.109 = f32[4,52,1024]{2,1,0:T(8,128)S(1)} all-to-all(f32[4,52,1024]{2,1,0:T(8,128)S(1)} %pad_maximum_fusion.1), channel_id=1, replica_groups=mesh['blk'=64,'lev'=4] {'lev'}, dimensions={0} | all-to-all | bytes 1703936 | tf_op jit(solution)/shard_map/all_to_all | solution.py:226
  197.1 0.9 copy.141
  198.0 0.6 slice_reduce_fusion
  (75 shorter events, 4.9 us)
Async XLA Ops:
  0.6 18.2 %copy-start = (f32[64,128]{1,0:T(8,128)S(1)}, f32[64,128]{1,0:T(8,128)}, u32[]{:S(2)}) copy-start(f32[64,128]{1,0:T(8,128)} %param.15) | copy-start | bytes 98308
  0.6 7.0 %copy-start.2 = (f32[64,3,1024]{2,0,1:T(8,128)S(1)}, f32[64,3,1024]{2,0,1:T(8,128)}, u32[]{:S(2)}) copy-start(f32[64,3,1024]{2,0,1:T(8,128)} %param.10) | copy-start | bytes 2359300
  2.0 11.2 %all-to-all-start = ((f32[3,4,1]{0,2,1:T(1,128)}), f32[3,4,1]{0,2,1:T(1,128)S(1)}, u32[]{:S(2)}, u32[]{:S(2)}) async-start(f32[3,4,1]{0,2,1:T(1,128)} %broadcast_in_dim.9), calls=%async_computation | async-start | bytes 4096 | tf_op jit(solution)/shard_map/all_to_all | solution.py:159
  6.3 1.9 copy-start.6
  6.3 2.7 %copy-start.5 = (s32[64]{0:T(128)S(1)}, s32[64]{0:T(128)}, u32[]{:S(2)}) copy-start(s32[64]{0:T(128)} %param.19) | copy-start | bytes 772
  6.3 3.0 %copy-start.7 = (s32[64,1]{0,1:T(1,128)S(1)}, s32[64,1]{0,1:T(1,128)}, u32[]{:S(2)}) copy-start(s32[64,1]{0,1:T(1,128)} %param.16) | copy-start | bytes 772
  6.3 3.2 %copy-start.3 = (f32[64,3,1024]{2,0,1:T(8,128)S(1)}, f32[64,3,1024]{2,0,1:T(8,128)}, u32[]{:S(2)}) copy-start(f32[64,3,1024]{2,0,1:T(8,128)} %param.12) | copy-start | bytes 2359300
  13.2 5.1 %copy-start.8 = (s32[64]{0:T(128)S(1)}, s32[64]{0:T(128)}, u32[]{:S(2)}) copy-start(s32[64]{0:T(128)} %param.17) | copy-start | bytes 772
  13.2 41.9 %all-to-all-start.1 = ((f32[3,3,64,1024]{3,1,0,2:T(4,128)}), f32[3,3,64,1024]{3,1,0,2:T(4,128)S(1)}, u32[]{:S(2)}, u32[]{:S(2)}) async-start(f32[3,3,64,1024]{3,1,0,2:T(4,128)} %maximum_bitcast_fusion), calls=%async_computation.1 | async-start | bytes 6291456 | tf_op jit(solution)/shard_map/all_to_all | solution.py:112
  58.2 9.7 %copy-start.1 = (f32[2,64,3,1024]{3,1,2,0:T(8,128)S(1)}, f32[2,64,3,1024]{3,1,2,0:T(8,128)}, u32[]{:S(2)}) copy-start(f32[2,64,3,1024]{3,1,2,0:T(8,128)} %param.11) | copy-start | bytes 4718596
  64.7 9.3 %all-to-all-start.2 = ((f32[12,16,128]{2,1,0:T(8,128)}), f32[12,16,128]{2,1,0:T(8,128)S(1)}, u32[]{:S(2)}, u32[]{:S(2)}) async-start(f32[12,16,128]{2,1,0:T(8,128)} %convolution_multiply_fusion.1), calls=%async_computation.2 | async-start | bytes 196608 | tf_op jit(solution)/shard_map/all_to_all | solution.py:190
  69.1 18.6 %collective-permute-start.2 = (f32[2,3,16,1024]{3,2,1,0:T(8,128)}, f32[2,3,16,1024]{3,2,1,0:T(8,128)S(1)}, u32[]{:S(2)}, u32[]{:S(2)}) collective-permute-start(f32[2,3,16,1024]{3,2,1,0:T(8,128)} %get-tuple-element.26), channel_id=1, source_target_pairs={{0,3},{1,0},{2,1},{3,2},{4,7},{5,4},{6,5},{7,6},{8,11},{9,8},{10,9... | collective-permute-start | bytes 1179656 | tf_op jit(solution)/shard_map/ppermute | solution.py:125
  72.3 15.4 %collective-permute-start.1 = (f32[2,3,16,1024]{3,2,1,0:T(8,128)}, f32[2,3,16,1024]{3,2,1,0:T(8,128)S(1)}, u32[]{:S(2)}, u32[]{:S(2)}) collective-permute-start(f32[2,3,16,1024]{3,2,1,0:T(8,128)} %get-tuple-element.24), channel_id=1, source_target_pairs={{0,2},{1,3},{2,0},{3,1},{4,6},{5,7},{6,4},{7,5},{8,10},{9,11},{10,... | collective-permute-start | bytes 1179656 | tf_op jit(solution)/shard_map/ppermute | solution.py:125
  73.1 17.9 %collective-permute-start = (f32[2,3,16,1024]{3,2,1,0:T(8,128)}, f32[2,3,16,1024]{3,2,1,0:T(8,128)S(1)}, u32[]{:S(2)}, u32[]{:S(2)}) collective-permute-start(f32[2,3,16,1024]{3,2,1,0:T(8,128)} %get-tuple-element.25), channel_id=1, source_target_pairs={{0,1},{1,2},{2,3},{3,0},{4,5},{5,6},{6,7},{7,4},{8,9},{9,10},{10,1... | collective-permute-start | bytes 1179656 | tf_op jit(solution)/shard_map/ppermute | solution.py:125
  75.4 23.6 %all-to-all-start.3 = ((f32[64,2,512]{2,1,0:T(2,128)}), f32[64,2,512]{2,1,0:T(2,128)S(1)}, u32[]{:S(2)}, u32[]{:S(2)}) async-start(f32[64,2,512]{2,1,0:T(2,128)} %copy.125), calls=%async_computation.3 | async-start | bytes 524288 | tf_op jit(solution)/shard_map/all_to_all | solution.py:198
  100.5 9.6 %all-to-all-start.4 = ((f32[3,64,128]{2,0,1:T(4,128)}), f32[3,64,128]{2,0,1:T(4,128)S(1)}, u32[]{:S(2)}, u32[]{:S(2)}) async-start(f32[3,64,128]{2,0,1:T(4,128)} %copy.128), calls=%async_computation.4 | async-start | bytes 262144 | tf_op jit(solution)/shard_map/all_to_all | solution.py:112
  116.7 9.7 %copy-start.4 = (f32[16,1024]{1,0:T(8,128)S(1)}, f32[16,1024]{1,0:T(8,128)}, u32[]{:S(2)}) copy-start(f32[16,1024]{1,0:T(8,128)} %get-tuple-element.12) | copy-start | bytes 196612
  123.1 9.1 %all-to-all-start.5 = ((f32[12,16,128]{2,1,0:T(8,128)}), f32[12,16,128]{2,1,0:T(8,128)S(1)}, u32[]{:S(2)}, u32[]{:S(2)}) async-start(f32[12,16,128]{2,1,0:T(8,128)} %convolution_multiply_fusion), calls=%async_computation.5 | async-start | bytes 196608 | tf_op jit(solution)/shard_map/all_to_all | solution.py:190
  133.9 27.0 %all-to-all-start.6 = ((f32[64,2,1408]{2,1,0:T(2,128)}), f32[64,2,1408]{2,1,0:T(2,128)S(1)}, u32[]{:S(2)}, u32[]{:S(2)}) async-start(f32[64,2,1408]{2,1,0:T(2,128)} %pad_maximum_fusion.2), calls=%async_computation.6 | async-start | bytes 1441792 | tf_op jit(solution)/shard_map/all_to_all | solution.py:198
  162.6 10.0 %all-to-all-start.7 = ((f32[3,64,128]{2,0,1:T(4,128)}), f32[3,64,128]{2,0,1:T(4,128)S(1)}, u32[]{:S(2)}, u32[]{:S(2)}) async-start(f32[3,64,128]{2,0,1:T(4,128)} %copy.137), calls=%async_computation.7 | async-start | bytes 262144 | tf_op jit(solution)/shard_map/all_to_all | solution.py:112

commit v3 on v2

--- a/solution.py
+++ b/solution.py
@@ -13,16 +13,12 @@
 HI = lax.Precision.HIGHEST
 
 
-def solve_kernel(ep_ref, a_ref, s_ref, k_ref, x_ref, g_ref, r_ref):
-    level_count = a_ref.shape[0]
-    grad = ep_ref[0] * a_ref[0]
-    for level in range(1, level_count):
-        grad = grad + ep_ref[level] * a_ref[level]
-    g_ref[...] = grad
+def eliminate(right_of, k_ref, x_ref, r_ref):
+    level_count = k_ref.shape[0]
     prev_ratio = None
     prev_scaled = None
     for level in range(level_count):
-        right = a_ref[level] * s_ref[level]
+        right = right_of(level)
         lower_k = k_ref[level - 1] if level > 0 else None
         upper_k = k_ref[level] if level < level_count - 1 else None
         if level == 0:
@@ -43,20 +39,42 @@
         x_ref[level] = solved
 
 
-def column_solve(ep, adjoint, survive, mixing):
-    level_count, blocks, cells = adjoint.shape
+def first_kernel(b_ref, k_ref, x_ref, r_ref):
+    eliminate(lambda level: b_ref[level], k_ref, x_ref, r_ref)
+
+
+def next_kernel(ep_ref, a_ref, s_ref, k_ref, x_ref, g_ref, r_ref):
+    level_count = a_ref.shape[0]
+    grad = ep_ref[0] * a_ref[0]
+    for level in range(1, level_count):
+        grad = grad + ep_ref[level] * a_ref[level]
+    g_ref[...] = grad
+    eliminate(lambda level: a_ref[level] * s_ref[level], k_ref, x_ref, r_ref)
+
+
+def column_solve(mixing, right=None, ep=None, adjoint=None, survive=None):
+    level_count, blocks, cells = mixing.shape
     chunk = 256
     spec = pl.BlockSpec((level_count, blocks, chunk), lambda c: (0, 0, c))
+    scratch = [pltpu.VMEM((level_count, blocks, chunk), jnp.float32)]
+    solved_shape = jax.ShapeDtypeStruct(mixing.shape, jnp.float32)
+    if right is not None:
+        return pl.pallas_call(
+            first_kernel,
+            grid=(cells // chunk,),
+            in_specs=[spec, spec],
+            out_specs=spec,
+            out_shape=solved_shape,
+            scratch_shapes=scratch,
+            interpret=INTERPRET,
+        )(right, mixing)
     return pl.pallas_call(
-        solve_kernel,
+        next_kernel,
         grid=(cells // chunk,),
         in_specs=[pl.BlockSpec(memory_space=pltpu.SMEM), spec, spec, spec],
         out_specs=[spec, pl.BlockSpec((blocks, chunk), lambda c: (0, c))],
-        out_shape=[
-            jax.ShapeDtypeStruct(adjoint.shape, jnp.float32),
-            jax.ShapeDtypeStruct((blocks, cells), jnp.float32),
-        ],
-        scratch_shapes=[pltpu.VMEM((level_count, blocks, chunk), jnp.float32)],
+        out_shape=[solved_shape, jax.ShapeDtypeStruct((blocks, cells), jnp.float32)],
+        scratch_shapes=scratch,
         interpret=INTERPRET,
     )(ep, adjoint, survive, mixing)
 
@@ -152,25 +170,25 @@
     levels = lev_dev * lev_groups
     cap = 2
 
-    state = to_columns(jnp.stack([adjoint_in, jnp.exp(-oh_rate), mixing]).transpose(0, 2, 1, 3))
-    adjoint, survive, column_mixing = state[0], state[1], state[2]
-    flows = courant.transpose(0, 2, 1, 3)
-    ep = jnp.broadcast_to(emission_profile[:, None], (lev_dev, lev_groups))
-    ep = lax.all_to_all(ep, "lev", split_axis=1, concat_axis=0, tiled=True).reshape(levels)
+    survive = jnp.exp(-oh_rate)
+    state = to_columns(jnp.stack([adjoint_in * survive, mixing]).transpose(0, 2, 1, 3))
+    right, column_mixing = state[0], state[1]
+    ep = jnp.broadcast_to(emission_profile[:, None, None], (lev_dev, lev_groups, 1))
+    deferred = (courant.transpose(0, 2, 1, 3), survive.transpose(1, 0, 2), ep)
+    grad_sum = jnp.sum(adjoint_in * emission_profile[None, :, None], axis=1)
 
     own_steps = lax.dynamic_slice_in_dim(substeps, lev_index * own, own)
     row_steps = jnp.tile(own_steps, levels)[:, None]
     own_weight = lax.dynamic_slice_in_dim(nest_weight, lev_index * own, own)
-    own_owner = lax.dynamic_slice_in_dim(tile_owner, lev_index * own, own)
 
     face_pack = pack_plan(dest_device[:, 0], peer_count, cap)
     tiles_total = blocks * peer_count // 4
     group_size = tiles_total // peer_count
-    tile_pack = pack_plan(own_owner // group_size, peer_count, cap)
+    tile_pack = pack_plan(tile_owner // group_size, peer_count, cap)
     info = jnp.stack(
         [
             jnp.dot(face_pack, (dest_slot + 1).astype(jnp.float32), precision=HI),
-            jnp.dot(tile_pack, (own_owner % group_size + 1).astype(jnp.float32), precision=HI),
+            jnp.dot(tile_pack, (tile_owner % group_size + 1).astype(jnp.float32), precision=HI),
         ],
         axis=1,
     )
@@ -178,13 +196,17 @@
     face_width = lev_dev * cycle_len
 
     pick = face_matrix(side_len, cell_count)
-    grad_sum = jnp.zeros((own, cell_count), jnp.float32)
     for step_index in range(STEPS):
-        solved, grad_step = column_solve(ep, adjoint, survive, column_mixing)
         if step_index == 0:
-            flows, solved = lax.optimization_barrier((flows, solved))
-            flows = ring_columns(flows, lev_index, lev_groups).reshape(2, levels * own, cell_count)
-        grad_sum = grad_sum + grad_step
+            solved = column_solve(column_mixing, right=right)
+            deferred, solved = lax.optimization_barrier((deferred, solved))
+            flows = ring_columns(deferred[0], lev_index, lev_groups).reshape(2, levels * own, cell_count)
+            column_survive = ring_columns(deferred[1], lev_index, lev_groups)
+            ep = ring_columns(deferred[2], lev_index, lev_groups).reshape(levels)
+        else:
+            solved, grad_step = column_solve(column_mixing, ep=ep, adjoint=adjoint, survive=column_survive)
+            mine = lax.dynamic_slice_in_dim(grad_sum, lev_index * own, own)
+            grad_sum = lax.dynamic_update_slice_in_dim(grad_sum, mine + grad_step, lev_index * own, 0)
         flat = solved.reshape(levels * own, cell_count)
         cycle_out = jnp.dot(flat, pick, precision=HI).reshape(levels, own, cycle_len) * own_weight[None]
         by_level = lax.all_to_all(cycle_out, "lev", split_axis=0, concat_axis=1, tiled=True)

time: 200 us -> 197 us (0.985)
  waiting for transfers between devices: 81.8 us -> 71 us
  starting transfers between devices: 46.3 us -> 54.2 us
  matrix products: 10.4 us -> 8.37 us
    all_to_all x3, waiting for transfers between devices: 46.7 us -> 29.5 us  [to_columns(): lax.all_to_all(x, 'lev', split_axis=x.ndim - 2, concat_axis=x.ndim - 3, t...]
    ppermute x3 -> x9, starting transfers between devices: 4.89 us -> 13.2 us  [ring_columns(): piece = lax.ppermute(piece, 'lev', ring)]
    all_to_all x2, waiting for transfers between devices: 4.24 us -> 11.5 us  [local(): lax.all_to_all(cycle_out, 'lev', split_axis=0, concat_axis=1, tiled=True)]
    all_to_all x2, waiting for transfers between devices: 27.4 us -> 20.5 us  [local(): got = lax.all_to_all(sent, 'blk', split_axis=0, concat_axis=0, tiled=True)]
    ppermute x3 -> x9, waiting for transfers between devices: 3.5 us -> 9.38 us  [ring_columns(): piece = lax.ppermute(piece, 'lev', ring)]
    all_to_all x1 -> x0, starting transfers between devices: 4.29 us -> none  [local(): lax.all_to_all(ep, 'lev', split_axis=1, concat_axis=0, tiled=True)]
    all_to_all x2, starting transfers between devices: 18.6 us -> 22.6 us  [local(): got = lax.all_to_all(sent, 'blk', split_axis=0, concat_axis=0, tiled=True)]
    transpose x1, other arithmetic: 2.65 us -> 0.1 us  [local(): jnp.stack([adjoint_in * survive, mixing]).transpose(0, 2, 1, 3)]
  transfers between devices with their start and end apart: 11 -> 16, of which waited for: 8 -> 7; matrix products, arithmetic and copies ran while one was open for 7% -> 7% of each run, Pallas kernels for 0% -> 0%
where the time goes in v3:
time: 197 us; the launch traced here: 195 us
  waiting for transfers between devices  71 us (36%)
  starting transfers between devices  54.2 us (28%)
  Pallas kernels  18 us (9%)
  blocking collectives  16.7 us (8%)
  local copies, waits for them, and re-layouts  16.5 us (8%)
  other arithmetic  9.49 us (5%)
  matrix products  8.37 us (4%)
    all_to_all x3, waiting for transfers between devices, to_columns(): lax.all_to_all(x, 'lev', split_axis=x.ndim - 2, concat_axis=x.ndim - 3, t...  29.5 us
    all_to_all x2, starting transfers between devices, local(): got = lax.all_to_all(sent, 'blk', split_axis=0, concat_axis=0, tiled=True)  22.6 us
    all_to_all x2, waiting for transfers between devices, local(): got = lax.all_to_all(sent, 'blk', split_axis=0, concat_axis=0, tiled=True)  20.5 us
    all_to_all x1, blocking collectives, local(): lax.all_to_all(packed, 'lev', split_axis=0, concat_axis=0, tiled=True)  16.7 us
    ppermute x9, starting transfers between devices, ring_columns(): piece = lax.ppermute(piece, 'lev', ring)  13.2 us
    all_to_all x2, waiting for transfers between devices, local(): lax.all_to_all(cycle_out, 'lev', split_axis=0, concat_axis=1, tiled=True)  11.5 us
    all_to_all x3, starting transfers between devices, to_columns(): lax.all_to_all(x, 'lev', split_axis=x.ndim - 2, concat_axis=x.ndim - 3, t...  11.1 us
    pallas_call x2, Pallas kernels, advect(): pl.pallas_call(functools.partial(stencil_kernel, side_len), grid=(rows //...  10.2 us
  transfers between devices with their start and end apart: 16, of which 7 were waited for; matrix products, arithmetic and copies ran while one was open for 7% of the time, Pallas kernels for 0%

profile of v3, /device:TPU:8, one launch (start us, length us, event | category | flops | bytes accessed | tf_op | source)
XLA Modules:
  0.0 195.4 jit_solution(11637145384102286945)
XLA Ops:
  0.7 1.7 multiply_bitcast_fusion
  2.5 2.4 %copy.181 = f32[2,3,64,1024]{3,0,1,2:T(2,128)} copy(f32[2,3,64,1024]{3,2,1,0:T(8,128)S(1)} %maximum_bitcast_fusion) | data formatting | bytes 3145728 | tf_op jit(solution)/shard_map/transpose | solution.py:174
  4.8 4.4 %all-to-all-start = ((f32[2,3,64,1024]{3,0,1,2:T(2,128)}), f32[2,3,64,1024]{3,0,1,2:T(2,128)S(1)}, u32[]{:S(2)}, u32[]{:S(2)}) async-start(f32[2,3,64,1024]{3,0,1,2:T(2,128)} %copy.181), calls=%async_computation | async-start | bytes 3145728 | tf_op jit(solution)/shard_map/all_to_all | solution.py:130
  9.6 0.7 broadcast_in_dim_tile.4.st_ref
  11.5 18.5 %all-to-all-done = f32[2,3,64,1024]{3,0,1,2:T(2,128)S(1)} async-done(((f32[2,3,64,1024]{3,0,1,2:T(2,128)}), f32[2,3,64,1024]{3,0,1,2:T(2,128)S(1)}, u32[]{:S(2)}, u32[]{:S(2)}) %all-to-all-start) | async-done | bytes 1572896 | tf_op jit(solution)/shard_map/all_to_all | solution.py:130
  30.5 1.3 fusion.56
  31.8 3.9 %shard_map.113 = f32[12,16,1024]{2,1,0:T(8,128)} custom-call(f32[12,16,1024]{2,1,0:T(8,128)} %bitcast.152, f32[12,16,1024]{2,1,0:T(8,128)} %bitcast.139), custom_call_target="tpu_custom_call" | custom-call | tf_op jit(solution)/shard_map/pallas_call | solution.py:62
  35.7 1.2 collective-permute-start.2
  36.9 1.5 collective-permute-start.1
  38.4 1.1 dynamic-slice_bitcast_fusion.3
  39.5 3.2 %collective-permute-start.5 = (f32[2,3,16,1024]{3,2,1,0:T(8,128)}, f32[2,3,16,1024]{3,2,1,0:T(8,128)S(1)}, u32[]{:S(2)}, u32[]{:S(2)}) collective-permute-start(f32[2,3,16,1024]{3,2,1,0:T(8,128)} %get-tuple-element.21), channel_id=1, source_target_pairs={{0,3},{1,0},{2,1},{3,2},{4,7},{5,4},{6,5},{7,6},{8,11},{9,8},{10,9... | collective-permute-start | bytes 1179656 | tf_op jit(solution)/shard_map/ppermute | solution.py:143
  42.7 0.9 collective-permute-start.4
  43.6 1.2 convolution_multiply_fusion.1
  44.8 3.9 %all-to-all-start.1 = ((f32[12,16,128]{2,1,0:T(8,128)}), f32[12,16,128]{2,1,0:T(8,128)S(1)}, u32[]{:S(2)}, u32[]{:S(2)}) async-start(f32[12,16,128]{2,1,0:T(8,128)} %convolution_multiply_fusion.1), calls=%async_computation.1 | async-start | bytes 196608 | tf_op jit(solution)/shard_map/all_to_all | solution.py:212
  48.7 0.7 dynamic-slice_bitcast_fusion.7
  49.5 3.2 %collective-permute-start.8 = (f32[3,16,1024]{2,1,0:T(8,128)}, f32[3,16,1024]{2,1,0:T(8,128)}, u32[]{:S(2)}, u32[]{:S(2)}) collective-permute-start(f32[3,16,1024]{2,1,0:T(8,128)} %get-tuple-element.27), channel_id=1, source_target_pairs={{0,3},{1,0},{2,1},{3,2},{4,7},{5,4},{6,5},{7,6},{8,11},{9,8},{10,9... | collective-permute-start | bytes 589832 | tf_op jit(solution)/shard_map/ppermute | solution.py:143
  52.7 0.9 collective-permute-start.7
  53.6 0.9 collective-permute-start.6
  55.6 7.3 %all-to-all-done.1 = f32[12,16,128]{2,1,0:T(8,128)S(1)} async-done(((f32[12,16,128]{2,1,0:T(8,128)}), f32[12,16,128]{2,1,0:T(8,128)S(1)}, u32[]{:S(2)}, u32[]{:S(2)}) %all-to-all-start.1) | async-done | bytes 98336 | tf_op jit(solution)/shard_map/all_to_all | solution.py:212
  63.4 0.9 copy.191
  64.3 12.3 %all-to-all-start.2 = ((f32[64,2,512]{2,1,0:T(2,128)}), f32[64,2,512]{2,1,0:T(2,128)}, u32[]{:S(2)}, u32[]{:S(2)}) async-start(f32[64,2,512]{2,1,0:T(2,128)} %copy.191), calls=%async_computation.2 | async-start | bytes 524288 | tf_op jit(solution)/shard_map/all_to_all | solution.py:220
  76.6 1.5 collective-permute-start.3
  78.1 1.2 pad_maximum_fusion.2
  79.9 1.0 bitcast_select_fusion.s_ref
  80.9 9.4 %collective-permute-done.3 = f32[2,3,16,1024]{3,2,1,0:T(8,128)S(1)} collective-permute-done((f32[2,3,16,1024]{3,2,1,0:T(8,128)}, f32[2,3,16,1024]{3,2,1,0:T(8,128)S(1)}, u32[]{:S(2)}, u32[]{:S(2)}) %collective-permute-start.3) | collective-permute-done | bytes 393248 | tf_op jit(solution)/shard_map/ppermute | solution.py:143
  91.4 1.1 reshape.212
  93.2 0.7 copy.194
  93.9 3.3 %all-to-all-start.3 = ((f32[3,64,128]{2,0,1:T(4,128)}), f32[3,64,128]{2,0,1:T(4,128)S(1)}, u32[]{:S(2)}, u32[]{:S(2)}) async-start(f32[3,64,128]{2,0,1:T(4,128)} %copy.194), calls=%async_computation.3 | async-start | bytes 262144 | tf_op jit(solution)/shard_map/all_to_all | solution.py:130
  97.2 1.2 fusion.55
  98.5 4.7 %all-to-all-done.3 = f32[3,64,128]{2,0,1:T(4,128)S(1)} async-done(((f32[3,64,128]{2,0,1:T(4,128)}), f32[3,64,128]{2,0,1:T(4,128)S(1)}, u32[]{:S(2)}, u32[]{:S(2)}) %all-to-all-start.3) | async-done | bytes 98336 | tf_op jit(solution)/shard_map/all_to_all | solution.py:130
  103.2 1.4 fusion.4.add_ref
  104.6 5.1 %shard_map.114 = f32[192,1024]{1,0:T(8,128)} custom-call(s32[192,1]{1,0:T(8,128)} %broadcast_in_dim_tile.4.st_ref, f32[192,1024]{1,0:T(8,128)} %bitcast.141, f32[192,1024]{1,0:T(8,128)} %bitcast.144, f32[192,1024]{1,0:T(8,128)} %bitcast.142, f32[192,1024]{1,0:T(8,128)} %fusion.4.add_ref), custom_call_target="tpu_custom_call" | custom-call | tf_op jit(solution)/shard_map/pallas_call | solution.py:104
  109.7 3.9 %shard_map.115 = (f32[12,16,1024]{2,1,0:T(8,128)}, f32[16,1024]{1,0:T(8,128)}) custom-call(f32[12]{0:T(128)} %broadcast_select_fusion.ep_ref, f32[12,16,1024]{2,1,0:T(8,128)} %bitcast.150, f32[12,16,1024]{2,1,0:T(8,128)} %bitcast_select_fusion.s_ref, f32[12,16,1024]{2,1,0:T(8,128)} %bitcast.140), custom_call_target="tpu_custom_call" | custom-call | tf_op jit(solution)/shard_map/pallas_call | solution.py:71
  113.7 2.3 %convolution_multiply_fusion = f32[12,16,128]{2,1,0:T(8,128)} fusion(f32[12,16,1024]{2,1,0:T(8,128)} %get-tuple-element.12, s32[128]{0:T(128)S(1)} %pad_add_fusion, f32[16,128]{1,0:T(8,128)S(1)} %constant_dynamic-slice_fusion), kind=kOutput, calls=%fused_computation.8 | convolution fusion | flops 302145536 | bytes 893440 | tf_op jit(solution)/shard_map/dot_general | solution.py:211
  116.0 3.3 %all-to-all-start.4 = ((f32[12,16,128]{2,1,0:T(8,128)}), f32[12,16,128]{2,1,0:T(8,128)S(1)}, u32[]{:S(2)}, u32[]{:S(2)}) async-start(f32[12,16,128]{2,1,0:T(8,128)} %convolution_multiply_fusion), calls=%async_computation.4 | async-start | bytes 196608 | tf_op jit(solution)/shard_map/all_to_all | solution.py:212
  119.3 0.9 add_dynamic-update-slice_fusion
  120.9 4.2 %all-to-all-done.4 = f32[12,16,128]{2,1,0:T(8,128)S(1)} async-done(((f32[12,16,128]{2,1,0:T(8,128)}), f32[12,16,128]{2,1,0:T(8,128)S(1)}, u32[]{:S(2)}, u32[]{:S(2)}) %all-to-all-start.4) | async-done | bytes 98336 | tf_op jit(solution)/shard_map/all_to_all | solution.py:212
  125.7 1.2 pad_maximum_fusion.3
  126.8 10.3 %all-to-all-start.5 = ((f32[64,2,1408]{2,1,0:T(2,128)}), f32[64,2,1408]{2,1,0:T(2,128)S(1)}, u32[]{:S(2)}, u32[]{:S(2)}) async-start(f32[64,2,1408]{2,1,0:T(2,128)} %pad_maximum_fusion.3), calls=%async_computation.5 | async-start | bytes 1441792 | tf_op jit(solution)/shard_map/all_to_all | solution.py:220
  137.2 20.5 %all-to-all-done.5 = f32[64,2,1408]{2,1,0:T(2,128)S(1)} async-done(((f32[64,2,1408]{2,1,0:T(2,128)}), f32[64,2,1408]{2,1,0:T(2,128)S(1)}, u32[]{:S(2)}, u32[]{:S(2)}) %all-to-all-start.5) | async-done | bytes 720928 | tf_op jit(solution)/shard_map/all_to_all | solution.py:220
  158.6 0.7 copy.207
  159.4 3.3 %all-to-all-start.6 = ((f32[3,64,128]{2,0,1:T(4,128)}), f32[3,64,128]{2,0,1:T(4,128)S(1)}, u32[]{:S(2)}, u32[]{:S(2)}) async-start(f32[3,64,128]{2,0,1:T(4,128)} %copy.207), calls=%async_computation.6 | async-start | bytes 262144 | tf_op jit(solution)/shard_map/all_to_all | solution.py:130
  163.0 6.3 %all-to-all-done.6 = f32[3,64,128]{2,0,1:T(4,128)S(1)} async-done(((f32[3,64,128]{2,0,1:T(4,128)}), f32[3,64,128]{2,0,1:T(4,128)S(1)}, u32[]{:S(2)}, u32[]{:S(2)}) %all-to-all-start.6) | async-done | bytes 98336 | tf_op jit(solution)/shard_map/all_to_all | solution.py:130
  169.4 1.4 fusion.3.add_ref
  170.7 5.1 %shard_map.116 = f32[192,1024]{1,0:T(8,128)} custom-call(s32[192,1]{1,0:T(8,128)} %broadcast_in_dim_tile.4.st_ref, f32[192,1024]{1,0:T(8,128)} %bitcast.153, f32[192,1024]{1,0:T(8,128)} %bitcast.145, f32[192,1024]{1,0:T(8,128)} %bitcast.143, f32[192,1024]{1,0:T(8,128)} %fusion.3.add_ref), custom_call_target="tpu_custom_call" | custom-call | tf_op jit(solution)/shard_map/pallas_call | solution.py:104
  175.9 1.2 pad_maximum_fusion.1
  177.1 16.7 %all_to_all.96 = f32[4,52,1024]{2,1,0:T(8,128)S(1)} all-to-all(f32[4,52,1024]{2,1,0:T(8,128)S(1)} %pad_maximum_fusion.1), channel_id=1, replica_groups=mesh['blk'=64,'lev'=4] {'lev'}, dimensions={0} | all-to-all | bytes 1703936 | tf_op jit(solution)/shard_map/all_to_all | solution.py:248
  193.8 0.9 copy.211
  (94 shorter events, 9.1 us)
Async XLA Ops:
  0.6 10.8 %copy-start = (f32[64,128]{1,0:T(8,128)S(1)}, f32[64,128]{1,0:T(8,128)}, u32[]{:S(2)}) copy-start(f32[64,128]{1,0:T(8,128)} %param.15) | copy-start | bytes 98308
  0.6 1.7 copy-start.3
  4.8 4.7 %copy-start.5 = (s32[64]{0:T(128)S(1)}, s32[64]{0:T(128)}, u32[]{:S(2)}) copy-start(s32[64]{0:T(128)} %param.14) | copy-start | bytes 772
  4.8 5.5 %copy-start.6 = (s32[64]{0:T(128)S(1)}, s32[64]{0:T(128)}, u32[]{:S(2)}) copy-start(s32[64]{0:T(128)} %param.19) | copy-start | bytes 772
  4.8 5.8 %copy-start.7 = (s32[64,1]{0,1:T(1,128)S(1)}, s32[64,1]{0,1:T(1,128)}, u32[]{:S(2)}) copy-start(s32[64,1]{0,1:T(1,128)} %param.16) | copy-start | bytes 772
  4.8 6.1 %copy-start.8 = (s32[64]{0:T(128)S(1)}, s32[64]{0:T(128)}, u32[]{:S(2)}) copy-start(s32[64]{0:T(128)} %param.17) | copy-start | bytes 772
  4.8 25.1 %all-to-all-start = ((f32[2,3,64,1024]{3,0,1,2:T(2,128)}), f32[2,3,64,1024]{3,0,1,2:T(2,128)S(1)}, u32[]{:S(2)}, u32[]{:S(2)}) async-start(f32[2,3,64,1024]{3,0,1,2:T(2,128)} %copy.181), calls=%async_computation | async-start | bytes 3145728 | tf_op jit(solution)/shard_map/all_to_all | solution.py:130
  31.8 3.9 %copy-start.4 = (f32[3]{0:T(128)S(1)}, f32[3]{0:T(128)}, u32[]{:S(2)}) copy-start(f32[3]{0:T(128)} %param.18) | copy-start | bytes 40
  31.8 6.6 %copy-start.2 = (f32[2,64,3,1024]{3,1,2,0:T(8,128)S(1)}, f32[2,64,3,1024]{3,1,2,0:T(8,128)}, u32[]{:S(2)}) copy-start(f32[2,64,3,1024]{3,1,2,0:T(8,128)} %param.11) | copy-start | bytes 4718596
  35.7 13.8 %collective-permute-start.2 = (f32[3,1,1]{0,2,1:T(1,128)S(1)}, f32[3,1,1]{0,2,1:T(1,128)S(1)}, u32[]{:S(2)}, u32[]{:S(2)}) collective-permute-start(f32[3,1,1]{0,2,1:T(1,128)S(1)} %get-tuple-element.32), channel_id=1, source_target_pairs={{0,3},{1,0},{2,1},{3,2},{4,7},{5,4},{6,5},{7,6},{8,11},{9,8},{10,9... | collective-permute-start | bytes 44 | tf_op jit(solution)/shard_map/ppermute | solution.py:143
  36.9 15.8 %collective-permute-start.1 = (f32[3,1,1]{0,2,1:T(1,128)S(1)}, f32[3,1,1]{0,2,1:T(1,128)S(1)}, u32[]{:S(2)}, u32[]{:S(2)}) collective-permute-start(f32[3,1,1]{0,2,1:T(1,128)S(1)} %get-tuple-element.33), channel_id=1, source_target_pairs={{0,2},{1,3},{2,0},{3,1},{4,6},{5,7},{6,4},{7,5},{8,10},{9,11},{10,... | collective-permute-start | bytes 44 | tf_op jit(solution)/shard_map/ppermute | solution.py:143
  38.4 15.2 %collective-permute-start = (f32[3,1,1]{0,2,1:T(1,128)S(1)}, f32[3,1,1]{0,2,1:T(1,128)S(1)}, u32[]{:S(2)}, u32[]{:S(2)}) collective-permute-start(f32[3,1,1]{0,2,1:T(1,128)S(1)} %get-tuple-element.34), channel_id=1, source_target_pairs={{0,1},{1,2},{2,3},{3,0},{4,5},{5,6},{6,7},{7,4},{8,9},{9,10},{10,1... | collective-permute-start | bytes 44 | tf_op jit(solution)/shard_map/ppermute | solution.py:143
  38.4 5.2 %copy-start.1 = (f32[12,16,1024]{2,1,0:T(8,128)S(1)}, f32[12,16,1024]{2,1,0:T(8,128)}, u32[]{:S(2)}) copy-start(f32[12,16,1024]{2,1,0:T(8,128)} %shard_map.113) | copy-start | bytes 2359300
  39.5 41.4 %collective-permute-start.5 = (f32[2,3,16,1024]{3,2,1,0:T(8,128)}, f32[2,3,16,1024]{3,2,1,0:T(8,128)S(1)}, u32[]{:S(2)}, u32[]{:S(2)}) collective-permute-start(f32[2,3,16,1024]{3,2,1,0:T(8,128)} %get-tuple-element.21), channel_id=1, source_target_pairs={{0,3},{1,0},{2,1},{3,2},{4,7},{5,4},{6,5},{7,6},{8,11},{9,8},{10,9... | collective-permute-start | bytes 1179656 | tf_op jit(solution)/shard_map/ppermute | solution.py:143
  42.7 38.2 %collective-permute-start.4 = (f32[2,3,16,1024]{3,2,1,0:T(8,128)}, f32[2,3,16,1024]{3,2,1,0:T(8,128)S(1)}, u32[]{:S(2)}, u32[]{:S(2)}) collective-permute-start(f32[2,3,16,1024]{3,2,1,0:T(8,128)} %get-tuple-element.19), channel_id=1, source_target_pairs={{0,2},{1,3},{2,0},{3,1},{4,6},{5,7},{6,4},{7,5},{8,10},{9,11},{10,... | collective-permute-start | bytes 1179656 | tf_op jit(solution)/shard_map/ppermute | solution.py:143
  44.8 18.2 %all-to-all-start.1 = ((f32[12,16,128]{2,1,0:T(8,128)}), f32[12,16,128]{2,1,0:T(8,128)S(1)}, u32[]{:S(2)}, u32[]{:S(2)}) async-start(f32[12,16,128]{2,1,0:T(8,128)} %convolution_multiply_fusion.1), calls=%async_computation.1 | async-start | bytes 196608 | tf_op jit(solution)/shard_map/all_to_all | solution.py:212
  49.5 27.1 %collective-permute-start.8 = (f32[3,16,1024]{2,1,0:T(8,128)}, f32[3,16,1024]{2,1,0:T(8,128)}, u32[]{:S(2)}, u32[]{:S(2)}) collective-permute-start(f32[3,16,1024]{2,1,0:T(8,128)} %get-tuple-element.27), channel_id=1, source_target_pairs={{0,3},{1,0},{2,1},{3,2},{4,7},{5,4},{6,5},{7,6},{8,11},{9,8},{10,9... | collective-permute-start | bytes 589832 | tf_op jit(solution)/shard_map/ppermute | solution.py:143
  52.7 25.4 %collective-permute-start.7 = (f32[3,16,1024]{2,1,0:T(8,128)S(1)}, f32[3,16,1024]{2,1,0:T(8,128)}, u32[]{:S(2)}, u32[]{:S(2)}) collective-permute-start(f32[3,16,1024]{2,1,0:T(8,128)S(1)} %get-tuple-element.25), channel_id=1, source_target_pairs={{0,2},{1,3},{2,0},{3,1},{4,6},{5,7},{6,4},{7,5},{8,10},{9,11},{10,... | collective-permute-start | bytes 589832 | tf_op jit(solution)/shard_map/ppermute | solution.py:143
  53.6 24.5 %collective-permute-start.6 = (f32[3,16,1024]{2,1,0:T(8,128)S(1)}, f32[3,16,1024]{2,1,0:T(8,128)}, u32[]{:S(2)}, u32[]{:S(2)}) collective-permute-start(f32[3,16,1024]{2,1,0:T(8,128)S(1)} %get-tuple-element.26), channel_id=1, source_target_pairs={{0,1},{1,2},{2,3},{3,0},{4,5},{5,6},{6,7},{7,4},{8,9},{9,10},{10,1... | collective-permute-start | bytes 589832 | tf_op jit(solution)/shard_map/ppermute | solution.py:143
  64.3 27.1 %all-to-all-start.2 = ((f32[64,2,512]{2,1,0:T(2,128)}), f32[64,2,512]{2,1,0:T(2,128)}, u32[]{:S(2)}, u32[]{:S(2)}) async-start(f32[64,2,512]{2,1,0:T(2,128)} %copy.191), calls=%async_computation.2 | async-start | bytes 524288 | tf_op jit(solution)/shard_map/all_to_all | solution.py:220
  76.6 13.7 %collective-permute-start.3 = (f32[2,3,16,1024]{3,2,1,0:T(8,128)}, f32[2,3,16,1024]{3,2,1,0:T(8,128)S(1)}, u32[]{:S(2)}, u32[]{:S(2)}) collective-permute-start(f32[2,3,16,1024]{3,2,1,0:T(8,128)} %get-tuple-element.20), channel_id=1, source_target_pairs={{0,1},{1,2},{2,3},{3,0},{4,5},{5,6},{6,7},{7,4},{8,9},{9,10},{10,1... | collective-permute-start | bytes 1179656 | tf_op jit(solution)/shard_map/ppermute | solution.py:143
  93.9 9.3 %all-to-all-start.3 = ((f32[3,64,128]{2,0,1:T(4,128)}), f32[3,64,128]{2,0,1:T(4,128)S(1)}, u32[]{:S(2)}, u32[]{:S(2)}) async-start(f32[3,64,128]{2,0,1:T(4,128)} %copy.194), calls=%async_computation.3 | async-start | bytes 262144 | tf_op jit(solution)/shard_map/all_to_all | solution.py:130
  116.0 9.1 %all-to-all-start.4 = ((f32[12,16,128]{2,1,0:T(8,128)}), f32[12,16,128]{2,1,0:T(8,128)S(1)}, u32[]{:S(2)}, u32[]{:S(2)}) async-start(f32[12,16,128]{2,1,0:T(8,128)} %convolution_multiply_fusion), calls=%async_computation.4 | async-start | bytes 196608 | tf_op jit(solution)/shard_map/all_to_all | solution.py:212
  126.8 30.9 %all-to-all-start.5 = ((f32[64,2,1408]{2,1,0:T(2,128)}), f32[64,2,1408]{2,1,0:T(2,128)S(1)}, u32[]{:S(2)}, u32[]{:S(2)}) async-start(f32[64,2,1408]{2,1,0:T(2,128)} %pad_maximum_fusion.3), calls=%async_computation.5 | async-start | bytes 1441792 | tf_op jit(solution)/shard_map/all_to_all | solution.py:220
  159.4 10.0 %all-to-all-start.6 = ((f32[3,64,128]{2,0,1:T(4,128)}), f32[3,64,128]{2,0,1:T(4,128)S(1)}, u32[]{:S(2)}, u32[]{:S(2)}) async-start(f32[3,64,128]{2,0,1:T(4,128)} %copy.207), calls=%async_computation.6 | async-start | bytes 262144 | tf_op jit(solution)/shard_map/all_to_all | solution.py:130

commit v4 on v3

--- a/solution.py
+++ b/solution.py
@@ -148,6 +148,15 @@
     return got.reshape(lead + (lev_groups * lev_dev, own, cells))
 
 
+def ring_sum(x, lev_index, lev_groups):
+    total = lax.dynamic_index_in_dim(x, lev_index, axis=x.ndim - 2, keepdims=False)
+    for shift in range(1, lev_groups):
+        piece = lax.dynamic_index_in_dim(x, (lev_index + shift) % lev_groups, axis=x.ndim - 2, keepdims=False)
+        ring = [(src, (src + shift) % lev_groups) for src in range(lev_groups)]
+        total = total + lax.ppermute(piece, "lev", ring)
+    return total
+
+
 def local(
     adjoint_in,
     courant,
@@ -215,7 +224,8 @@
         if step_index == 0:
             sent = jnp.concatenate([sent, info], axis=2)
         if step_index == STEPS - 1:
-            tile_sent = jnp.dot(tile_pack, grad_sum, precision=HI).reshape(peer_count, cap, cell_count)
+            quarter = ring_sum(grad_sum.reshape(blocks, lev_groups, cell_count // lev_groups), lev_index, lev_groups)
+            tile_sent = jnp.dot(tile_pack, quarter, precision=HI).reshape(peer_count, cap, -1)
             sent = jnp.concatenate([sent, tile_sent], axis=2)
         got = lax.all_to_all(sent, "blk", split_axis=0, concat_axis=0, tiled=True)
         got = got.reshape(peer_count * cap, -1)
@@ -241,12 +251,13 @@
     packed = jnp.concatenate(
         [
             adjoint.reshape(lev_groups, lev_dev * own, cell_count),
-            tile_parts.reshape(lev_groups, tile_rows, cell_count),
+            tile_parts.reshape(lev_groups, 1, cell_count),
         ],
         axis=1,
     )
     packed = lax.all_to_all(packed, "lev", split_axis=0, concat_axis=0, tiled=True)
-    tile_grad = jnp.sum(packed[:, lev_dev * own :], axis=0)
+    tile_grad = packed[:, lev_dev * own].reshape(lev_groups, tile_rows, cell_count // lev_groups)
+    tile_grad = tile_grad.transpose(1, 0, 2).reshape(tile_rows, cell_count)
     adjoint_out = packed[:, : lev_dev * own].reshape(lev_groups, lev_dev, own, cell_count)
     adjoint_out = adjoint_out.transpose(0, 2, 1, 3).reshape(blocks, lev_dev, cell_count)
     return (adjoint_out, tile_grad)

time: 197 us -> 191 us (0.970)
  waiting for transfers between devices: 71 us -> 63.9 us
  starting transfers between devices: 54.2 us -> 58.4 us
    all_to_all x2, waiting for transfers between devices: 20.5 us -> 12.8 us  [local(): got = lax.all_to_all(sent, 'blk', split_axis=0, concat_axis=0, tiled=True)]
    ppermute x0 -> x3, starting transfers between devices: none -> 2.71 us  [ring_sum(): total = total + lax.ppermute(piece, 'lev', ring)]
  transfers between devices with their start and end apart: 16 -> 19, of which waited for: 7 -> 7; matrix products, arithmetic and copies ran while one was open for 7% -> 8% of each run, Pallas kernels for 0% -> 0%
where the time goes in v4:
time: 191 us; the launch traced here: 190 us
  waiting for transfers between devices  63.9 us (33%)
  starting transfers between devices  58.4 us (31%)
  Pallas kernels  18.1 us (9%)
  local copies, waits for them, and re-layouts  17.9 us (9%)
  blocking collectives  15.6 us (8%)
  other arithmetic  7.79 us (4%)
  matrix products  6.97 us (4%)
    all_to_all x3, waiting for transfers between devices, to_columns(): lax.all_to_all(x, 'lev', split_axis=x.ndim - 2, concat_axis=x.ndim - 3, t...  28.9 us
    all_to_all x2, starting transfers between devices, local(): got = lax.all_to_all(sent, 'blk', split_axis=0, concat_axis=0, tiled=True)  22.6 us
    all_to_all x1, blocking collectives, local(): lax.all_to_all(packed, 'lev', split_axis=0, concat_axis=0, tiled=True)  15.6 us
    ppermute x9, starting transfers between devices, ring_columns(): piece = lax.ppermute(piece, 'lev', ring)  13.2 us
    all_to_all x2, waiting for transfers between devices, local(): got = lax.all_to_all(sent, 'blk', split_axis=0, concat_axis=0, tiled=True)  12.8 us
    all_to_all x2, waiting for transfers between devices, local(): lax.all_to_all(cycle_out, 'lev', split_axis=0, concat_axis=1, tiled=True)  12.8 us
    all_to_all x3, starting transfers between devices, to_columns(): lax.all_to_all(x, 'lev', split_axis=x.ndim - 2, concat_axis=x.ndim - 3, t...  11.1 us
    pallas_call x2, Pallas kernels, advect(): pl.pallas_call(functools.partial(stencil_kernel, side_len), grid=(rows //...  10.2 us
  transfers between devices with their start and end apart: 19, of which 7 were waited for; matrix products, arithmetic and copies ran while one was open for 8% of the time, Pallas kernels for 0%

profile of v4, /device:TPU:8, one launch (start us, length us, event | category | flops | bytes accessed | tf_op | source)
XLA Modules:
  0.0 190.0 jit_solution(59629276563527804)
XLA Ops:
  0.7 1.7 multiply_bitcast_fusion
  2.5 2.4 %copy.200 = f32[2,3,64,1024]{3,0,1,2:T(2,128)} copy(f32[2,3,64,1024]{3,2,1,0:T(8,128)S(1)} %maximum_bitcast_fusion) | data formatting | bytes 3145728 | tf_op jit(solution)/shard_map/transpose | solution.py:183
  4.9 4.4 %all-to-all-start = ((f32[2,3,64,1024]{3,0,1,2:T(2,128)}), f32[2,3,64,1024]{3,0,1,2:T(2,128)S(1)}, u32[]{:S(2)}, u32[]{:S(2)}) async-start(f32[2,3,64,1024]{3,0,1,2:T(2,128)} %copy.200), calls=%async_computation | async-start | bytes 3145728 | tf_op jit(solution)/shard_map/all_to_all | solution.py:130
  9.6 0.7 broadcast_in_dim_tile.4.st_ref
  11.5 18.5 %all-to-all-done = f32[2,3,64,1024]{3,0,1,2:T(2,128)S(1)} async-done(((f32[2,3,64,1024]{3,0,1,2:T(2,128)}), f32[2,3,64,1024]{3,0,1,2:T(2,128)S(1)}, u32[]{:S(2)}, u32[]{:S(2)}) %all-to-all-start) | async-done | bytes 1572896 | tf_op jit(solution)/shard_map/all_to_all | solution.py:130
  30.5 1.3 fusion.60
  31.8 3.9 %shard_map.113 = f32[12,16,1024]{2,1,0:T(8,128)} custom-call(f32[12,16,1024]{2,1,0:T(8,128)} %bitcast.171, f32[12,16,1024]{2,1,0:T(8,128)} %bitcast.159), custom_call_target="tpu_custom_call" | custom-call | tf_op jit(solution)/shard_map/pallas_call | solution.py:62
  35.7 1.2 collective-permute-start.2
  37.0 1.5 collective-permute-start.1
  38.5 1.1 dynamic-slice_bitcast_fusion.3
  39.5 3.2 %collective-permute-start.5 = (f32[2,3,16,1024]{3,2,1,0:T(8,128)}, f32[2,3,16,1024]{3,2,1,0:T(8,128)S(1)}, u32[]{:S(2)}, u32[]{:S(2)}) collective-permute-start(f32[2,3,16,1024]{3,2,1,0:T(8,128)} %get-tuple-element.21), channel_id=1, source_target_pairs={{0,3},{1,0},{2,1},{3,2},{4,7},{5,4},{6,5},{7,6},{8,11},{9,8},{10,9... | collective-permute-start | bytes 1179656 | tf_op jit(solution)/shard_map/ppermute | solution.py:143
  42.7 0.9 collective-permute-start.4
  43.6 1.2 convolution_multiply_fusion.1
  44.8 3.9 %all-to-all-start.1 = ((f32[12,16,128]{2,1,0:T(8,128)}), f32[12,16,128]{2,1,0:T(8,128)S(1)}, u32[]{:S(2)}, u32[]{:S(2)}) async-start(f32[12,16,128]{2,1,0:T(8,128)} %convolution_multiply_fusion.1), calls=%async_computation.1 | async-start | bytes 196608 | tf_op jit(solution)/shard_map/all_to_all | solution.py:221
  48.7 0.8 dynamic-slice_bitcast_fusion.7
  49.5 3.2 %collective-permute-start.8 = (f32[3,16,1024]{2,1,0:T(8,128)}, f32[3,16,1024]{2,1,0:T(8,128)}, u32[]{:S(2)}, u32[]{:S(2)}) collective-permute-start(f32[3,16,1024]{2,1,0:T(8,128)} %get-tuple-element.27), channel_id=1, source_target_pairs={{0,3},{1,0},{2,1},{3,2},{4,7},{5,4},{6,5},{7,6},{8,11},{9,8},{10,9... | collective-permute-start | bytes 589832 | tf_op jit(solution)/shard_map/ppermute | solution.py:143
  52.7 0.9 collective-permute-start.7
  53.6 0.9 collective-permute-start.6
  55.6 7.3 %all-to-all-done.1 = f32[12,16,128]{2,1,0:T(8,128)S(1)} async-done(((f32[12,16,128]{2,1,0:T(8,128)}), f32[12,16,128]{2,1,0:T(8,128)S(1)}, u32[]{:S(2)}, u32[]{:S(2)}) %all-to-all-start.1) | async-done | bytes 98336 | tf_op jit(solution)/shard_map/all_to_all | solution.py:221
  63.4 0.9 copy.210
  64.3 12.3 %all-to-all-start.2 = ((f32[64,2,512]{2,1,0:T(2,128)}), f32[64,2,512]{2,1,0:T(2,128)}, u32[]{:S(2)}, u32[]{:S(2)}) async-start(f32[64,2,512]{2,1,0:T(2,128)} %copy.210), calls=%async_computation.2 | async-start | bytes 524288 | tf_op jit(solution)/shard_map/all_to_all | solution.py:230
  76.6 1.5 collective-permute-start.3
  78.1 1.2 pad_maximum_fusion.2
  79.9 1.0 bitcast_select_fusion.s_ref
  80.9 9.4 %collective-permute-done.3 = f32[2,3,16,1024]{3,2,1,0:T(8,128)S(1)} collective-permute-done((f32[2,3,16,1024]{3,2,1,0:T(8,128)}, f32[2,3,16,1024]{3,2,1,0:T(8,128)S(1)}, u32[]{:S(2)}, u32[]{:S(2)}) %collective-permute-start.3) | collective-permute-done | bytes 393248 | tf_op jit(solution)/shard_map/ppermute | solution.py:143
  91.5 1.1 reshape.218
  93.9 3.3 %all-to-all-start.3 = ((f32[3,64,128]{2,0,1:T(4,128)}), f32[3,64,128]{2,0,1:T(4,128)S(1)}, u32[]{:S(2)}, u32[]{:S(2)}) async-start(f32[3,64,128]{2,0,1:T(4,128)} %copy.213), calls=%async_computation.3 | async-start | bytes 262144 | tf_op jit(solution)/shard_map/all_to_all | solution.py:130
  97.3 1.2 fusion.59
  98.5 4.7 %all-to-all-done.3 = f32[3,64,128]{2,0,1:T(4,128)S(1)} async-done(((f32[3,64,128]{2,0,1:T(4,128)}), f32[3,64,128]{2,0,1:T(4,128)S(1)}, u32[]{:S(2)}, u32[]{:S(2)}) %all-to-all-start.3) | async-done | bytes 98336 | tf_op jit(solution)/shard_map/all_to_all | solution.py:130
  103.2 1.4 fusion.2.add_ref
  104.6 5.1 %shard_map.114 = f32[192,1024]{1,0:T(8,128)} custom-call(s32[192,1]{1,0:T(8,128)} %broadcast_in_dim_tile.4.st_ref, f32[192,1024]{1,0:T(8,128)} %bitcast.161, f32[192,1024]{1,0:T(8,128)} %bitcast.164, f32[192,1024]{1,0:T(8,128)} %bitcast.162, f32[192,1024]{1,0:T(8,128)} %fusion.2.add_ref), custom_call_target="tpu_custom_call" | custom-call | tf_op jit(solution)/shard_map/pallas_call | solution.py:104
  109.7 4.0 %shard_map.115 = (f32[12,16,1024]{2,1,0:T(8,128)}, f32[16,1024]{1,0:T(8,128)}) custom-call(f32[12]{0:T(128)} %broadcast_select_fusion.ep_ref, f32[12,16,1024]{2,1,0:T(8,128)} %bitcast.170, f32[12,16,1024]{2,1,0:T(8,128)} %bitcast_select_fusion.s_ref, f32[12,16,1024]{2,1,0:T(8,128)} %bitcast.160), custom_call_target="tpu_custom_call" | custom-call | tf_op jit(solution)/shard_map/pallas_call | solution.py:71
  113.7 0.9 add_dynamic-update-slice_fusion
  115.1 1.2 collective-permute-start.11
  116.3 1.5 collective-permute-start.10
  117.8 1.2 convolution_multiply_fusion
  119.0 4.8 %all-to-all-start.4 = ((f32[12,16,128]{2,1,0:T(8,128)}), f32[12,16,128]{2,1,0:T(8,128)S(1)}, u32[]{:S(2)}, u32[]{:S(2)}) async-start(f32[12,16,128]{2,1,0:T(8,128)} %convolution_multiply_fusion), calls=%async_computation.4 | async-start | bytes 196608 | tf_op jit(solution)/shard_map/all_to_all | solution.py:221
  124.1 5.5 %all-to-all-done.4 = f32[12,16,128]{2,1,0:T(8,128)S(1)} async-done(((f32[12,16,128]{2,1,0:T(8,128)}), f32[12,16,128]{2,1,0:T(8,128)S(1)}, u32[]{:S(2)}, u32[]{:S(2)}) %all-to-all-start.4) | async-done | bytes 98336 | tf_op jit(solution)/shard_map/all_to_all | solution.py:221
  130.1 1.0 copy.224
  131.0 10.3 %all-to-all-start.5 = ((f32[64,2,640]{2,1,0:T(2,128)}), f32[64,2,640]{2,1,0:T(2,128)S(1)}, u32[]{:S(2)}, u32[]{:S(2)}) async-start(f32[64,2,640]{2,1,0:T(2,128)} %copy.224), calls=%async_computation.5 | async-start | bytes 655360 | tf_op jit(solution)/shard_map/all_to_all | solution.py:230
  141.4 12.8 %all-to-all-done.5 = f32[64,2,640]{2,1,0:T(2,128)S(1)} async-done(((f32[64,2,640]{2,1,0:T(2,128)}), f32[64,2,640]{2,1,0:T(2,128)S(1)}, u32[]{:S(2)}, u32[]{:S(2)}) %all-to-all-start.5) | async-done | bytes 327712 | tf_op jit(solution)/shard_map/all_to_all | solution.py:230
  155.6 3.3 %all-to-all-start.6 = ((f32[3,64,128]{2,0,1:T(4,128)}), f32[3,64,128]{2,0,1:T(4,128)S(1)}, u32[]{:S(2)}, u32[]{:S(2)}) async-start(f32[3,64,128]{2,0,1:T(4,128)} %copy.227), calls=%async_computation.6 | async-start | bytes 262144 | tf_op jit(solution)/shard_map/all_to_all | solution.py:130
  159.2 5.7 %all-to-all-done.6 = f32[3,64,128]{2,0,1:T(4,128)S(1)} async-done(((f32[3,64,128]{2,0,1:T(4,128)}), f32[3,64,128]{2,0,1:T(4,128)S(1)}, u32[]{:S(2)}, u32[]{:S(2)}) %all-to-all-start.6) | async-done | bytes 98336 | tf_op jit(solution)/shard_map/all_to_all | solution.py:130
  164.9 1.4 fusion.1.add_ref
  166.3 5.1 %shard_map.116 = f32[192,1024]{1,0:T(8,128)} custom-call(s32[192,1]{1,0:T(8,128)} %broadcast_in_dim_tile.4.st_ref, f32[192,1024]{1,0:T(8,128)} %bitcast.172, f32[192,1024]{1,0:T(8,128)} %bitcast.165, f32[192,1024]{1,0:T(8,128)} %bitcast.163, f32[192,1024]{1,0:T(8,128)} %fusion.1.add_ref), custom_call_target="tpu_custom_call" | custom-call | tf_op jit(solution)/shard_map/pallas_call | solution.py:104
  171.4 1.2 pad_maximum_fusion.1
  172.7 15.6 %all_to_all.96 = f32[4,49,1024]{2,1,0:T(8,128)S(1)} all-to-all(f32[4,49,1024]{2,1,0:T(8,128)S(1)} %pad_maximum_fusion.1), channel_id=1, replica_groups=mesh['blk'=64,'lev'=4] {'lev'}, dimensions={0} | all-to-all | bytes 1605632 | tf_op jit(solution)/shard_map/all_to_all | solution.py:258
  188.4 0.9 copy.232
  (109 shorter events, 10.1 us)
Async XLA Ops:
  0.6 10.8 %copy-start = (f32[64,128]{1,0:T(8,128)S(1)}, f32[64,128]{1,0:T(8,128)}, u32[]{:S(2)}) copy-start(f32[64,128]{1,0:T(8,128)} %param.15) | copy-start | bytes 98308
  0.6 1.7 copy-start.4
  4.8 4.7 %copy-start.6 = (s32[64]{0:T(128)S(1)}, s32[64]{0:T(128)}, u32[]{:S(2)}) copy-start(s32[64]{0:T(128)} %param.14) | copy-start | bytes 772
  4.8 5.5 %copy-start.7 = (s32[64]{0:T(128)S(1)}, s32[64]{0:T(128)}, u32[]{:S(2)}) copy-start(s32[64]{0:T(128)} %param.19) | copy-start | bytes 772
  4.8 5.8 %copy-start.8 = (s32[64,1]{0,1:T(1,128)S(1)}, s32[64,1]{0,1:T(1,128)}, u32[]{:S(2)}) copy-start(s32[64,1]{0,1:T(1,128)} %param.16) | copy-start | bytes 772
  4.8 6.1 %copy-start.9 = (s32[64]{0:T(128)S(1)}, s32[64]{0:T(128)}, u32[]{:S(2)}) copy-start(s32[64]{0:T(128)} %param.17) | copy-start | bytes 772
  4.9 25.1 %all-to-all-start = ((f32[2,3,64,1024]{3,0,1,2:T(2,128)}), f32[2,3,64,1024]{3,0,1,2:T(2,128)S(1)}, u32[]{:S(2)}, u32[]{:S(2)}) async-start(f32[2,3,64,1024]{3,0,1,2:T(2,128)} %copy.200), calls=%async_computation | async-start | bytes 3145728 | tf_op jit(solution)/shard_map/all_to_all | solution.py:130
  31.8 3.9 %copy-start.5 = (f32[3]{0:T(128)S(1)}, f32[3]{0:T(128)}, u32[]{:S(2)}) copy-start(f32[3]{0:T(128)} %param.18) | copy-start | bytes 40
  31.8 6.7 %copy-start.3 = (f32[2,64,3,1024]{3,1,2,0:T(8,128)S(1)}, f32[2,64,3,1024]{3,1,2,0:T(8,128)}, u32[]{:S(2)}) copy-start(f32[2,64,3,1024]{3,1,2,0:T(8,128)} %param.11) | copy-start | bytes 4718596
  35.7 13.8 %collective-permute-start.2 = (f32[3,1,1]{0,2,1:T(1,128)S(1)}, f32[3,1,1]{0,2,1:T(1,128)S(1)}, u32[]{:S(2)}, u32[]{:S(2)}) collective-permute-start(f32[3,1,1]{0,2,1:T(1,128)S(1)} %get-tuple-element.36), channel_id=1, source_target_pairs={{0,3},{1,0},{2,1},{3,2},{4,7},{5,4},{6,5},{7,6},{8,11},{9,8},{10,9... | collective-permute-start | bytes 44 | tf_op jit(solution)/shard_map/ppermute | solution.py:143
  37.0 15.8 %collective-permute-start.1 = (f32[3,1,1]{0,2,1:T(1,128)S(1)}, f32[3,1,1]{0,2,1:T(1,128)S(1)}, u32[]{:S(2)}, u32[]{:S(2)}) collective-permute-start(f32[3,1,1]{0,2,1:T(1,128)S(1)} %get-tuple-element.37), channel_id=1, source_target_pairs={{0,2},{1,3},{2,0},{3,1},{4,6},{5,7},{6,4},{7,5},{8,10},{9,11},{10,... | collective-permute-start | bytes 44 | tf_op jit(solution)/shard_map/ppermute | solution.py:143
  38.5 15.2 %collective-permute-start = (f32[3,1,1]{0,2,1:T(1,128)S(1)}, f32[3,1,1]{0,2,1:T(1,128)S(1)}, u32[]{:S(2)}, u32[]{:S(2)}) collective-permute-start(f32[3,1,1]{0,2,1:T(1,128)S(1)} %get-tuple-element.38), channel_id=1, source_target_pairs={{0,1},{1,2},{2,3},{3,0},{4,5},{5,6},{6,7},{7,4},{8,9},{9,10},{10,1... | collective-permute-start | bytes 44 | tf_op jit(solution)/shard_map/ppermute | solution.py:143
  38.5 5.1 %copy-start.1 = (f32[12,16,1024]{2,1,0:T(8,128)S(1)}, f32[12,16,1024]{2,1,0:T(8,128)}, u32[]{:S(2)}) copy-start(f32[12,16,1024]{2,1,0:T(8,128)} %shard_map.113) | copy-start | bytes 2359300
  39.5 41.4 %collective-permute-start.5 = (f32[2,3,16,1024]{3,2,1,0:T(8,128)}, f32[2,3,16,1024]{3,2,1,0:T(8,128)S(1)}, u32[]{:S(2)}, u32[]{:S(2)}) collective-permute-start(f32[2,3,16,1024]{3,2,1,0:T(8,128)} %get-tuple-element.21), channel_id=1, source_target_pairs={{0,3},{1,0},{2,1},{3,2},{4,7},{5,4},{6,5},{7,6},{8,11},{9,8},{10,9... | collective-permute-start | bytes 1179656 | tf_op jit(solution)/shard_map/ppermute | solution.py:143
  42.7 38.2 %collective-permute-start.4 = (f32[2,3,16,1024]{3,2,1,0:T(8,128)}, f32[2,3,16,1024]{3,2,1,0:T(8,128)S(1)}, u32[]{:S(2)}, u32[]{:S(2)}) collective-permute-start(f32[2,3,16,1024]{3,2,1,0:T(8,128)} %get-tuple-element.19), channel_id=1, source_target_pairs={{0,2},{1,3},{2,0},{3,1},{4,6},{5,7},{6,4},{7,5},{8,10},{9,11},{10,... | collective-permute-start | bytes 1179656 | tf_op jit(solution)/shard_map/ppermute | solution.py:143
  44.8 18.2 %all-to-all-start.1 = ((f32[12,16,128]{2,1,0:T(8,128)}), f32[12,16,128]{2,1,0:T(8,128)S(1)}, u32[]{:S(2)}, u32[]{:S(2)}) async-start(f32[12,16,128]{2,1,0:T(8,128)} %convolution_multiply_fusion.1), calls=%async_computation.1 | async-start | bytes 196608 | tf_op jit(solution)/shard_map/all_to_all | solution.py:221
  49.5 27.1 %collective-permute-start.8 = (f32[3,16,1024]{2,1,0:T(8,128)}, f32[3,16,1024]{2,1,0:T(8,128)}, u32[]{:S(2)}, u32[]{:S(2)}) collective-permute-start(f32[3,16,1024]{2,1,0:T(8,128)} %get-tuple-element.27), channel_id=1, source_target_pairs={{0,3},{1,0},{2,1},{3,2},{4,7},{5,4},{6,5},{7,6},{8,11},{9,8},{10,9... | collective-permute-start | bytes 589832 | tf_op jit(solution)/shard_map/ppermute | solution.py:143
  52.7 25.4 %collective-permute-start.7 = (f32[3,16,1024]{2,1,0:T(8,128)S(1)}, f32[3,16,1024]{2,1,0:T(8,128)}, u32[]{:S(2)}, u32[]{:S(2)}) collective-permute-start(f32[3,16,1024]{2,1,0:T(8,128)S(1)} %get-tuple-element.25), channel_id=1, source_target_pairs={{0,2},{1,3},{2,0},{3,1},{4,6},{5,7},{6,4},{7,5},{8,10},{9,11},{10,... | collective-permute-start | bytes 589832 | tf_op jit(solution)/shard_map/ppermute | solution.py:143
  53.6 24.5 %collective-permute-start.6 = (f32[3,16,1024]{2,1,0:T(8,128)S(1)}, f32[3,16,1024]{2,1,0:T(8,128)}, u32[]{:S(2)}, u32[]{:S(2)}) collective-permute-start(f32[3,16,1024]{2,1,0:T(8,128)S(1)} %get-tuple-element.26), channel_id=1, source_target_pairs={{0,1},{1,2},{2,3},{3,0},{4,5},{5,6},{6,7},{7,4},{8,9},{9,10},{10,1... | collective-permute-start | bytes 589832 | tf_op jit(solution)/shard_map/ppermute | solution.py:143
  64.3 27.1 %all-to-all-start.2 = ((f32[64,2,512]{2,1,0:T(2,128)}), f32[64,2,512]{2,1,0:T(2,128)}, u32[]{:S(2)}, u32[]{:S(2)}) async-start(f32[64,2,512]{2,1,0:T(2,128)} %copy.210), calls=%async_computation.2 | async-start | bytes 524288 | tf_op jit(solution)/shard_map/all_to_all | solution.py:230
  76.6 13.7 %collective-permute-start.3 = (f32[2,3,16,1024]{3,2,1,0:T(8,128)}, f32[2,3,16,1024]{3,2,1,0:T(8,128)S(1)}, u32[]{:S(2)}, u32[]{:S(2)}) collective-permute-start(f32[2,3,16,1024]{3,2,1,0:T(8,128)} %get-tuple-element.20), channel_id=1, source_target_pairs={{0,1},{1,2},{2,3},{3,0},{4,5},{5,6},{6,7},{7,4},{8,9},{9,10},{10,1... | collective-permute-start | bytes 1179656 | tf_op jit(solution)/shard_map/ppermute | solution.py:143
  93.9 9.3 %all-to-all-start.3 = ((f32[3,64,128]{2,0,1:T(4,128)}), f32[3,64,128]{2,0,1:T(4,128)S(1)}, u32[]{:S(2)}, u32[]{:S(2)}) async-start(f32[3,64,128]{2,0,1:T(4,128)} %copy.213), calls=%async_computation.3 | async-start | bytes 262144 | tf_op jit(solution)/shard_map/all_to_all | solution.py:130
  113.7 4.0 %copy-start.2 = (f32[12,16,1024]{2,1,0:T(8,128)S(1)}, f32[12,16,1024]{2,1,0:T(8,128)}, u32[]{:S(2)}) copy-start(f32[12,16,1024]{2,1,0:T(8,128)} %get-tuple-element.12) | copy-start | bytes 2359300
  115.1 8.7 %collective-permute-start.11 = (f32[64,256]{1,0:T(8,128)S(1)}, f32[64,256]{1,0:T(8,128)S(1)}, u32[]{:S(2)}, u32[]{:S(2)}) collective-permute-start(f32[64,256]{1,0:T(8,128)S(1)} %bitcast.192), channel_id=1, source_target_pairs={{0,3},{1,0},{2,1},{3,2},{4,7},{5,4},{6,5},{7,6},{8,11},{9,8},{10,9... | collective-permute-start | bytes 196616 | tf_op jit(solution)/shard_map/ppermute | solution.py:156
  116.3 7.5 %collective-permute-start.10 = (f32[64,256]{1,0:T(8,128)S(1)}, f32[64,256]{1,0:T(8,128)S(1)}, u32[]{:S(2)}, u32[]{:S(2)}) collective-permute-start(f32[64,256]{1,0:T(8,128)S(1)} %bitcast.193), channel_id=1, source_target_pairs={{0,2},{1,3},{2,0},{3,1},{4,6},{5,7},{6,4},{7,5},{8,10},{9,11},{10,... | collective-permute-start | bytes 196616 | tf_op jit(solution)/shard_map/ppermute | solution.py:156
  117.8 6.0 %collective-permute-start.9 = (f32[64,256]{1,0:T(8,128)S(1)}, f32[64,256]{1,0:T(8,128)S(1)}, u32[]{:S(2)}, u32[]{:S(2)}) collective-permute-start(f32[64,256]{1,0:T(8,128)S(1)} %bitcast.194), channel_id=1, source_target_pairs={{0,1},{1,2},{2,3},{3,0},{4,5},{5,6},{6,7},{7,4},{8,9},{9,10},{10,1... | collective-permute-start | bytes 196616 | tf_op jit(solution)/shard_map/ppermute | solution.py:156
  119.0 10.6 %all-to-all-start.4 = ((f32[12,16,128]{2,1,0:T(8,128)}), f32[12,16,128]{2,1,0:T(8,128)S(1)}, u32[]{:S(2)}, u32[]{:S(2)}) async-start(f32[12,16,128]{2,1,0:T(8,128)} %convolution_multiply_fusion), calls=%async_computation.4 | async-start | bytes 196608 | tf_op jit(solution)/shard_map/all_to_all | solution.py:221
  131.0 23.2 %all-to-all-start.5 = ((f32[64,2,640]{2,1,0:T(2,128)}), f32[64,2,640]{2,1,0:T(2,128)S(1)}, u32[]{:S(2)}, u32[]{:S(2)}) async-start(f32[64,2,640]{2,1,0:T(2,128)} %copy.224), calls=%async_computation.5 | async-start | bytes 655360 | tf_op jit(solution)/shard_map/all_to_all | solution.py:230
  155.6 9.3 %all-to-all-start.6 = ((f32[3,64,128]{2,0,1:T(4,128)}), f32[3,64,128]{2,0,1:T(4,128)S(1)}, u32[]{:S(2)}, u32[]{:S(2)}) async-start(f32[3,64,128]{2,0,1:T(4,128)} %copy.227), calls=%async_computation.6 | async-start | bytes 262144 | tf_op jit(solution)/shard_map/all_to_all | solution.py:130

commit v5 on v4

--- a/solution.py
+++ b/solution.py
@@ -79,7 +79,7 @@
     )(ep, adjoint, survive, mixing)
 
 
-def stencil_kernel(side_len, st_ref, v_ref, e_ref, n_ref, add_ref, o_ref):
+def stencil_kernel(side_len, st_ref, v_ref, e_ref, n_ref, o_ref):
     v = v_ref[...]
     east_c = e_ref[...]
     north_c = n_ref[...]
@@ -94,21 +94,21 @@
         north_adj = jnp.where(north_ok, pltpu.roll(v, cells - side_len, 1), 0.0)
         moved = keep * v + east_c * east_adj + north_c * north_adj
         v = jnp.where(substep < steps, moved, v)
-    o_ref[...] = v + add_ref[...]
-
-
-def advect(side_len, steps, adjoint, east_c, north_c, added):
+    o_ref[...] = v
+
+
+def advect(side_len, steps, adjoint, east_c, north_c):
     rows, cells = adjoint.shape
     tile = 64
     spec = pl.BlockSpec((tile, cells), lambda r: (r, 0))
     return pl.pallas_call(
         functools.partial(stencil_kernel, side_len),
         grid=(rows // tile,),
-        in_specs=[pl.BlockSpec((tile, 1), lambda r: (r, 0)), spec, spec, spec, spec],
+        in_specs=[pl.BlockSpec((tile, 1), lambda r: (r, 0)), spec, spec, spec],
         out_specs=spec,
         out_shape=jax.ShapeDtypeStruct(adjoint.shape, jnp.float32),
         interpret=INTERPRET,
-    )(steps, adjoint, east_c, north_c, added)
+    )(steps, adjoint, east_c, north_c)
 
 
 def face_matrix(side_len, cells):
@@ -146,6 +146,19 @@
     order = (lev_index - jnp.arange(lev_groups, dtype=jnp.int32)) % lev_groups
     got = jnp.take(got, order, axis=len(lead))
     return got.reshape(lead + (lev_groups * lev_dev, own, cells))
+
+
+def ring_exchange(x, lev_index, lev_groups):
+    got = []
+    for shift in range(lev_groups):
+        piece = lax.dynamic_index_in_dim(x, (lev_index + shift) % lev_groups, axis=0, keepdims=False)
+        if shift:
+            ring = [(src, (src + shift) % lev_groups) for src in range(lev_groups)]
+            piece = lax.ppermute(piece, "lev", ring)
+        got.append(piece)
+    got = jnp.stack(got, axis=0)
+    order = (lev_index - jnp.arange(lev_groups, dtype=jnp.int32)) % lev_groups
+    return jnp.take(got, order, axis=0)
 
 
 def ring_sum(x, lev_index, lev_groups):
@@ -242,24 +255,23 @@
             tile_got = got[:, face_width:]
         got = got[:, :face_width].reshape(peer_count * cap, lev_dev, cycle_len)
         arrivals = jnp.einsum("ts,slk->ltk", face_take, got, precision=HI)
-        arrivals = to_columns(arrivals).reshape(levels * own, cycle_len)
-        added = jnp.dot(arrivals, pick.T, precision=HI)
-        adjoint = advect(side_len, row_steps, flat, flows[0], flows[1], added).reshape(levels, own, cell_count)
+        advected = advect(side_len, row_steps, flat, flows[0], flows[1])
+        if step_index < STEPS - 1:
+            arrivals = to_columns(arrivals).reshape(levels * own, cycle_len)
+            added = jnp.dot(arrivals, pick.T, precision=HI)
+            adjoint = (advected + added).reshape(levels, own, cell_count)
+
+    by_dest = advected.reshape(lev_groups, lev_dev, own, cell_count)
+    by_src = ring_exchange(by_dest, lev_index, lev_groups)
+    advected = by_src.transpose(1, 0, 2, 3).reshape(lev_dev, blocks, cell_count)
+    added = jnp.dot(arrivals.reshape(lev_dev * blocks, cycle_len), pick.T, precision=HI)
+    adjoint_out = (advected + added.reshape(lev_dev, blocks, cell_count)).transpose(1, 0, 2)
 
     tile_parts = jnp.dot(tile_take, tile_got, precision=HI)
     tile_rows = group_size // lev_groups
-    packed = jnp.concatenate(
-        [
-            adjoint.reshape(lev_groups, lev_dev * own, cell_count),
-            tile_parts.reshape(lev_groups, 1, cell_count),
-        ],
-        axis=1,
-    )
-    packed = lax.all_to_all(packed, "lev", split_axis=0, concat_axis=0, tiled=True)
-    tile_grad = packed[:, lev_dev * own].reshape(lev_groups, tile_rows, cell_count // lev_groups)
+    tile_parts = tile_parts.reshape(lev_groups, tile_rows, cell_count // lev_groups)
+    tile_grad = ring_exchange(tile_parts, lev_index, lev_groups)
     tile_grad = tile_grad.transpose(1, 0, 2).reshape(tile_rows, cell_count)
-    adjoint_out = packed[:, : lev_dev * own].reshape(lev_groups, lev_dev, own, cell_count)
-    adjoint_out = adjoint_out.transpose(0, 2, 1, 3).reshape(blocks, lev_dev, cell_count)
     return (adjoint_out, tile_grad)
 
 

time: 191 us -> 169 us (0.88)
  blocking collectives: 15.6 us -> 0 us
  waiting for transfers between devices: 63.9 us -> 50.7 us
  starting transfers between devices: 58.4 us -> 64.9 us
    all_to_all x1 -> x0, blocking collectives: 15.6 us -> none  [local(): lax.all_to_all(packed, 'lev', split_axis=0, concat_axis=0, tiled=True)]
    ppermute x9, waiting for transfers between devices: 9.38 us -> 23.7 us  [ring_columns(): piece = lax.ppermute(piece, 'lev', ring)]
    all_to_all x2, waiting for transfers between devices: 12.8 us -> 0.01 us  [local(): got = lax.all_to_all(sent, 'blk', split_axis=0, concat_axis=0, tiled=True)]
    all_to_all x2, waiting for transfers between devices: 12.8 us -> 0.46 us  [local(): lax.all_to_all(cycle_out, 'lev', split_axis=0, concat_axis=1, tiled=True)]
    ppermute x0 -> x6, starting transfers between devices: none -> 11.1 us  [ring_exchange(): piece = lax.ppermute(piece, 'lev', ring)]
    all_to_all x3 -> x2, waiting for transfers between devices: 28.9 us -> 18.7 us  [to_columns(): lax.all_to_all(x, 'lev', split_axis=x.ndim - 2, concat_axis=x.ndim - 3, t...]
    ppermute x0 -> x6, waiting for transfers between devices: none -> 7.86 us  [ring_exchange(): piece = lax.ppermute(piece, 'lev', ring)]
    ppermute x9, starting transfers between devices: 13.2 us -> 9.31 us  [ring_columns(): piece = lax.ppermute(piece, 'lev', ring)]
  transfers between devices with their start and end apart: 19 -> 24, of which waited for: 7 -> 9; matrix products, arithmetic and copies ran while one was open for 8% -> 10% of each run, Pallas kernels for 0% -> 6%
where the time goes in v5:
time: 169 us; the launch traced here: 168 us
  starting transfers between devices  64.9 us (38%)
  waiting for transfers between devices  50.7 us (30%)
  Pallas kernels  17.6 us (10%)
  local copies, waits for them, and re-layouts  17.3 us (10%)
  matrix products  8.16 us (5%)
  other arithmetic  7.99 us (5%)
    ppermute x9, waiting for transfers between devices, ring_columns(): piece = lax.ppermute(piece, 'lev', ring)  23.7 us
    all_to_all x2, starting transfers between devices, local(): got = lax.all_to_all(sent, 'blk', split_axis=0, concat_axis=0, tiled=True)  22.6 us
    all_to_all x2, waiting for transfers between devices, to_columns(): lax.all_to_all(x, 'lev', split_axis=x.ndim - 2, concat_axis=x.ndim - 3, t...  18.7 us
    ppermute x6, starting transfers between devices, ring_exchange(): piece = lax.ppermute(piece, 'lev', ring)  11.1 us
    pallas_call x2, Pallas kernels, advect(): pl.pallas_call(functools.partial(stencil_kernel, side_len), grid=(rows //...  9.91 us
    ppermute x9, starting transfers between devices, ring_columns(): piece = lax.ppermute(piece, 'lev', ring)  9.31 us
    all_to_all x2, starting transfers between devices, to_columns(): lax.all_to_all(x, 'lev', split_axis=x.ndim - 2, concat_axis=x.ndim - 3, t...  9.01 us
    ppermute x6, waiting for transfers between devices, ring_exchange(): piece = lax.ppermute(piece, 'lev', ring)  7.86 us
  transfers between devices with their start and end apart: 24, of which 9 were waited for; matrix products, arithmetic and copies ran while one was open for 10% of the time, Pallas kernels for 6%

profile of v5, /device:TPU:8, one launch (start us, length us, event | category | flops | bytes accessed | tf_op | source)
XLA Modules:
  0.0 167.9 jit_solution(12122266190367151054)
XLA Ops:
  0.7 1.7 %multiply_reduce_fusion = (f32[64,1024]{1,0:T(8,128)S(1)}, f32[1,64,3,1024]{3,1,2,0:T(8,128)S(1)}, f32[3,64,1024]{2,1,0:T(8,128)S(1)}) fusion(f32[64,3,1024]{2,0,1:T(8,128)} %param.12, f32[3]{0:T(128)} %param.20, f32[64,3,1024]{2,0,1:T(8,128)} %param.15), kind=kLoop, calls=%fused_computation.21 | loop fusion | flops 720896 | bytes 3407884 | tf_op jit(solution)/shard_map/reduce_sum | solution.py:200
  2.5 2.4 %copy.180 = f32[2,3,64,1024]{3,0,1,2:T(2,128)} copy(f32[2,3,64,1024]{3,2,1,0:T(8,128)S(1)} %maximum_bitcast_fusion) | data formatting | bytes 3145728 | tf_op jit(solution)/shard_map/transpose | solution.py:196
  5.0 4.4 %all-to-all-start = ((f32[2,3,64,1024]{3,0,1,2:T(2,128)}), f32[2,3,64,1024]{3,0,1,2:T(2,128)S(1)}, u32[]{:S(2)}, u32[]{:S(2)}) async-start(f32[2,3,64,1024]{3,0,1,2:T(2,128)} %copy.180), calls=%async_computation | async-start | bytes 3145728 | tf_op jit(solution)/shard_map/all_to_all | solution.py:130
  9.5 0.7 broadcast_in_dim_tile.4.st_ref
  11.4 18.7 %all-to-all-done = f32[2,3,64,1024]{3,0,1,2:T(2,128)S(1)} async-done(((f32[2,3,64,1024]{3,0,1,2:T(2,128)}), f32[2,3,64,1024]{3,0,1,2:T(2,128)S(1)}, u32[]{:S(2)}, u32[]{:S(2)}) %all-to-all-start) | async-done | bytes 1572896 | tf_op jit(solution)/shard_map/all_to_all | solution.py:130
  30.6 1.3 fusion.63
  31.9 3.7 %shard_map.113 = f32[12,16,1024]{2,1,0:T(8,128)} custom-call(f32[12,16,1024]{2,1,0:T(8,128)} %bitcast.187, f32[12,16,1024]{2,1,0:T(8,128)} %bitcast.172), custom_call_target="tpu_custom_call" | custom-call | tf_op jit(solution)/shard_map/pallas_call | solution.py:62
  35.6 0.8 dynamic-slice_bitcast_fusion.10
  37.0 2.1 %collective-permute-start.7 = (f32[3,16,1024]{2,1,0:T(8,128)}, f32[3,16,1024]{2,1,0:T(8,128)}, u32[]{:S(2)}, u32[]{:S(2)}) collective-permute-start(f32[3,16,1024]{2,1,0:T(8,128)} %get-tuple-element.33), channel_id=1, source_target_pairs={{0,2},{1,3},{2,0},{3,1},{4,6},{5,7},{6,4},{7,5},{8,10},{9,11},{10,... | collective-permute-start | bytes 589832 | tf_op jit(solution)/shard_map/ppermute | solution.py:143
  39.7 1.1 dynamic-slice_bitcast_fusion.3
  40.8 1.4 collective-permute-start.3
  42.2 1.2 convolution_multiply_fusion.1
  43.4 3.3 %all-to-all-start.1 = ((f32[12,16,128]{2,1,0:T(8,128)}), f32[12,16,128]{2,1,0:T(8,128)S(1)}, u32[]{:S(2)}, u32[]{:S(2)}) async-start(f32[12,16,128]{2,1,0:T(8,128)} %convolution_multiply_fusion.1), calls=%async_computation.1 | async-start | bytes 196608 | tf_op jit(solution)/shard_map/all_to_all | solution.py:234
  46.7 2.0 %collective-permute-start = (f32[3,1,1]{0,2,1:T(1,128)S(1)}, f32[3,1,1]{0,2,1:T(1,128)S(1)}, u32[]{:S(2)}, u32[]{:S(2)}) collective-permute-start(f32[3,1,1]{0,2,1:T(1,128)S(1)} %get-tuple-element.47), channel_id=1, source_target_pairs={{0,1},{1,2},{2,3},{3,0},{4,5},{5,6},{6,7},{7,4},{8,9},{9,10},{10,1... | collective-permute-start | bytes 44 | tf_op jit(solution)/shard_map/ppermute | solution.py:143
  48.7 8.5 %collective-permute-done = f32[3,1,1]{0,2,1:T(1,128)S(1)} collective-permute-done((f32[3,1,1]{0,2,1:T(1,128)S(1)}, f32[3,1,1]{0,2,1:T(1,128)S(1)}, u32[]{:S(2)}, u32[]{:S(2)}) %collective-permute-start) | collective-permute-done | bytes 44 | tf_op jit(solution)/shard_map/ppermute | solution.py:143
  57.2 5.1 %collective-permute-done.1 = f32[3,1,1]{0,2,1:T(1,128)S(1)} collective-permute-done((f32[3,1,1]{0,2,1:T(1,128)S(1)}, f32[3,1,1]{0,2,1:T(1,128)S(1)}, u32[]{:S(2)}, u32[]{:S(2)}) %collective-permute-start.1) | collective-permute-done | bytes 44 | tf_op jit(solution)/shard_map/ppermute | solution.py:143
  62.3 3.6 %collective-permute-done.2 = f32[3,1,1]{0,2,1:T(1,128)S(1)} collective-permute-done((f32[3,1,1]{0,2,1:T(1,128)S(1)}, f32[3,1,1]{0,2,1:T(1,128)S(1)}, u32[]{:S(2)}, u32[]{:S(2)}) %collective-permute-start.2) | collective-permute-done | bytes 44 | tf_op jit(solution)/shard_map/ppermute | solution.py:143
  67.5 0.9 copy.191
  68.4 12.3 %all-to-all-start.2 = ((f32[64,2,512]{2,1,0:T(2,128)}), f32[64,2,512]{2,1,0:T(2,128)}, u32[]{:S(2)}, u32[]{:S(2)}) async-start(f32[64,2,512]{2,1,0:T(2,128)} %copy.191), calls=%async_computation.2 | async-start | bytes 524288 | tf_op jit(solution)/shard_map/all_to_all | solution.py:243
  80.8 2.7 %collective-permute-start.5 = (f32[2,3,16,1024]{3,2,1,0:T(8,128)}, f32[2,3,16,1024]{3,2,1,0:T(8,128)}, u32[]{:S(2)}, u32[]{:S(2)}) collective-permute-start(f32[2,3,16,1024]{3,2,1,0:T(8,128)} %get-tuple-element.22), channel_id=1, source_target_pairs={{0,3},{1,0},{2,1},{3,2},{4,7},{5,4},{6,5},{7,6},{8,11},{9,8},{10,9... | collective-permute-start | bytes 1179656 | tf_op jit(solution)/shard_map/ppermute | solution.py:143
  83.4 1.1 pad_maximum_fusion.1
  85.1 1.1 broadcast_select_fusion
  86.2 6.6 %collective-permute-done.5 = f32[2,3,16,1024]{3,2,1,0:T(8,128)} collective-permute-done((f32[2,3,16,1024]{3,2,1,0:T(8,128)}, f32[2,3,16,1024]{3,2,1,0:T(8,128)}, u32[]{:S(2)}, u32[]{:S(2)}) %collective-permute-start.5) | collective-permute-done | bytes 393248 | tf_op jit(solution)/shard_map/ppermute | solution.py:143
  92.8 1.1 pad_maximum_fusion
  94.9 1.1 reshape.223
  97.4 4.6 %all-to-all-start.3 = ((f32[3,64,128]{2,0,1:T(4,128)}), f32[3,64,128]{2,0,1:T(4,128)S(1)}, u32[]{:S(2)}, u32[]{:S(2)}) async-start(f32[3,64,128]{2,0,1:T(4,128)} %copy.194), calls=%async_computation.3 | async-start | bytes 262144 | tf_op jit(solution)/shard_map/all_to_all | solution.py:130
  102.0 1.3 fusion.62
  103.3 4.9 %shard_map.114 = f32[192,1024]{1,0:T(8,128)} custom-call(s32[192,1]{1,0:T(8,128)} %broadcast_in_dim_tile.4.st_ref, f32[192,1024]{1,0:T(8,128)} %bitcast.174, f32[192,1024]{1,0:T(8,128)} %bitcast.177, f32[192,1024]{1,0:T(8,128)} %bitcast.175), custom_call_target="tpu_custom_call" | custom-call | tf_op jit(solution)/shard_map/pallas_call | solution.py:104
  108.2 2.5 %convolution_add_fusion.1 = f32[192,1024]{1,0:T(8,128)} fusion(f32[192,1024]{1,0:T(8,128)} %shard_map.114, f32[192,128]{1,0:T(8,128)S(1)} %bitcast.196, s32[128]{0:T(128)S(1)} %pad_add_fusion), kind=kOutput, calls=%fused_computation.11 | convolution fusion | flops 302317568 | bytes 1671680 | tf_op jit(solution)/shard_map/dot_general | solution.py:261
  110.8 3.9 %shard_map.115 = (f32[12,16,1024]{2,1,0:T(8,128)}, f32[16,1024]{1,0:T(8,128)}) custom-call(f32[12]{0:T(128)} %reshape.288.ep_ref, f32[12,16,1024]{2,1,0:T(8,128)} %bitcast.182, f32[12,16,1024]{2,1,0:T(8,128)} %bitcast.181, f32[12,16,1024]{2,1,0:T(8,128)} %bitcast.173), custom_call_target="tpu_custom_call" | custom-call | tf_op jit(solution)/shard_map/pallas_call | solution.py:71
  114.7 0.9 add_dynamic-update-slice_fusion
  116.0 2.1 %collective-permute-start.12 = (f32[64,256]{1,0:T(8,128)S(1)}, f32[64,256]{1,0:T(8,128)S(1)}, u32[]{:S(2)}, u32[]{:S(2)}) collective-permute-start(f32[64,256]{1,0:T(8,128)S(1)} %bitcast.206), channel_id=1, source_target_pairs={{0,1},{1,2},{2,3},{3,0},{4,5},{5,6},{6,7},{7,4},{8,9},{9,10},{10,1... | collective-permute-start | bytes 196616 | tf_op jit(solution)/shard_map/ppermute | solution.py:169
  118.1 2.7 %collective-permute-start.13 = (f32[64,256]{1,0:T(8,128)S(1)}, f32[64,256]{1,0:T(8,128)S(1)}, u32[]{:S(2)}, u32[]{:S(2)}) collective-permute-start(f32[64,256]{1,0:T(8,128)S(1)} %bitcast.207), channel_id=1, source_target_pairs={{0,2},{1,3},{2,0},{3,1},{4,6},{5,7},{6,4},{7,5},{8,10},{9,11},{10,... | collective-permute-start | bytes 196616 | tf_op jit(solution)/shard_map/ppermute | solution.py:169
  120.8 1.5 collective-permute-start.14
  122.2 1.2 convolution_multiply_fusion
  123.4 3.3 %all-to-all-start.4 = ((f32[12,16,128]{2,1,0:T(8,128)}), f32[12,16,128]{2,1,0:T(8,128)S(1)}, u32[]{:S(2)}, u32[]{:S(2)}) async-start(f32[12,16,128]{2,1,0:T(8,128)} %convolution_multiply_fusion), calls=%async_computation.4 | async-start | bytes 196608 | tf_op jit(solution)/shard_map/all_to_all | solution.py:234
  126.8 5.0 %shard_map.116 = f32[192,1024]{1,0:T(8,128)} custom-call(s32[192,1]{1,0:T(8,128)} %broadcast_in_dim_tile.4.st_ref, f32[192,1024]{1,0:T(8,128)} %bitcast.186, f32[192,1024]{1,0:T(8,128)} %bitcast.178, f32[192,1024]{1,0:T(8,128)} %bitcast.176), custom_call_target="tpu_custom_call" | custom-call | tf_op jit(solution)/shard_map/pallas_call | solution.py:104
  133.0 1.0 copy.206
  134.0 10.3 %all-to-all-start.5 = ((f32[64,2,640]{2,1,0:T(2,128)}), f32[64,2,640]{2,1,0:T(2,128)S(1)}, u32[]{:S(2)}, u32[]{:S(2)}) async-start(f32[64,2,640]{2,1,0:T(2,128)} %copy.206), calls=%async_computation.5 | async-start | bytes 655360 | tf_op jit(solution)/shard_map/all_to_all | solution.py:243
  144.4 1.6 collective-permute-start.9
  146.0 2.7 %collective-permute-start.10 = (f32[3,16,1024]{2,1,0:T(8,128)S(1)}, f32[3,16,1024]{2,1,0:T(8,128)S(1)}, u32[]{:S(2)}, u32[]{:S(2)}) collective-permute-start(f32[3,16,1024]{2,1,0:T(8,128)S(1)} %get-tuple-element.30), channel_id=1, source_target_pairs={{0,2},{1,3},{2,0},{3,1},{4,6},{5,7},{6,4},{7,5},{8,10},{9,11},{10,... | collective-permute-start | bytes 589832 | tf_op jit(solution)/shard_map/ppermute | solution.py:157
  148.7 1.5 collective-permute-start.11
  150.1 2.5 %collective-permute-done.9 = f32[3,16,1024]{2,1,0:T(8,128)S(1)} collective-permute-done((f32[3,16,1024]{2,1,0:T(8,128)S(1)}, f32[3,16,1024]{2,1,0:T(8,128)S(1)}, u32[]{:S(2)}, u32[]{:S(2)}) %collective-permute-start.9) | collective-permute-done | bytes 196640 | tf_op jit(solution)/shard_map/ppermute | solution.py:157
  152.6 5.2 %collective-permute-done.10 = f32[3,16,1024]{2,1,0:T(8,128)S(1)} collective-permute-done((f32[3,16,1024]{2,1,0:T(8,128)S(1)}, f32[3,16,1024]{2,1,0:T(8,128)S(1)}, u32[]{:S(2)}, u32[]{:S(2)}) %collective-permute-start.10) | collective-permute-done | bytes 196640 | tf_op jit(solution)/shard_map/ppermute | solution.py:157
  159.3 1.4 collective-permute-start.15
  160.7 2.4 %collective-permute-start.16 = (f32[4,256]{1,0:T(4,128)S(1)}, f32[4,256]{1,0:T(4,128)S(1)}, u32[]{:S(2)}, u32[]{:S(2)}) collective-permute-start(f32[4,256]{1,0:T(4,128)S(1)} %get-tuple-element.42), channel_id=1, source_target_pairs={{0,2},{1,3},{2,0},{3,1},{4,6},{5,7},{6,4},{7,5},{8,10},{9,11},{10,... | collective-permute-start | bytes 12296 | tf_op jit(solution)/shard_map/ppermute | solution.py:157
  163.1 1.6 collective-permute-start.17
  165.1 1.4 fusion
  (121 shorter events, 12.5 us)
Async XLA Ops:
  0.6 10.8 %copy-start = (f32[64,128]{1,0:T(8,128)S(1)}, f32[64,128]{1,0:T(8,128)}, u32[]{:S(2)}) copy-start(f32[64,128]{1,0:T(8,128)} %param.17) | copy-start | bytes 98308
  0.6 1.8 %copy-start.5 = (f32[64,3,1024]{2,0,1:T(8,128)S(1)}, f32[64,3,1024]{2,0,1:T(8,128)}, u32[]{:S(2)}) copy-start(f32[64,3,1024]{2,0,1:T(8,128)} %param.14) | copy-start | bytes 2359300
  4.9 4.5 %copy-start.7 = (s32[64]{0:T(128)S(1)}, s32[64]{0:T(128)}, u32[]{:S(2)}) copy-start(s32[64]{0:T(128)} %param.16) | copy-start | bytes 772
  4.9 5.3 %copy-start.8 = (s32[64,1]{0,1:T(1,128)S(1)}, s32[64,1]{0,1:T(1,128)}, u32[]{:S(2)}) copy-start(s32[64,1]{0,1:T(1,128)} %param.18) | copy-start | bytes 772
  4.9 5.5 %copy-start.9 = (s32[64]{0:T(128)S(1)}, s32[64]{0:T(128)}, u32[]{:S(2)}) copy-start(s32[64]{0:T(128)} %param.21) | copy-start | bytes 772
  5.0 5.8 %copy-start.10 = (s32[64]{0:T(128)S(1)}, s32[64]{0:T(128)}, u32[]{:S(2)}) copy-start(s32[64]{0:T(128)} %param.19) | copy-start | bytes 772
  5.0 25.1 %all-to-all-start = ((f32[2,3,64,1024]{3,0,1,2:T(2,128)}), f32[2,3,64,1024]{3,0,1,2:T(2,128)S(1)}, u32[]{:S(2)}, u32[]{:S(2)}) async-start(f32[2,3,64,1024]{3,0,1,2:T(2,128)} %copy.180), calls=%async_computation | async-start | bytes 3145728 | tf_op jit(solution)/shard_map/all_to_all | solution.py:130
  31.9 3.7 %copy-start.6 = (f32[3]{0:T(128)S(1)}, f32[3]{0:T(128)}, u32[]{:S(2)}) copy-start(f32[3]{0:T(128)} %param.20) | copy-start | bytes 40
  35.6 4.1 %copy-start.4 = (f32[2,64,3,1024]{3,1,2,0:T(8,128)S(1)}, f32[2,64,3,1024]{3,1,2,0:T(8,128)}, u32[]{:S(2)}) copy-start(f32[2,64,3,1024]{3,1,2,0:T(8,128)} %param.13) | copy-start | bytes 4718596
  36.5 44.3 %collective-permute-start.6 = (f32[3,16,1024]{2,1,0:T(8,128)}, f32[3,16,1024]{2,1,0:T(8,128)S(1)}, u32[]{:S(2)}, u32[]{:S(2)}) collective-permute-start(f32[3,16,1024]{2,1,0:T(8,128)} %get-tuple-element.34), channel_id=1, source_target_pairs={{0,1},{1,2},{2,3},{3,0},{4,5},{5,6},{6,7},{7,4},{8,9},{9,10},{10,1... | collective-permute-start | bytes 589832 | tf_op jit(solution)/shard_map/ppermute | solution.py:143
  37.0 46.4 %collective-permute-start.7 = (f32[3,16,1024]{2,1,0:T(8,128)}, f32[3,16,1024]{2,1,0:T(8,128)}, u32[]{:S(2)}, u32[]{:S(2)}) collective-permute-start(f32[3,16,1024]{2,1,0:T(8,128)} %get-tuple-element.33), channel_id=1, source_target_pairs={{0,2},{1,3},{2,0},{3,1},{4,6},{5,7},{6,4},{7,5},{8,10},{9,11},{10,... | collective-permute-start | bytes 589832 | tf_op jit(solution)/shard_map/ppermute | solution.py:143
  39.1 44.3 %collective-permute-start.8 = (f32[3,16,1024]{2,1,0:T(8,128)S(1)}, f32[3,16,1024]{2,1,0:T(8,128)}, u32[]{:S(2)}, u32[]{:S(2)}) collective-permute-start(f32[3,16,1024]{2,1,0:T(8,128)S(1)} %get-tuple-element.35), channel_id=1, source_target_pairs={{0,3},{1,0},{2,1},{3,2},{4,7},{5,4},{6,5},{7,6},{8,11},{9,8},{10,9... | collective-permute-start | bytes 589832 | tf_op jit(solution)/shard_map/ppermute | solution.py:143
  39.7 2.5 %copy-start.1 = (f32[12,16,1024]{2,1,0:T(8,128)S(1)}, f32[12,16,1024]{2,1,0:T(8,128)}, u32[]{:S(2)}) copy-start(f32[12,16,1024]{2,1,0:T(8,128)} %shard_map.113) | copy-start | bytes 2359300
  40.8 45.4 %collective-permute-start.3 = (f32[2,3,16,1024]{3,2,1,0:T(8,128)}, f32[2,3,16,1024]{3,2,1,0:T(8,128)S(1)}, u32[]{:S(2)}, u32[]{:S(2)}) collective-permute-start(f32[2,3,16,1024]{3,2,1,0:T(8,128)} %get-tuple-element.21), channel_id=1, source_target_pairs={{0,1},{1,2},{2,3},{3,0},{4,5},{5,6},{6,7},{7,4},{8,9},{9,10},{10,1... | collective-permute-start | bytes 1179656 | tf_op jit(solution)/shard_map/ppermute | solution.py:143
  43.4 23.7 %all-to-all-start.1 = ((f32[12,16,128]{2,1,0:T(8,128)}), f32[12,16,128]{2,1,0:T(8,128)S(1)}, u32[]{:S(2)}, u32[]{:S(2)}) async-start(f32[12,16,128]{2,1,0:T(8,128)} %convolution_multiply_fusion.1), calls=%async_computation.1 | async-start | bytes 196608 | tf_op jit(solution)/shard_map/all_to_all | solution.py:234
  46.7 10.4 %collective-permute-start = (f32[3,1,1]{0,2,1:T(1,128)S(1)}, f32[3,1,1]{0,2,1:T(1,128)S(1)}, u32[]{:S(2)}, u32[]{:S(2)}) collective-permute-start(f32[3,1,1]{0,2,1:T(1,128)S(1)} %get-tuple-element.47), channel_id=1, source_target_pairs={{0,1},{1,2},{2,3},{3,0},{4,5},{5,6},{6,7},{7,4},{8,9},{9,10},{10,1... | collective-permute-start | bytes 44 | tf_op jit(solution)/shard_map/ppermute | solution.py:143
  57.2 5.1 %collective-permute-start.1 = (f32[3,1,1]{0,2,1:T(1,128)S(1)}, f32[3,1,1]{0,2,1:T(1,128)S(1)}, u32[]{:S(2)}, u32[]{:S(2)}) collective-permute-start(f32[3,1,1]{0,2,1:T(1,128)S(1)} %get-tuple-element.46), channel_id=1, source_target_pairs={{0,2},{1,3},{2,0},{3,1},{4,6},{5,7},{6,4},{7,5},{8,10},{9,11},{10,... | collective-permute-start | bytes 44 | tf_op jit(solution)/shard_map/ppermute | solution.py:143
  62.3 3.6 %collective-permute-start.2 = (f32[3,1,1]{0,2,1:T(1,128)S(1)}, f32[3,1,1]{0,2,1:T(1,128)S(1)}, u32[]{:S(2)}, u32[]{:S(2)}) collective-permute-start(f32[3,1,1]{0,2,1:T(1,128)S(1)} %get-tuple-element.45), channel_id=1, source_target_pairs={{0,3},{1,0},{2,1},{3,2},{4,7},{5,4},{6,5},{7,6},{8,11},{9,8},{10,9... | collective-permute-start | bytes 44 | tf_op jit(solution)/shard_map/ppermute | solution.py:143
  65.8 20.4 %collective-permute-start.4 = (f32[2,3,16,1024]{3,2,1,0:T(8,128)}, f32[2,3,16,1024]{3,2,1,0:T(8,128)S(1)}, u32[]{:S(2)}, u32[]{:S(2)}) collective-permute-start(f32[2,3,16,1024]{3,2,1,0:T(8,128)} %get-tuple-element.20), channel_id=1, source_target_pairs={{0,2},{1,3},{2,0},{3,1},{4,6},{5,7},{6,4},{7,5},{8,10},{9,11},{10,... | collective-permute-start | bytes 1179656 | tf_op jit(solution)/shard_map/ppermute | solution.py:143
  68.4 26.5 %all-to-all-start.2 = ((f32[64,2,512]{2,1,0:T(2,128)}), f32[64,2,512]{2,1,0:T(2,128)}, u32[]{:S(2)}, u32[]{:S(2)}) async-start(f32[64,2,512]{2,1,0:T(2,128)} %copy.191), calls=%async_computation.2 | async-start | bytes 524288 | tf_op jit(solution)/shard_map/all_to_all | solution.py:243
  80.8 12.0 %collective-permute-start.5 = (f32[2,3,16,1024]{3,2,1,0:T(8,128)}, f32[2,3,16,1024]{3,2,1,0:T(8,128)}, u32[]{:S(2)}, u32[]{:S(2)}) collective-permute-start(f32[2,3,16,1024]{3,2,1,0:T(8,128)} %get-tuple-element.22), channel_id=1, source_target_pairs={{0,3},{1,0},{2,1},{3,2},{4,7},{5,4},{6,5},{7,6},{8,11},{9,8},{10,9... | collective-permute-start | bytes 1179656 | tf_op jit(solution)/shard_map/ppermute | solution.py:143
  97.4 10.8 %all-to-all-start.3 = ((f32[3,64,128]{2,0,1:T(4,128)}), f32[3,64,128]{2,0,1:T(4,128)S(1)}, u32[]{:S(2)}, u32[]{:S(2)}) async-start(f32[3,64,128]{2,0,1:T(4,128)} %copy.194), calls=%async_computation.3 | async-start | bytes 262144 | tf_op jit(solution)/shard_map/all_to_all | solution.py:130
  114.7 7.6 %copy-start.3 = (f32[12,16,1024]{2,1,0:T(8,128)S(1)}, f32[12,16,1024]{2,1,0:T(8,128)}, u32[]{:S(2)}) copy-start(f32[12,16,1024]{2,1,0:T(8,128)} %get-tuple-element.13) | copy-start | bytes 2359300
  116.0 15.7 %collective-permute-start.12 = (f32[64,256]{1,0:T(8,128)S(1)}, f32[64,256]{1,0:T(8,128)S(1)}, u32[]{:S(2)}, u32[]{:S(2)}) collective-permute-start(f32[64,256]{1,0:T(8,128)S(1)} %bitcast.206), channel_id=1, source_target_pairs={{0,1},{1,2},{2,3},{3,0},{4,5},{5,6},{6,7},{7,4},{8,9},{9,10},{10,1... | collective-permute-start | bytes 196616 | tf_op jit(solution)/shard_map/ppermute | solution.py:169
  118.1 13.6 %collective-permute-start.13 = (f32[64,256]{1,0:T(8,128)S(1)}, f32[64,256]{1,0:T(8,128)S(1)}, u32[]{:S(2)}, u32[]{:S(2)}) collective-permute-start(f32[64,256]{1,0:T(8,128)S(1)} %bitcast.207), channel_id=1, source_target_pairs={{0,2},{1,3},{2,0},{3,1},{4,6},{5,7},{6,4},{7,5},{8,10},{9,11},{10,... | collective-permute-start | bytes 196616 | tf_op jit(solution)/shard_map/ppermute | solution.py:169
  120.8 10.9 %collective-permute-start.14 = (f32[64,256]{1,0:T(8,128)S(1)}, f32[64,256]{1,0:T(8,128)S(1)}, u32[]{:S(2)}, u32[]{:S(2)}) collective-permute-start(f32[64,256]{1,0:T(8,128)S(1)} %bitcast.208), channel_id=1, source_target_pairs={{0,3},{1,0},{2,1},{3,2},{4,7},{5,4},{6,5},{7,6},{8,11},{9,8},{10,9... | collective-permute-start | bytes 196616 | tf_op jit(solution)/shard_map/ppermute | solution.py:169
  123.4 9.1 %all-to-all-start.4 = ((f32[12,16,128]{2,1,0:T(8,128)}), f32[12,16,128]{2,1,0:T(8,128)S(1)}, u32[]{:S(2)}, u32[]{:S(2)}) async-start(f32[12,16,128]{2,1,0:T(8,128)} %convolution_multiply_fusion), calls=%async_computation.4 | async-start | bytes 196608 | tf_op jit(solution)/shard_map/all_to_all | solution.py:234
  132.0 12.3 %copy-start.2 = (f32[192,1024]{1,0:T(8,128)S(1)}, f32[192,1024]{1,0:T(8,128)}, u32[]{:S(2)}) copy-start(f32[192,1024]{1,0:T(8,128)} %shard_map.116) | copy-start | bytes 2359300
  134.0 24.8 %all-to-all-start.5 = ((f32[64,2,640]{2,1,0:T(2,128)}), f32[64,2,640]{2,1,0:T(2,128)S(1)}, u32[]{:S(2)}, u32[]{:S(2)}) async-start(f32[64,2,640]{2,1,0:T(2,128)} %copy.206), calls=%async_computation.5 | async-start | bytes 655360 | tf_op jit(solution)/shard_map/all_to_all | solution.py:243
  144.4 8.2 %collective-permute-start.9 = (f32[3,16,1024]{2,1,0:T(8,128)S(1)}, f32[3,16,1024]{2,1,0:T(8,128)S(1)}, u32[]{:S(2)}, u32[]{:S(2)}) collective-permute-start(f32[3,16,1024]{2,1,0:T(8,128)S(1)} %get-tuple-element.31), channel_id=1, source_target_pairs={{0,1},{1,2},{2,3},{3,0},{4,5},{5,6},{6,7},{7,4},{8,9},{9,10},{10,1... | collective-permute-start | bytes 589832 | tf_op jit(solution)/shard_map/ppermute | solution.py:157
  146.0 11.8 %collective-permute-start.10 = (f32[3,16,1024]{2,1,0:T(8,128)S(1)}, f32[3,16,1024]{2,1,0:T(8,128)S(1)}, u32[]{:S(2)}, u32[]{:S(2)}) collective-permute-start(f32[3,16,1024]{2,1,0:T(8,128)S(1)} %get-tuple-element.30), channel_id=1, source_target_pairs={{0,2},{1,3},{2,0},{3,1},{4,6},{5,7},{6,4},{7,5},{8,10},{9,11},{10,... | collective-permute-start | bytes 589832 | tf_op jit(solution)/shard_map/ppermute | solution.py:157
  148.7 9.1 %collective-permute-start.11 = (f32[3,16,1024]{2,1,0:T(8,128)S(1)}, f32[3,16,1024]{2,1,0:T(8,128)S(1)}, u32[]{:S(2)}, u32[]{:S(2)}) collective-permute-start(f32[3,16,1024]{2,1,0:T(8,128)S(1)} %get-tuple-element.29), channel_id=1, source_target_pairs={{0,3},{1,0},{2,1},{3,2},{4,7},{5,4},{6,5},{7,6},{8,11},{9,8},{10,9... | collective-permute-start | bytes 589832 | tf_op jit(solution)/shard_map/ppermute | solution.py:157
  159.3 7.2 %collective-permute-start.15 = (f32[4,256]{1,0:T(4,128)S(1)}, f32[4,256]{1,0:T(4,128)S(1)}, u32[]{:S(2)}, u32[]{:S(2)}) collective-permute-start(f32[4,256]{1,0:T(4,128)S(1)} %get-tuple-element.43), channel_id=1, source_target_pairs={{0,1},{1,2},{2,3},{3,0},{4,5},{5,6},{6,7},{7,4},{8,9},{9,10},{10,1... | collective-permute-start | bytes 12296 | tf_op jit(solution)/shard_map/ppermute | solution.py:157
  160.7 5.8 %collective-permute-start.16 = (f32[4,256]{1,0:T(4,128)S(1)}, f32[4,256]{1,0:T(4,128)S(1)}, u32[]{:S(2)}, u32[]{:S(2)}) collective-permute-start(f32[4,256]{1,0:T(4,128)S(1)} %get-tuple-element.42), channel_id=1, source_target_pairs={{0,2},{1,3},{2,0},{3,1},{4,6},{5,7},{6,4},{7,5},{8,10},{9,11},{10,... | collective-permute-start | bytes 12296 | tf_op jit(solution)/shard_map/ppermute | solution.py:157
  163.1 3.6 %collective-permute-start.17 = (f32[4,256]{1,0:T(4,128)S(1)}, f32[4,256]{1,0:T(4,128)S(1)}, u32[]{:S(2)}, u32[]{:S(2)}) collective-permute-start(f32[4,256]{1,0:T(4,128)S(1)} %get-tuple-element.41), channel_id=1, source_target_pairs={{0,3},{1,0},{2,1},{3,2},{4,7},{5,4},{6,5},{7,6},{8,11},{9,8},{10,9... | collective-permute-start | bytes 12296 | tf_op jit(solution)/shard_map/ppermute | solution.py:157

commit v6 on v5

--- a/solution.py
+++ b/solution.py
@@ -196,7 +196,8 @@
     state = to_columns(jnp.stack([adjoint_in * survive, mixing]).transpose(0, 2, 1, 3))
     right, column_mixing = state[0], state[1]
     ep = jnp.broadcast_to(emission_profile[:, None, None], (lev_dev, lev_groups, 1))
-    deferred = (courant.transpose(0, 2, 1, 3), survive.transpose(1, 0, 2), ep)
+    ep = ring_columns(ep, lev_index, lev_groups).reshape(levels)
+    deferred = (courant.transpose(0, 2, 1, 3), survive.transpose(1, 0, 2))
     grad_sum = jnp.sum(adjoint_in * emission_profile[None, :, None], axis=1)
 
     own_steps = lax.dynamic_slice_in_dim(substeps, lev_index * own, own)
@@ -224,7 +225,6 @@
             deferred, solved = lax.optimization_barrier((deferred, solved))
             flows = ring_columns(deferred[0], lev_index, lev_groups).reshape(2, levels * own, cell_count)
             column_survive = ring_columns(deferred[1], lev_index, lev_groups)
-            ep = ring_columns(deferred[2], lev_index, lev_groups).reshape(levels)
         else:
             solved, grad_step = column_solve(column_mixing, ep=ep, adjoint=adjoint, survive=column_survive)
             mine = lax.dynamic_slice_in_dim(grad_sum, lev_index * own, own)

time: 169 us -> 155 us (0.917)
  waiting for transfers between devices: 50.7 us -> 33 us
  starting transfers between devices: 64.9 us -> 69.9 us
    ppermute x9, waiting for transfers between devices: 23.7 us -> 7.34 us  [ring_columns(): piece = lax.ppermute(piece, 'lev', ring)]
    ppermute x9, starting transfers between devices: 9.31 us -> 15.1 us  [ring_columns(): piece = lax.ppermute(piece, 'lev', ring)]
    all_to_all x2, waiting for transfers between devices: 18.7 us -> 16.7 us  [to_columns(): lax.all_to_all(x, 'lev', split_axis=x.ndim - 2, concat_axis=x.ndim - 3, t...]
  transfers between devices with their start and end apart: 24 -> 24, of which waited for: 9 -> 7; matrix products, arithmetic and copies ran while one was open for 10% -> 13% of each run, Pallas kernels for 6% -> 6%
where the time goes in v6:
time: 155 us; the launch traced here: 154 us
  starting transfers between devices  69.9 us (45%)
  waiting for transfers between devices  33 us (21%)
  Pallas kernels  17.6 us (11%)
  local copies, waits for them, and re-layouts  17.4 us (11%)
  matrix products  8.16 us (5%)
  other arithmetic  6.97 us (4%)
    all_to_all x2, starting transfers between devices, local(): got = lax.all_to_all(sent, 'blk', split_axis=0, concat_axis=0, tiled=True)  22.6 us
    all_to_all x2, waiting for transfers between devices, to_columns(): lax.all_to_all(x, 'lev', split_axis=x.ndim - 2, concat_axis=x.ndim - 3, t...  16.7 us
    ppermute x9, starting transfers between devices, ring_columns(): piece = lax.ppermute(piece, 'lev', ring)  15.1 us
    ppermute x6, starting transfers between devices, ring_exchange(): piece = lax.ppermute(piece, 'lev', ring)  11.1 us
    pallas_call x2, Pallas kernels, advect(): pl.pallas_call(functools.partial(stencil_kernel, side_len), grid=(rows //...  9.91 us
    ppermute x6, waiting for transfers between devices, ring_exchange(): piece = lax.ppermute(piece, 'lev', ring)  7.86 us
    all_to_all x2, starting transfers between devices, local(): lax.all_to_all(cycle_out, 'lev', split_axis=0, concat_axis=1, tiled=True)  7.49 us
    all_to_all x2, starting transfers between devices, to_columns(): lax.all_to_all(x, 'lev', split_axis=x.ndim - 2, concat_axis=x.ndim - 3, t...  7.35 us
  transfers between devices with their start and end apart: 24, of which 7 were waited for; matrix products, arithmetic and copies ran while one was open for 13% of the time, Pallas kernels for 6%

profile of v6, /device:TPU:8, one launch (start us, length us, event | category | flops | bytes accessed | tf_op | source)
XLA Modules:
  0.0 154.3 jit_solution(9924658588814867457)
XLA Ops:
  0.7 1.6 %collective-permute-start = (f32[3,1,1]{0,2,1:T(1,128)}, f32[3,1,1]{0,2,1:T(1,128)S(1)}, u32[]{:S(2)}, u32[]{:S(2)}) collective-permute-start(f32[3,1,1]{0,2,1:T(1,128)} %bitcast.213), channel_id=1, source_target_pairs={{0,1},{1,2},{2,3},{3,0},{4,5},{5,6},{6,7},{7,4},{8,9},{9,10},{10,1... | collective-permute-start | bytes 44 | tf_op jit(solution)/shard_map/ppermute | solution.py:143
  2.2 2.7 %collective-permute-start.1 = (f32[3,1,1]{0,2,1:T(1,128)}, f32[3,1,1]{0,2,1:T(1,128)S(1)}, u32[]{:S(2)}, u32[]{:S(2)}) collective-permute-start(f32[3,1,1]{0,2,1:T(1,128)} %bitcast.214), channel_id=1, source_target_pairs={{0,2},{1,3},{2,0},{3,1},{4,6},{5,7},{6,4},{7,5},{8,10},{9,11},{10,... | collective-permute-start | bytes 44 | tf_op jit(solution)/shard_map/ppermute | solution.py:143
  5.0 1.4 collective-permute-start.2
  6.4 1.6 %multiply_reduce_fusion = (f32[64,1024]{1,0:T(8,128)S(1)}, f32[1,64,3,1024]{3,1,2,0:T(8,128)S(1)}, f32[3,64,1024]{2,1,0:T(8,128)S(1)}) fusion(f32[64,3,1024]{2,0,1:T(8,128)} %param.12, f32[3]{0:T(128)} %param.20, f32[64,3,1024]{2,0,1:T(8,128)} %param.15), kind=kLoop, calls=%fused_computation.21 | loop fusion | flops 720896 | bytes 3407884 | tf_op jit(solution)/shard_map/reduce_sum | solution.py:201
  8.1 2.4 %copy.180 = f32[2,3,64,1024]{3,0,1,2:T(2,128)} copy(f32[2,3,64,1024]{3,2,1,0:T(8,128)S(1)} %maximum_bitcast_fusion) | data formatting | bytes 3145728 | tf_op jit(solution)/shard_map/transpose | solution.py:196
  10.6 3.7 %all-to-all-start = ((f32[2,3,64,1024]{3,0,1,2:T(2,128)}), f32[2,3,64,1024]{3,0,1,2:T(2,128)S(1)}, u32[]{:S(2)}, u32[]{:S(2)}) async-start(f32[2,3,64,1024]{3,0,1,2:T(2,128)} %copy.180), calls=%async_computation | async-start | bytes 3145728 | tf_op jit(solution)/shard_map/all_to_all | solution.py:130
  14.5 0.7 broadcast_in_dim_tile.4.st_ref
  17.7 16.7 %all-to-all-done = f32[2,3,64,1024]{3,0,1,2:T(2,128)S(1)} async-done(((f32[2,3,64,1024]{3,0,1,2:T(2,128)}), f32[2,3,64,1024]{3,0,1,2:T(2,128)S(1)}, u32[]{:S(2)}, u32[]{:S(2)}) %all-to-all-start) | async-done | bytes 1572896 | tf_op jit(solution)/shard_map/all_to_all | solution.py:130
  34.9 1.3 fusion.62
  36.2 3.7 %shard_map.113 = f32[12,16,1024]{2,1,0:T(8,128)} custom-call(f32[12,16,1024]{2,1,0:T(8,128)} %bitcast.187, f32[12,16,1024]{2,1,0:T(8,128)} %bitcast.172), custom_call_target="tpu_custom_call" | custom-call | tf_op jit(solution)/shard_map/pallas_call | solution.py:62
  39.9 0.9 dynamic-slice_bitcast_fusion.10
  41.4 2.1 %collective-permute-start.7 = (f32[3,16,1024]{2,1,0:T(8,128)}, f32[3,16,1024]{2,1,0:T(8,128)}, u32[]{:S(2)}, u32[]{:S(2)}) collective-permute-start(f32[3,16,1024]{2,1,0:T(8,128)} %get-tuple-element.31), channel_id=1, source_target_pairs={{0,2},{1,3},{2,0},{3,1},{4,6},{5,7},{6,4},{7,5},{8,10},{9,11},{10,... | collective-permute-start | bytes 589832 | tf_op jit(solution)/shard_map/ppermute | solution.py:143
  44.1 1.2 convolution_multiply_fusion.1
  45.3 4.2 %all-to-all-start.1 = ((f32[12,16,128]{2,1,0:T(8,128)}), f32[12,16,128]{2,1,0:T(8,128)S(1)}, u32[]{:S(2)}, u32[]{:S(2)}) async-start(f32[12,16,128]{2,1,0:T(8,128)} %convolution_multiply_fusion.1), calls=%async_computation.1 | async-start | bytes 196608 | tf_op jit(solution)/shard_map/all_to_all | solution.py:234
  49.5 1.1 dynamic-slice_bitcast_fusion.3
  50.5 2.0 %collective-permute-start.3 = (f32[2,3,16,1024]{3,2,1,0:T(8,128)}, f32[2,3,16,1024]{3,2,1,0:T(8,128)S(1)}, u32[]{:S(2)}, u32[]{:S(2)}) collective-permute-start(f32[2,3,16,1024]{3,2,1,0:T(8,128)} %get-tuple-element.19), channel_id=1, source_target_pairs={{0,1},{1,2},{2,3},{3,0},{4,5},{5,6},{6,7},{7,4},{8,9},{9,10},{10,1... | collective-permute-start | bytes 1179656 | tf_op jit(solution)/shard_map/ppermute | solution.py:143
  52.6 2.7 %collective-permute-start.4 = (f32[2,3,16,1024]{3,2,1,0:T(8,128)}, f32[2,3,16,1024]{3,2,1,0:T(8,128)S(1)}, u32[]{:S(2)}, u32[]{:S(2)}) collective-permute-start(f32[2,3,16,1024]{3,2,1,0:T(8,128)} %get-tuple-element.18), channel_id=1, source_target_pairs={{0,2},{1,3},{2,0},{3,1},{4,6},{5,7},{6,4},{7,5},{8,10},{9,11},{10,... | collective-permute-start | bytes 1179656 | tf_op jit(solution)/shard_map/ppermute | solution.py:143
  56.3 0.9 copy.191
  57.2 12.3 %all-to-all-start.2 = ((f32[64,2,512]{2,1,0:T(2,128)}), f32[64,2,512]{2,1,0:T(2,128)}, u32[]{:S(2)}, u32[]{:S(2)}) async-start(f32[64,2,512]{2,1,0:T(2,128)} %copy.191), calls=%async_computation.2 | async-start | bytes 524288 | tf_op jit(solution)/shard_map/all_to_all | solution.py:243
  69.5 1.4 collective-permute-start.5
  70.9 1.2 pad_maximum_fusion.1
  72.7 1.1 broadcast_select_fusion
  73.8 7.3 %collective-permute-done.5 = f32[2,3,16,1024]{3,2,1,0:T(8,128)S(1)} collective-permute-done((f32[2,3,16,1024]{3,2,1,0:T(8,128)}, f32[2,3,16,1024]{3,2,1,0:T(8,128)S(1)}, u32[]{:S(2)}, u32[]{:S(2)}) %collective-permute-start.5) | collective-permute-done | bytes 393248 | tf_op jit(solution)/shard_map/ppermute | solution.py:143
  82.3 1.1 reshape.218
  84.0 0.7 copy.194
  84.8 3.6 %all-to-all-start.3 = ((f32[3,64,128]{2,0,1:T(4,128)}), f32[3,64,128]{2,0,1:T(4,128)S(1)}, u32[]{:S(2)}, u32[]{:S(2)}) async-start(f32[3,64,128]{2,0,1:T(4,128)} %copy.194), calls=%async_computation.3 | async-start | bytes 262144 | tf_op jit(solution)/shard_map/all_to_all | solution.py:130
  88.4 1.3 fusion.61
  89.7 4.9 %shard_map.114 = f32[192,1024]{1,0:T(8,128)} custom-call(s32[192,1]{1,0:T(8,128)} %broadcast_in_dim_tile.4.st_ref, f32[192,1024]{1,0:T(8,128)} %bitcast.174, f32[192,1024]{1,0:T(8,128)} %bitcast.177, f32[192,1024]{1,0:T(8,128)} %bitcast.175), custom_call_target="tpu_custom_call" | custom-call | tf_op jit(solution)/shard_map/pallas_call | solution.py:104
  94.6 2.5 %convolution_add_fusion.1 = f32[192,1024]{1,0:T(8,128)} fusion(f32[192,1024]{1,0:T(8,128)} %shard_map.114, f32[192,128]{1,0:T(8,128)S(1)} %bitcast.197, s32[128]{0:T(128)S(1)} %pad_add_fusion), kind=kOutput, calls=%fused_computation.11 | convolution fusion | flops 302317568 | bytes 1671680 | tf_op jit(solution)/shard_map/dot_general | solution.py:261
  97.2 3.9 %shard_map.115 = (f32[12,16,1024]{2,1,0:T(8,128)}, f32[16,1024]{1,0:T(8,128)}) custom-call(f32[12]{0:T(128)} %reshape.283.ep_ref, f32[12,16,1024]{2,1,0:T(8,128)} %bitcast.182, f32[12,16,1024]{2,1,0:T(8,128)} %bitcast.181, f32[12,16,1024]{2,1,0:T(8,128)} %bitcast.173), custom_call_target="tpu_custom_call" | custom-call | tf_op jit(solution)/shard_map/pallas_call | solution.py:71
  101.1 0.9 add_dynamic-update-slice_fusion
  102.4 2.1 %collective-permute-start.12 = (f32[64,256]{1,0:T(8,128)S(1)}, f32[64,256]{1,0:T(8,128)S(1)}, u32[]{:S(2)}, u32[]{:S(2)}) collective-permute-start(f32[64,256]{1,0:T(8,128)S(1)} %bitcast.206), channel_id=1, source_target_pairs={{0,1},{1,2},{2,3},{3,0},{4,5},{5,6},{6,7},{7,4},{8,9},{9,10},{10,1... | collective-permute-start | bytes 196616 | tf_op jit(solution)/shard_map/ppermute | solution.py:169
  104.5 2.7 %collective-permute-start.13 = (f32[64,256]{1,0:T(8,128)S(1)}, f32[64,256]{1,0:T(8,128)S(1)}, u32[]{:S(2)}, u32[]{:S(2)}) collective-permute-start(f32[64,256]{1,0:T(8,128)S(1)} %bitcast.207), channel_id=1, source_target_pairs={{0,2},{1,3},{2,0},{3,1},{4,6},{5,7},{6,4},{7,5},{8,10},{9,11},{10,... | collective-permute-start | bytes 196616 | tf_op jit(solution)/shard_map/ppermute | solution.py:169
  107.2 1.5 collective-permute-start.14
  108.6 1.2 convolution_multiply_fusion
  109.8 3.3 %all-to-all-start.4 = ((f32[12,16,128]{2,1,0:T(8,128)}), f32[12,16,128]{2,1,0:T(8,128)S(1)}, u32[]{:S(2)}, u32[]{:S(2)}) async-start(f32[12,16,128]{2,1,0:T(8,128)} %convolution_multiply_fusion), calls=%async_computation.4 | async-start | bytes 196608 | tf_op jit(solution)/shard_map/all_to_all | solution.py:234
  113.2 5.0 %shard_map.116 = f32[192,1024]{1,0:T(8,128)} custom-call(s32[192,1]{1,0:T(8,128)} %broadcast_in_dim_tile.4.st_ref, f32[192,1024]{1,0:T(8,128)} %bitcast.186, f32[192,1024]{1,0:T(8,128)} %bitcast.178, f32[192,1024]{1,0:T(8,128)} %bitcast.176), custom_call_target="tpu_custom_call" | custom-call | tf_op jit(solution)/shard_map/pallas_call | solution.py:104
  119.4 1.0 copy.206
  120.4 10.3 %all-to-all-start.5 = ((f32[64,2,640]{2,1,0:T(2,128)}), f32[64,2,640]{2,1,0:T(2,128)S(1)}, u32[]{:S(2)}, u32[]{:S(2)}) async-start(f32[64,2,640]{2,1,0:T(2,128)} %copy.206), calls=%async_computation.5 | async-start | bytes 655360 | tf_op jit(solution)/shard_map/all_to_all | solution.py:243
  130.8 1.6 %collective-permute-start.9 = (f32[3,16,1024]{2,1,0:T(8,128)S(1)}, f32[3,16,1024]{2,1,0:T(8,128)S(1)}, u32[]{:S(2)}, u32[]{:S(2)}) collective-permute-start(f32[3,16,1024]{2,1,0:T(8,128)S(1)} %get-tuple-element.29), channel_id=1, source_target_pairs={{0,1},{1,2},{2,3},{3,0},{4,5},{5,6},{6,7},{7,4},{8,9},{9,10},{10,1... | collective-permute-start | bytes 589832 | tf_op jit(solution)/shard_map/ppermute | solution.py:157
  132.4 2.7 %collective-permute-start.10 = (f32[3,16,1024]{2,1,0:T(8,128)S(1)}, f32[3,16,1024]{2,1,0:T(8,128)S(1)}, u32[]{:S(2)}, u32[]{:S(2)}) collective-permute-start(f32[3,16,1024]{2,1,0:T(8,128)S(1)} %get-tuple-element.28), channel_id=1, source_target_pairs={{0,2},{1,3},{2,0},{3,1},{4,6},{5,7},{6,4},{7,5},{8,10},{9,11},{10,... | collective-permute-start | bytes 589832 | tf_op jit(solution)/shard_map/ppermute | solution.py:157
  135.1 1.5 collective-permute-start.11
  136.5 2.5 %collective-permute-done.9 = f32[3,16,1024]{2,1,0:T(8,128)S(1)} collective-permute-done((f32[3,16,1024]{2,1,0:T(8,128)S(1)}, f32[3,16,1024]{2,1,0:T(8,128)S(1)}, u32[]{:S(2)}, u32[]{:S(2)}) %collective-permute-start.9) | collective-permute-done | bytes 196640 | tf_op jit(solution)/shard_map/ppermute | solution.py:157
  139.0 5.2 %collective-permute-done.10 = f32[3,16,1024]{2,1,0:T(8,128)S(1)} collective-permute-done((f32[3,16,1024]{2,1,0:T(8,128)S(1)}, f32[3,16,1024]{2,1,0:T(8,128)S(1)}, u32[]{:S(2)}, u32[]{:S(2)}) %collective-permute-start.10) | collective-permute-done | bytes 196640 | tf_op jit(solution)/shard_map/ppermute | solution.py:157
  145.7 1.4 collective-permute-start.15
  147.1 2.4 %collective-permute-start.16 = (f32[4,256]{1,0:T(4,128)S(1)}, f32[4,256]{1,0:T(4,128)S(1)}, u32[]{:S(2)}, u32[]{:S(2)}) collective-permute-start(f32[4,256]{1,0:T(4,128)S(1)} %get-tuple-element.40), channel_id=1, source_target_pairs={{0,2},{1,3},{2,0},{3,1},{4,6},{5,7},{6,4},{7,5},{8,10},{9,11},{10,... | collective-permute-start | bytes 12296 | tf_op jit(solution)/shard_map/ppermute | solution.py:157
  149.5 1.6 %collective-permute-start.17 = (f32[4,256]{1,0:T(4,128)S(1)}, f32[4,256]{1,0:T(4,128)S(1)}, u32[]{:S(2)}, u32[]{:S(2)}) collective-permute-start(f32[4,256]{1,0:T(4,128)S(1)} %get-tuple-element.39), channel_id=1, source_target_pairs={{0,3},{1,0},{2,1},{3,2},{4,7},{5,4},{6,5},{7,6},{8,11},{9,8},{10,9... | collective-permute-start | bytes 12296 | tf_op jit(solution)/shard_map/ppermute | solution.py:157
  151.5 1.4 fusion
  (121 shorter events, 12.5 us)
Async XLA Ops:
  0.6 15.7 %copy-start = (f32[64,128]{1,0:T(8,128)S(1)}, f32[64,128]{1,0:T(8,128)}, u32[]{:S(2)}) copy-start(f32[64,128]{1,0:T(8,128)} %param.17) | copy-start | bytes 98308
  0.6 7.4 %copy-start.6 = (f32[64,3,1024]{2,0,1:T(8,128)S(1)}, f32[64,3,1024]{2,0,1:T(8,128)}, u32[]{:S(2)}) copy-start(f32[64,3,1024]{2,0,1:T(8,128)} %param.14) | copy-start | bytes 2359300
  0.7 15.7 %collective-permute-start = (f32[3,1,1]{0,2,1:T(1,128)}, f32[3,1,1]{0,2,1:T(1,128)S(1)}, u32[]{:S(2)}, u32[]{:S(2)}) collective-permute-start(f32[3,1,1]{0,2,1:T(1,128)} %bitcast.213), channel_id=1, source_target_pairs={{0,1},{1,2},{2,3},{3,0},{4,5},{5,6},{6,7},{7,4},{8,9},{9,10},{10,1... | collective-permute-start | bytes 44 | tf_op jit(solution)/shard_map/ppermute | solution.py:143
  2.2 14.2 %collective-permute-start.1 = (f32[3,1,1]{0,2,1:T(1,128)}, f32[3,1,1]{0,2,1:T(1,128)S(1)}, u32[]{:S(2)}, u32[]{:S(2)}) collective-permute-start(f32[3,1,1]{0,2,1:T(1,128)} %bitcast.214), channel_id=1, source_target_pairs={{0,2},{1,3},{2,0},{3,1},{4,6},{5,7},{6,4},{7,5},{8,10},{9,11},{10,... | collective-permute-start | bytes 44 | tf_op jit(solution)/shard_map/ppermute | solution.py:143
  5.0 11.4 %collective-permute-start.2 = (f32[3,1,1]{0,2,1:T(1,128)}, f32[3,1,1]{0,2,1:T(1,128)S(1)}, u32[]{:S(2)}, u32[]{:S(2)}) collective-permute-start(f32[3,1,1]{0,2,1:T(1,128)} %bitcast.215), channel_id=1, source_target_pairs={{0,3},{1,0},{2,1},{3,2},{4,7},{5,4},{6,5},{7,6},{8,11},{9,8},{10,9... | collective-permute-start | bytes 44 | tf_op jit(solution)/shard_map/ppermute | solution.py:143
  10.5 3.9 %copy-start.8 = (s32[64]{0:T(128)S(1)}, s32[64]{0:T(128)}, u32[]{:S(2)}) copy-start(s32[64]{0:T(128)} %param.16) | copy-start | bytes 772
  10.5 4.7 %copy-start.9 = (s32[64,1]{0,1:T(1,128)S(1)}, s32[64,1]{0,1:T(1,128)}, u32[]{:S(2)}) copy-start(s32[64,1]{0,1:T(1,128)} %param.18) | copy-start | bytes 772
  10.5 4.9 %copy-start.10 = (s32[64]{0:T(128)S(1)}, s32[64]{0:T(128)}, u32[]{:S(2)}) copy-start(s32[64]{0:T(128)} %param.21) | copy-start | bytes 772
  10.5 5.2 %copy-start.11 = (s32[64]{0:T(128)S(1)}, s32[64]{0:T(128)}, u32[]{:S(2)}) copy-start(s32[64]{0:T(128)} %param.19) | copy-start | bytes 772
  10.5 5.9 %copy-start.7 = (f32[3]{0:T(128)S(1)}, f32[3]{0:T(128)}, u32[]{:S(2)}) copy-start(f32[3]{0:T(128)} %param.20) | copy-start | bytes 40
  10.6 23.8 %all-to-all-start = ((f32[2,3,64,1024]{3,0,1,2:T(2,128)}), f32[2,3,64,1024]{3,0,1,2:T(2,128)S(1)}, u32[]{:S(2)}, u32[]{:S(2)}) async-start(f32[2,3,64,1024]{3,0,1,2:T(2,128)} %copy.180), calls=%async_computation | async-start | bytes 3145728 | tf_op jit(solution)/shard_map/all_to_all | solution.py:130
  39.9 4.2 %copy-start.1 = (f32[12,16,1024]{2,1,0:T(8,128)S(1)}, f32[12,16,1024]{2,1,0:T(8,128)}, u32[]{:S(2)}) copy-start(f32[12,16,1024]{2,1,0:T(8,128)} %shard_map.113) | copy-start | bytes 2359300
  39.9 9.6 %copy-start.4 = (f32[2,64,3,1024]{3,1,2,0:T(8,128)S(1)}, f32[2,64,3,1024]{3,1,2,0:T(8,128)}, u32[]{:S(2)}) copy-start(f32[2,64,3,1024]{3,1,2,0:T(8,128)} %param.13) | copy-start | bytes 4718596
  40.8 28.6 %collective-permute-start.6 = (f32[3,16,1024]{2,1,0:T(8,128)}, f32[3,16,1024]{2,1,0:T(8,128)}, u32[]{:S(2)}, u32[]{:S(2)}) collective-permute-start(f32[3,16,1024]{2,1,0:T(8,128)} %get-tuple-element.32), channel_id=1, source_target_pairs={{0,1},{1,2},{2,3},{3,0},{4,5},{5,6},{6,7},{7,4},{8,9},{9,10},{10,1... | collective-permute-start | bytes 589832 | tf_op jit(solution)/shard_map/ppermute | solution.py:143
  41.4 29.5 %collective-permute-start.7 = (f32[3,16,1024]{2,1,0:T(8,128)}, f32[3,16,1024]{2,1,0:T(8,128)}, u32[]{:S(2)}, u32[]{:S(2)}) collective-permute-start(f32[3,16,1024]{2,1,0:T(8,128)} %get-tuple-element.31), channel_id=1, source_target_pairs={{0,2},{1,3},{2,0},{3,1},{4,6},{5,7},{6,4},{7,5},{8,10},{9,11},{10,... | collective-permute-start | bytes 589832 | tf_op jit(solution)/shard_map/ppermute | solution.py:143
  43.5 27.5 %collective-permute-start.8 = (f32[3,16,1024]{2,1,0:T(8,128)}, f32[3,16,1024]{2,1,0:T(8,128)}, u32[]{:S(2)}, u32[]{:S(2)}) collective-permute-start(f32[3,16,1024]{2,1,0:T(8,128)} %get-tuple-element.33), channel_id=1, source_target_pairs={{0,3},{1,0},{2,1},{3,2},{4,7},{5,4},{6,5},{7,6},{8,11},{9,8},{10,9... | collective-permute-start | bytes 589832 | tf_op jit(solution)/shard_map/ppermute | solution.py:143
  45.3 10.5 %all-to-all-start.1 = ((f32[12,16,128]{2,1,0:T(8,128)}), f32[12,16,128]{2,1,0:T(8,128)S(1)}, u32[]{:S(2)}, u32[]{:S(2)}) async-start(f32[12,16,128]{2,1,0:T(8,128)} %convolution_multiply_fusion.1), calls=%async_computation.1 | async-start | bytes 196608 | tf_op jit(solution)/shard_map/all_to_all | solution.py:234
  50.5 20.4 %copy-start.5 = (f32[1,3,16,1024]{3,2,1,0:T(8,128)S(1)}, f32[1,3,16,1024]{3,2,1,0:T(8,128)}, u32[]{:S(2)}) copy-start(f32[1,3,16,1024]{3,2,1,0:T(8,128)} %get-tuple-element.30) | copy-start | bytes 589828
  50.5 23.2 %collective-permute-start.3 = (f32[2,3,16,1024]{3,2,1,0:T(8,128)}, f32[2,3,16,1024]{3,2,1,0:T(8,128)S(1)}, u32[]{:S(2)}, u32[]{:S(2)}) collective-permute-start(f32[2,3,16,1024]{3,2,1,0:T(8,128)} %get-tuple-element.19), channel_id=1, source_target_pairs={{0,1},{1,2},{2,3},{3,0},{4,5},{5,6},{6,7},{7,4},{8,9},{9,10},{10,1... | collective-permute-start | bytes 1179656 | tf_op jit(solution)/shard_map/ppermute | solution.py:143
  52.6 21.2 %collective-permute-start.4 = (f32[2,3,16,1024]{3,2,1,0:T(8,128)}, f32[2,3,16,1024]{3,2,1,0:T(8,128)S(1)}, u32[]{:S(2)}, u32[]{:S(2)}) collective-permute-start(f32[2,3,16,1024]{3,2,1,0:T(8,128)} %get-tuple-element.18), channel_id=1, source_target_pairs={{0,2},{1,3},{2,0},{3,1},{4,6},{5,7},{6,4},{7,5},{8,10},{9,11},{10,... | collective-permute-start | bytes 1179656 | tf_op jit(solution)/shard_map/ppermute | solution.py:143
  57.2 25.1 %all-to-all-start.2 = ((f32[64,2,512]{2,1,0:T(2,128)}), f32[64,2,512]{2,1,0:T(2,128)}, u32[]{:S(2)}, u32[]{:S(2)}) async-start(f32[64,2,512]{2,1,0:T(2,128)} %copy.191), calls=%async_computation.2 | async-start | bytes 524288 | tf_op jit(solution)/shard_map/all_to_all | solution.py:243
  69.5 11.6 %collective-permute-start.5 = (f32[2,3,16,1024]{3,2,1,0:T(8,128)}, f32[2,3,16,1024]{3,2,1,0:T(8,128)S(1)}, u32[]{:S(2)}, u32[]{:S(2)}) collective-permute-start(f32[2,3,16,1024]{3,2,1,0:T(8,128)} %get-tuple-element.20), channel_id=1, source_target_pairs={{0,3},{1,0},{2,1},{3,2},{4,7},{5,4},{6,5},{7,6},{8,11},{9,8},{10,9... | collective-permute-start | bytes 1179656 | tf_op jit(solution)/shard_map/ppermute | solution.py:143
  84.8 9.8 %all-to-all-start.3 = ((f32[3,64,128]{2,0,1:T(4,128)}), f32[3,64,128]{2,0,1:T(4,128)S(1)}, u32[]{:S(2)}, u32[]{:S(2)}) async-start(f32[3,64,128]{2,0,1:T(4,128)} %copy.194), calls=%async_computation.3 | async-start | bytes 262144 | tf_op jit(solution)/shard_map/all_to_all | solution.py:130
  101.1 7.6 %copy-start.3 = (f32[12,16,1024]{2,1,0:T(8,128)S(1)}, f32[12,16,1024]{2,1,0:T(8,128)}, u32[]{:S(2)}) copy-start(f32[12,16,1024]{2,1,0:T(8,128)} %get-tuple-element.11) | copy-start | bytes 2359300
  102.4 15.7 %collective-permute-start.12 = (f32[64,256]{1,0:T(8,128)S(1)}, f32[64,256]{1,0:T(8,128)S(1)}, u32[]{:S(2)}, u32[]{:S(2)}) collective-permute-start(f32[64,256]{1,0:T(8,128)S(1)} %bitcast.206), channel_id=1, source_target_pairs={{0,1},{1,2},{2,3},{3,0},{4,5},{5,6},{6,7},{7,4},{8,9},{9,10},{10,1... | collective-permute-start | bytes 196616 | tf_op jit(solution)/shard_map/ppermute | solution.py:169
  104.5 13.6 %collective-permute-start.13 = (f32[64,256]{1,0:T(8,128)S(1)}, f32[64,256]{1,0:T(8,128)S(1)}, u32[]{:S(2)}, u32[]{:S(2)}) collective-permute-start(f32[64,256]{1,0:T(8,128)S(1)} %bitcast.207), channel_id=1, source_target_pairs={{0,2},{1,3},{2,0},{3,1},{4,6},{5,7},{6,4},{7,5},{8,10},{9,11},{10,... | collective-permute-start | bytes 196616 | tf_op jit(solution)/shard_map/ppermute | solution.py:169
  107.2 10.9 %collective-permute-start.14 = (f32[64,256]{1,0:T(8,128)S(1)}, f32[64,256]{1,0:T(8,128)S(1)}, u32[]{:S(2)}, u32[]{:S(2)}) collective-permute-start(f32[64,256]{1,0:T(8,128)S(1)} %bitcast.208), channel_id=1, source_target_pairs={{0,3},{1,0},{2,1},{3,2},{4,7},{5,4},{6,5},{7,6},{8,11},{9,8},{10,9... | collective-permute-start | bytes 196616 | tf_op jit(solution)/shard_map/ppermute | solution.py:169
  109.8 9.1 %all-to-all-start.4 = ((f32[12,16,128]{2,1,0:T(8,128)}), f32[12,16,128]{2,1,0:T(8,128)S(1)}, u32[]{:S(2)}, u32[]{:S(2)}) async-start(f32[12,16,128]{2,1,0:T(8,128)} %convolution_multiply_fusion), calls=%async_computation.4 | async-start | bytes 196608 | tf_op jit(solution)/shard_map/all_to_all | solution.py:234
  118.4 12.3 %copy-start.2 = (f32[192,1024]{1,0:T(8,128)S(1)}, f32[192,1024]{1,0:T(8,128)}, u32[]{:S(2)}) copy-start(f32[192,1024]{1,0:T(8,128)} %shard_map.116) | copy-start | bytes 2359300
  120.4 24.8 %all-to-all-start.5 = ((f32[64,2,640]{2,1,0:T(2,128)}), f32[64,2,640]{2,1,0:T(2,128)S(1)}, u32[]{:S(2)}, u32[]{:S(2)}) async-start(f32[64,2,640]{2,1,0:T(2,128)} %copy.206), calls=%async_computation.5 | async-start | bytes 655360 | tf_op jit(solution)/shard_map/all_to_all | solution.py:243
  130.8 8.2 %collective-permute-start.9 = (f32[3,16,1024]{2,1,0:T(8,128)S(1)}, f32[3,16,1024]{2,1,0:T(8,128)S(1)}, u32[]{:S(2)}, u32[]{:S(2)}) collective-permute-start(f32[3,16,1024]{2,1,0:T(8,128)S(1)} %get-tuple-element.29), channel_id=1, source_target_pairs={{0,1},{1,2},{2,3},{3,0},{4,5},{5,6},{6,7},{7,4},{8,9},{9,10},{10,1... | collective-permute-start | bytes 589832 | tf_op jit(solution)/shard_map/ppermute | solution.py:157
  132.4 11.8 %collective-permute-start.10 = (f32[3,16,1024]{2,1,0:T(8,128)S(1)}, f32[3,16,1024]{2,1,0:T(8,128)S(1)}, u32[]{:S(2)}, u32[]{:S(2)}) collective-permute-start(f32[3,16,1024]{2,1,0:T(8,128)S(1)} %get-tuple-element.28), channel_id=1, source_target_pairs={{0,2},{1,3},{2,0},{3,1},{4,6},{5,7},{6,4},{7,5},{8,10},{9,11},{10,... | collective-permute-start | bytes 589832 | tf_op jit(solution)/shard_map/ppermute | solution.py:157
  135.1 9.1 %collective-permute-start.11 = (f32[3,16,1024]{2,1,0:T(8,128)S(1)}, f32[3,16,1024]{2,1,0:T(8,128)S(1)}, u32[]{:S(2)}, u32[]{:S(2)}) collective-permute-start(f32[3,16,1024]{2,1,0:T(8,128)S(1)} %get-tuple-element.27), channel_id=1, source_target_pairs={{0,3},{1,0},{2,1},{3,2},{4,7},{5,4},{6,5},{7,6},{8,11},{9,8},{10,9... | collective-permute-start | bytes 589832 | tf_op jit(solution)/shard_map/ppermute | solution.py:157
  145.7 7.2 %collective-permute-start.15 = (f32[4,256]{1,0:T(4,128)S(1)}, f32[4,256]{1,0:T(4,128)S(1)}, u32[]{:S(2)}, u32[]{:S(2)}) collective-permute-start(f32[4,256]{1,0:T(4,128)S(1)} %get-tuple-element.41), channel_id=1, source_target_pairs={{0,1},{1,2},{2,3},{3,0},{4,5},{5,6},{6,7},{7,4},{8,9},{9,10},{10,1... | collective-permute-start | bytes 12296 | tf_op jit(solution)/shard_map/ppermute | solution.py:157
  147.1 5.8 %collective-permute-start.16 = (f32[4,256]{1,0:T(4,128)S(1)}, f32[4,256]{1,0:T(4,128)S(1)}, u32[]{:S(2)}, u32[]{:S(2)}) collective-permute-start(f32[4,256]{1,0:T(4,128)S(1)} %get-tuple-element.40), channel_id=1, source_target_pairs={{0,2},{1,3},{2,0},{3,1},{4,6},{5,7},{6,4},{7,5},{8,10},{9,11},{10,... | collective-permute-start | bytes 12296 | tf_op jit(solution)/shard_map/ppermute | solution.py:157
  149.5 3.6 %collective-permute-start.17 = (f32[4,256]{1,0:T(4,128)S(1)}, f32[4,256]{1,0:T(4,128)S(1)}, u32[]{:S(2)}, u32[]{:S(2)}) collective-permute-start(f32[4,256]{1,0:T(4,128)S(1)} %get-tuple-element.39), channel_id=1, source_target_pairs={{0,3},{1,0},{2,1},{3,2},{4,7},{5,4},{6,5},{7,6},{8,11},{9,8},{10,9... | collective-permute-start | bytes 12296 | tf_op jit(solution)/shard_map/ppermute | solution.py:157

commit v7 on v6

--- a/solution.py
+++ b/solution.py
@@ -222,9 +222,8 @@
     for step_index in range(STEPS):
         if step_index == 0:
             solved = column_solve(column_mixing, right=right)
-            deferred, solved = lax.optimization_barrier((deferred, solved))
-            flows = ring_columns(deferred[0], lev_index, lev_groups).reshape(2, levels * own, cell_count)
-            column_survive = ring_columns(deferred[1], lev_index, lev_groups)
+            flows, solved = lax.optimization_barrier((deferred[0], solved))
+            flows = ring_columns(flows, lev_index, lev_groups).reshape(2, levels * own, cell_count)
         else:
             solved, grad_step = column_solve(column_mixing, ep=ep, adjoint=adjoint, survive=column_survive)
             mine = lax.dynamic_slice_in_dim(grad_sum, lev_index * own, own)
@@ -232,6 +231,9 @@
         flat = solved.reshape(levels * own, cell_count)
         cycle_out = jnp.dot(flat, pick, precision=HI).reshape(levels, own, cycle_len) * own_weight[None]
         by_level = lax.all_to_all(cycle_out, "lev", split_axis=0, concat_axis=1, tiled=True)
+        if step_index == 0:
+            column_survive, by_level = lax.optimization_barrier((deferred[1], by_level))
+            column_survive = ring_columns(column_survive, lev_index, lev_groups)
         sent = jnp.einsum("sb,lbk->slk", face_pack, by_level, precision=HI)
         sent = sent.reshape(peer_count, cap, face_width)
         if step_index == 0:
@@ -261,16 +263,21 @@
             added = jnp.dot(arrivals, pick.T, precision=HI)
             adjoint = (advected + added).reshape(levels, own, cell_count)
 
-    by_dest = advected.reshape(lev_groups, lev_dev, own, cell_count)
+    tile_parts = jnp.dot(tile_take, tile_got, precision=HI)
+    tile_rows = group_size // lev_groups
+    by_dest = jnp.concatenate(
+        [
+            advected.reshape(lev_groups, lev_dev * own, cell_count),
+            tile_parts.reshape(lev_groups, 1, cell_count),
+        ],
+        axis=1,
+    )
     by_src = ring_exchange(by_dest, lev_index, lev_groups)
-    advected = by_src.transpose(1, 0, 2, 3).reshape(lev_dev, blocks, cell_count)
+    advected = by_src[:, : lev_dev * own].reshape(lev_groups, lev_dev, own, cell_count)
+    advected = advected.transpose(1, 0, 2, 3).reshape(lev_dev, blocks, cell_count)
     added = jnp.dot(arrivals.reshape(lev_dev * blocks, cycle_len), pick.T, precision=HI)
     adjoint_out = (advected + added.reshape(lev_dev, blocks, cell_count)).transpose(1, 0, 2)
-
-    tile_parts = jnp.dot(tile_take, tile_got, precision=HI)
-    tile_rows = group_size // lev_groups
-    tile_parts = tile_parts.reshape(lev_groups, tile_rows, cell_count // lev_groups)
-    tile_grad = ring_exchange(tile_parts, lev_index, lev_groups)
+    tile_grad = by_src[:, lev_dev * own].reshape(lev_groups, tile_rows, cell_count // lev_groups)
     tile_grad = tile_grad.transpose(1, 0, 2).reshape(tile_rows, cell_count)
     return (adjoint_out, tile_grad)
 

time: 155 us -> 167 us (1.077)
  waiting for transfers between devices: 33 us -> 55.2 us
  starting transfers between devices: 69.9 us -> 58.2 us
  local copies, waits for them, and re-layouts: 17.4 us -> 15.6 us
    ppermute x6 -> x3, starting transfers between devices: 11.1 us -> 2.71 us  [ring_exchange(): piece = lax.ppermute(piece, 'lev', ring)]
    all_to_all x2, waiting for transfers between devices: 0.01 us -> 7.87 us  [local(): got = lax.all_to_all(sent, 'blk', split_axis=0, concat_axis=0, tiled=True)]
    ppermute x9, waiting for transfers between devices: 7.34 us -> 12.6 us  [ring_columns(): piece = lax.ppermute(piece, 'lev', ring)]
    all_to_all x2, waiting for transfers between devices: 1.02 us -> 5.7 us  [local(): lax.all_to_all(cycle_out, 'lev', split_axis=0, concat_axis=1, tiled=True)]
    ppermute x6 -> x3, waiting for transfers between devices: 7.86 us -> 12 us  [ring_exchange(): piece = lax.ppermute(piece, 'lev', ring)]
    ppermute x9, starting transfers between devices: 15.1 us -> 12.1 us  [ring_columns(): piece = lax.ppermute(piece, 'lev', ring)]
    all_to_all x2, starting transfers between devices: 22.6 us -> 24.4 us  [local(): got = lax.all_to_all(sent, 'blk', split_axis=0, concat_axis=0, tiled=True)]
  transfers between devices with their start and end apart: 24 -> 21, of which waited for: 7 -> 10; matrix products, arithmetic and copies ran while one was open for 13% -> 10% of each run, Pallas kernels for 6% -> 6%
where the time goes in v7:
time: 167 us; the launch traced here: 165 us
  starting transfers between devices  58.2 us (35%)
  waiting for transfers between devices  55.2 us (33%)
  Pallas kernels  17.7 us (11%)
  local copies, waits for them, and re-layouts  15.6 us (9%)
  matrix products  9.37 us (6%)
  other arithmetic  7.7 us (5%)
    all_to_all x2, starting transfers between devices, local(): got = lax.all_to_all(sent, 'blk', split_axis=0, concat_axis=0, tiled=True)  24.4 us
    all_to_all x2, waiting for transfers between devices, to_columns(): lax.all_to_all(x, 'lev', split_axis=x.ndim - 2, concat_axis=x.ndim - 3, t...  16.6 us
    ppermute x9, waiting for transfers between devices, ring_columns(): piece = lax.ppermute(piece, 'lev', ring)  12.6 us
    ppermute x9, starting transfers between devices, ring_columns(): piece = lax.ppermute(piece, 'lev', ring)  12.1 us
    ppermute x3, waiting for transfers between devices, ring_exchange(): piece = lax.ppermute(piece, 'lev', ring)  12 us
    pallas_call x2, Pallas kernels, advect(): pl.pallas_call(functools.partial(stencil_kernel, side_len), grid=(rows //...  9.88 us
    all_to_all x2, waiting for transfers between devices, local(): got = lax.all_to_all(sent, 'blk', split_axis=0, concat_axis=0, tiled=True)  7.87 us
    all_to_all x2, starting transfers between devices, to_columns(): lax.all_to_all(x, 'lev', split_axis=x.ndim - 2, concat_axis=x.ndim - 3, t...  7.09 us
  transfers between devices with their start and end apart: 21, of which 10 were waited for; matrix products, arithmetic and copies ran while one was open for 10% of the time, Pallas kernels for 6%

profile of v7, /device:TPU:8, one launch (start us, length us, event | category | flops | bytes accessed | tf_op | source)
XLA Modules:
  0.0 165.1 jit_solution(15247682024561887924)
XLA Ops:
  0.7 2.8 %collective-permute-start.2 = (f32[3,1,1]{0,2,1:T(1,128)}, f32[3,1,1]{0,2,1:T(1,128)S(1)}, u32[]{:S(2)}, u32[]{:S(2)}) collective-permute-start(f32[3,1,1]{0,2,1:T(1,128)} %bitcast.206), channel_id=1, source_target_pairs={{0,3},{1,0},{2,1},{3,2},{4,7},{5,4},{6,5},{7,6},{8,11},{9,8},{10,9... | collective-permute-start | bytes 44 | tf_op jit(solution)/shard_map/ppermute | solution.py:143
  3.5 0.8 collective-permute-start.1
  4.3 0.9 collective-permute-start
  5.2 1.7 %multiply_reduce_fusion = (f32[64,1024]{1,0:T(8,128)S(1)}, f32[1,64,3,1024]{3,1,2,0:T(8,128)S(1)}, f32[3,64,1024]{2,1,0:T(8,128)S(1)}) fusion(f32[64,3,1024]{2,0,1:T(8,128)} %param.10, f32[3]{0:T(128)} %param.18, f32[64,3,1024]{2,0,1:T(8,128)} %param.13), kind=kLoop, calls=%fused_computation.28 | loop fusion | flops 720896 | bytes 3407884 | tf_op jit(solution)/shard_map/reduce_sum | solution.py:201
  7.0 2.4 %copy.176 = f32[2,3,64,1024]{3,0,1,2:T(2,128)} copy(f32[2,3,64,1024]{3,2,1,0:T(8,128)S(1)} %maximum_bitcast_fusion) | data formatting | bytes 3145728 | tf_op jit(solution)/shard_map/transpose | solution.py:196
  9.4 3.8 %all-to-all-start = ((f32[2,3,64,1024]{3,0,1,2:T(2,128)}), f32[2,3,64,1024]{3,0,1,2:T(2,128)S(1)}, u32[]{:S(2)}, u32[]{:S(2)}) async-start(f32[2,3,64,1024]{3,0,1,2:T(2,128)} %copy.176), calls=%async_computation | async-start | bytes 3145728 | tf_op jit(solution)/shard_map/all_to_all | solution.py:130
  13.3 0.7 broadcast_in_dim_tile.4.st_ref
  16.6 16.6 %all-to-all-done = f32[2,3,64,1024]{3,0,1,2:T(2,128)S(1)} async-done(((f32[2,3,64,1024]{3,0,1,2:T(2,128)}), f32[2,3,64,1024]{3,0,1,2:T(2,128)S(1)}, u32[]{:S(2)}, u32[]{:S(2)}) %all-to-all-start) | async-done | bytes 1572896 | tf_op jit(solution)/shard_map/all_to_all | solution.py:130
  33.7 1.3 fusion.64
  35.1 3.9 %shard_map.113 = f32[12,16,1024]{2,1,0:T(8,128)} custom-call(f32[12,16,1024]{2,1,0:T(8,128)} %bitcast.181, f32[12,16,1024]{2,1,0:T(8,128)} %bitcast.166), custom_call_target="tpu_custom_call" | custom-call | tf_op jit(solution)/shard_map/pallas_call | solution.py:62
  38.9 2.3 %convolution_multiply_fusion.1 = f32[12,16,128]{2,1,0:T(8,128)} fusion(f32[12,16,1024]{2,1,0:T(8,128)} %shard_map.113, s32[128]{0:T(128)S(1)} %pad_add_fusion, f32[16,128]{1,0:T(8,128)S(1)} %constant_dynamic-slice_fusion.4), kind=kOutput, calls=%fused_computation.18 | convolution fusion | flops 302145536 | bytes 893440 | tf_op jit(solution)/shard_map/dot_general | solution.py:232
  41.3 3.3 %all-to-all-start.1 = ((f32[12,16,128]{2,1,0:T(8,128)}), f32[12,16,128]{2,1,0:T(8,128)S(1)}, u32[]{:S(2)}, u32[]{:S(2)}) async-start(f32[12,16,128]{2,1,0:T(8,128)} %convolution_multiply_fusion.1), calls=%async_computation.1 | async-start | bytes 196608 | tf_op jit(solution)/shard_map/all_to_all | solution.py:233
  44.6 1.1 dynamic-slice_bitcast_fusion.3
  45.7 3.2 %collective-permute-start.5 = (f32[2,3,16,1024]{3,2,1,0:T(8,128)}, f32[2,3,16,1024]{3,2,1,0:T(8,128)}, u32[]{:S(2)}, u32[]{:S(2)}) collective-permute-start(f32[2,3,16,1024]{3,2,1,0:T(8,128)} %get-tuple-element.21), channel_id=1, source_target_pairs={{0,3},{1,0},{2,1},{3,2},{4,7},{5,4},{6,5},{7,6},{8,11},{9,8},{10,9... | collective-permute-start | bytes 1179656 | tf_op jit(solution)/shard_map/ppermute | solution.py:143
  48.9 0.9 collective-permute-start.4
  50.4 1.8 %collective-permute-start.8 = (f32[3,16,1024]{2,1,0:T(8,128)S(1)}, f32[3,16,1024]{2,1,0:T(8,128)S(1)}, u32[]{:S(2)}, u32[]{:S(2)}) collective-permute-start(f32[3,16,1024]{2,1,0:T(8,128)S(1)} %get-tuple-element.34), channel_id=1, source_target_pairs={{0,3},{1,0},{2,1},{3,2},{4,7},{5,4},{6,5},{7,6},{8,11},{9,8},{10,9... | collective-permute-start | bytes 589832 | tf_op jit(solution)/shard_map/ppermute | solution.py:143
  52.2 1.5 collective-permute-start.7
  54.7 0.8 pad_maximum_fusion.4
  55.5 12.3 %all-to-all-start.2 = ((f32[64,2,512]{2,1,0:T(2,128)}), f32[64,2,512]{2,1,0:T(2,128)}, u32[]{:S(2)}, u32[]{:S(2)}) async-start(f32[64,2,512]{2,1,0:T(2,128)} %pad_maximum_fusion.4), calls=%async_computation.2 | async-start | bytes 524288 | tf_op jit(solution)/shard_map/all_to_all | solution.py:245
  67.8 4.7 %collective-permute-done.8 = f32[3,16,1024]{2,1,0:T(8,128)S(1)} collective-permute-done((f32[3,16,1024]{2,1,0:T(8,128)S(1)}, f32[3,16,1024]{2,1,0:T(8,128)S(1)}, u32[]{:S(2)}, u32[]{:S(2)}) %collective-permute-start.8) | collective-permute-done | bytes 196640 | tf_op jit(solution)/shard_map/ppermute | solution.py:143
  73.2 1.1 bitcast_select_fusion.s_ref
  74.3 7.9 %collective-permute-done.3 = f32[2,3,16,1024]{3,2,1,0:T(8,128)S(1)} collective-permute-done((f32[2,3,16,1024]{3,2,1,0:T(8,128)}, f32[2,3,16,1024]{3,2,1,0:T(8,128)S(1)}, u32[]{:S(2)}, u32[]{:S(2)}) %collective-permute-start.3) | collective-permute-done | bytes 393248 | tf_op jit(solution)/shard_map/ppermute | solution.py:143
  82.1 1.2 pad_maximum_fusion
  83.4 0.6 gather_fusion.1
  84.4 1.1 reshape.207
  86.2 0.7 copy.188
  86.9 3.3 %all-to-all-start.3 = ((f32[3,64,128]{2,0,1:T(4,128)}), f32[3,64,128]{2,0,1:T(4,128)S(1)}, u32[]{:S(2)}, u32[]{:S(2)}) async-start(f32[3,64,128]{2,0,1:T(4,128)} %copy.188), calls=%async_computation.3 | async-start | bytes 262144 | tf_op jit(solution)/shard_map/all_to_all | solution.py:130
  90.2 1.2 fusion.63
  91.4 4.9 %shard_map.114 = f32[192,1024]{1,0:T(8,128)} custom-call(s32[192,1]{1,0:T(8,128)} %broadcast_in_dim_tile.4.st_ref, f32[192,1024]{1,0:T(8,128)} %bitcast.168, f32[192,1024]{1,0:T(8,128)} %bitcast.171, f32[192,1024]{1,0:T(8,128)} %bitcast.169), custom_call_target="tpu_custom_call" | custom-call | tf_op jit(solution)/shard_map/pallas_call | solution.py:104
  96.4 2.5 %convolution_add_fusion.1 = f32[192,1024]{1,0:T(8,128)} fusion(f32[192,1024]{1,0:T(8,128)} %shard_map.114, f32[192,128]{1,0:T(8,128)S(1)} %bitcast.189, s32[128]{0:T(128)S(1)} %pad_add_fusion), kind=kOutput, calls=%fused_computation.14 | convolution fusion | flops 302317568 | bytes 1671680 | tf_op jit(solution)/shard_map/dot_general | solution.py:263
  98.9 4.0 %shard_map.115 = (f32[12,16,1024]{2,1,0:T(8,128)}, f32[16,1024]{1,0:T(8,128)}) custom-call(f32[12]{0:T(128)} %broadcast_select_fusion.1.ep_ref, f32[12,16,1024]{2,1,0:T(8,128)} %bitcast.175, f32[12,16,1024]{2,1,0:T(8,128)} %bitcast_select_fusion.s_ref, f32[12,16,1024]{2,1,0:T(8,128)} %bitcast.167), custom_call_target="tpu_custom_call" | custom-call | tf_op jit(solution)/shard_map/pallas_call | solution.py:71
  102.9 0.9 add_dynamic-update-slice_fusion
  104.2 3.3 %collective-permute-start.11 = (f32[64,256]{1,0:T(8,128)S(1)}, f32[64,256]{1,0:T(8,128)S(1)}, u32[]{:S(2)}, u32[]{:S(2)}) collective-permute-start(f32[64,256]{1,0:T(8,128)S(1)} %bitcast.201), channel_id=1, source_target_pairs={{0,3},{1,0},{2,1},{3,2},{4,7},{5,4},{6,5},{7,6},{8,11},{9,8},{10,9... | collective-permute-start | bytes 196616 | tf_op jit(solution)/shard_map/ppermute | solution.py:169
  107.5 0.8 collective-permute-start.10
  108.3 0.9 collective-permute-start.9
  109.2 1.2 convolution_multiply_fusion
  110.4 3.6 %all-to-all-start.4 = ((f32[12,16,128]{2,1,0:T(8,128)}), f32[12,16,128]{2,1,0:T(8,128)S(1)}, u32[]{:S(2)}, u32[]{:S(2)}) async-start(f32[12,16,128]{2,1,0:T(8,128)} %convolution_multiply_fusion), calls=%async_computation.4 | async-start | bytes 196608 | tf_op jit(solution)/shard_map/all_to_all | solution.py:233
  114.8 5.1 %all-to-all-done.4 = f32[12,16,128]{2,1,0:T(8,128)S(1)} async-done(((f32[12,16,128]{2,1,0:T(8,128)}), f32[12,16,128]{2,1,0:T(8,128)S(1)}, u32[]{:S(2)}, u32[]{:S(2)}) %all-to-all-start.4) | async-done | bytes 98336 | tf_op jit(solution)/shard_map/all_to_all | solution.py:233
  120.3 1.0 copy.199
  121.3 12.1 %all-to-all-start.5 = ((f32[64,2,640]{2,1,0:T(2,128)}), f32[64,2,640]{2,1,0:T(2,128)S(1)}, u32[]{:S(2)}, u32[]{:S(2)}) async-start(f32[64,2,640]{2,1,0:T(2,128)} %copy.199), calls=%async_computation.5 | async-start | bytes 655360 | tf_op jit(solution)/shard_map/all_to_all | solution.py:245
  133.4 5.0 %shard_map.116 = f32[192,1024]{1,0:T(8,128)} custom-call(s32[192,1]{1,0:T(8,128)} %broadcast_in_dim_tile.4.st_ref, f32[192,1024]{1,0:T(8,128)} %bitcast.179, f32[192,1024]{1,0:T(8,128)} %bitcast.172, f32[192,1024]{1,0:T(8,128)} %bitcast.170), custom_call_target="tpu_custom_call" | custom-call | tf_op jit(solution)/shard_map/pallas_call | solution.py:104
  138.4 7.9 %all-to-all-done.5 = f32[64,2,640]{2,1,0:T(2,128)S(1)} async-done(((f32[64,2,640]{2,1,0:T(2,128)}), f32[64,2,640]{2,1,0:T(2,128)S(1)}, u32[]{:S(2)}, u32[]{:S(2)}) %all-to-all-start.5) | async-done | bytes 327712 | tf_op jit(solution)/shard_map/all_to_all | solution.py:245
  146.9 1.2 collective-permute-start.14
  148.1 1.5 collective-permute-start.13
  150.0 5.4 %collective-permute-done.14 = f32[49,1024]{1,0:T(8,128)S(1)} collective-permute-done((f32[49,1024]{1,0:T(8,128)S(1)}, f32[49,1024]{1,0:T(8,128)S(1)}, u32[]{:S(2)}, u32[]{:S(2)}) %collective-permute-start.14) | collective-permute-done | bytes 200736 | tf_op jit(solution)/shard_map/ppermute | solution.py:157
  155.4 2.7 %collective-permute-done.13 = f32[49,1024]{1,0:T(8,128)S(1)} collective-permute-done((f32[49,1024]{1,0:T(8,128)S(1)}, f32[49,1024]{1,0:T(8,128)S(1)}, u32[]{:S(2)}, u32[]{:S(2)}) %collective-permute-start.13) | collective-permute-done | bytes 200736 | tf_op jit(solution)/shard_map/ppermute | solution.py:157
  158.2 3.9 %collective-permute-done.12 = f32[49,1024]{1,0:T(8,128)S(1)} collective-permute-done((f32[49,1024]{1,0:T(8,128)S(1)}, f32[49,1024]{1,0:T(8,128)S(1)}, u32[]{:S(2)}, u32[]{:S(2)}) %collective-permute-start.12) | collective-permute-done | bytes 200736 | tf_op jit(solution)/shard_map/ppermute | solution.py:157
  163.7 1.4 fusion
  (108 shorter events, 10.6 us)
Async XLA Ops:
  0.6 14.7 %copy-start = (f32[64,128]{1,0:T(8,128)S(1)}, f32[64,128]{1,0:T(8,128)}, u32[]{:S(2)}) copy-start(f32[64,128]{1,0:T(8,128)} %param.15) | copy-start | bytes 98308
  0.6 6.2 %copy-start.4 = (f32[64,3,1024]{2,0,1:T(8,128)S(1)}, f32[64,3,1024]{2,0,1:T(8,128)}, u32[]{:S(2)}) copy-start(f32[64,3,1024]{2,0,1:T(8,128)} %param.12) | copy-start | bytes 2359300
  0.7 14.7 %collective-permute-start.2 = (f32[3,1,1]{0,2,1:T(1,128)}, f32[3,1,1]{0,2,1:T(1,128)S(1)}, u32[]{:S(2)}, u32[]{:S(2)}) collective-permute-start(f32[3,1,1]{0,2,1:T(1,128)} %bitcast.206), channel_id=1, source_target_pairs={{0,3},{1,0},{2,1},{3,2},{4,7},{5,4},{6,5},{7,6},{8,11},{9,8},{10,9... | collective-permute-start | bytes 44 | tf_op jit(solution)/shard_map/ppermute | solution.py:143
  3.5 11.9 %collective-permute-start.1 = (f32[3,1,1]{0,2,1:T(1,128)}, f32[3,1,1]{0,2,1:T(1,128)S(1)}, u32[]{:S(2)}, u32[]{:S(2)}) collective-permute-start(f32[3,1,1]{0,2,1:T(1,128)} %bitcast.207), channel_id=1, source_target_pairs={{0,2},{1,3},{2,0},{3,1},{4,6},{5,7},{6,4},{7,5},{8,10},{9,11},{10,... | collective-permute-start | bytes 44 | tf_op jit(solution)/shard_map/ppermute | solution.py:143
  4.3 11.1 %collective-permute-start = (f32[3,1,1]{0,2,1:T(1,128)}, f32[3,1,1]{0,2,1:T(1,128)S(1)}, u32[]{:S(2)}, u32[]{:S(2)}) collective-permute-start(f32[3,1,1]{0,2,1:T(1,128)} %bitcast.208), channel_id=1, source_target_pairs={{0,1},{1,2},{2,3},{3,0},{4,5},{5,6},{6,7},{7,4},{8,9},{9,10},{10,1... | collective-permute-start | bytes 44 | tf_op jit(solution)/shard_map/ppermute | solution.py:143
  9.4 3.8 %copy-start.6 = (s32[64]{0:T(128)S(1)}, s32[64]{0:T(128)}, u32[]{:S(2)}) copy-start(s32[64]{0:T(128)} %param.14) | copy-start | bytes 772
  9.4 4.8 %copy-start.7 = (s32[64]{0:T(128)S(1)}, s32[64]{0:T(128)}, u32[]{:S(2)}) copy-start(s32[64]{0:T(128)} %param.19) | copy-start | bytes 772
  9.4 5.2 %copy-start.8 = (s32[64,1]{0,1:T(1,128)S(1)}, s32[64,1]{0,1:T(1,128)}, u32[]{:S(2)}) copy-start(s32[64,1]{0,1:T(1,128)} %param.16) | copy-start | bytes 772
  9.4 5.4 %copy-start.9 = (s32[64]{0:T(128)S(1)}, s32[64]{0:T(128)}, u32[]{:S(2)}) copy-start(s32[64]{0:T(128)} %param.17) | copy-start | bytes 772
  9.4 6.0 %copy-start.5 = (f32[3]{0:T(128)S(1)}, f32[3]{0:T(128)}, u32[]{:S(2)}) copy-start(f32[3]{0:T(128)} %param.18) | copy-start | bytes 40
  9.4 23.8 %all-to-all-start = ((f32[2,3,64,1024]{3,0,1,2:T(2,128)}), f32[2,3,64,1024]{3,0,1,2:T(2,128)S(1)}, u32[]{:S(2)}, u32[]{:S(2)}) async-start(f32[2,3,64,1024]{3,0,1,2:T(2,128)} %copy.176), calls=%async_computation | async-start | bytes 3145728 | tf_op jit(solution)/shard_map/all_to_all | solution.py:130
  35.0 9.5 %copy-start.3 = (f32[2,64,3,1024]{3,1,2,0:T(8,128)S(1)}, f32[2,64,3,1024]{3,1,2,0:T(8,128)}, u32[]{:S(2)}) copy-start(f32[2,64,3,1024]{3,1,2,0:T(8,128)} %param.11) | copy-start | bytes 4718596
  41.3 9.1 %all-to-all-start.1 = ((f32[12,16,128]{2,1,0:T(8,128)}), f32[12,16,128]{2,1,0:T(8,128)S(1)}, u32[]{:S(2)}, u32[]{:S(2)}) async-start(f32[12,16,128]{2,1,0:T(8,128)} %convolution_multiply_fusion.1), calls=%async_computation.1 | async-start | bytes 196608 | tf_op jit(solution)/shard_map/all_to_all | solution.py:233
  45.7 28.6 %collective-permute-start.5 = (f32[2,3,16,1024]{3,2,1,0:T(8,128)}, f32[2,3,16,1024]{3,2,1,0:T(8,128)}, u32[]{:S(2)}, u32[]{:S(2)}) collective-permute-start(f32[2,3,16,1024]{3,2,1,0:T(8,128)} %get-tuple-element.21), channel_id=1, source_target_pairs={{0,3},{1,0},{2,1},{3,2},{4,7},{5,4},{6,5},{7,6},{8,11},{9,8},{10,9... | collective-permute-start | bytes 1179656 | tf_op jit(solution)/shard_map/ppermute | solution.py:143
  48.9 25.4 %collective-permute-start.4 = (f32[2,3,16,1024]{3,2,1,0:T(8,128)}, f32[2,3,16,1024]{3,2,1,0:T(8,128)}, u32[]{:S(2)}, u32[]{:S(2)}) collective-permute-start(f32[2,3,16,1024]{3,2,1,0:T(8,128)} %get-tuple-element.19), channel_id=1, source_target_pairs={{0,2},{1,3},{2,0},{3,1},{4,6},{5,7},{6,4},{7,5},{8,10},{9,11},{10,... | collective-permute-start | bytes 1179656 | tf_op jit(solution)/shard_map/ppermute | solution.py:143
  50.4 22.1 %collective-permute-start.8 = (f32[3,16,1024]{2,1,0:T(8,128)S(1)}, f32[3,16,1024]{2,1,0:T(8,128)S(1)}, u32[]{:S(2)}, u32[]{:S(2)}) collective-permute-start(f32[3,16,1024]{2,1,0:T(8,128)S(1)} %get-tuple-element.34), channel_id=1, source_target_pairs={{0,3},{1,0},{2,1},{3,2},{4,7},{5,4},{6,5},{7,6},{8,11},{9,8},{10,9... | collective-permute-start | bytes 589832 | tf_op jit(solution)/shard_map/ppermute | solution.py:143
  52.2 20.3 %collective-permute-start.7 = (f32[3,16,1024]{2,1,0:T(8,128)S(1)}, f32[3,16,1024]{2,1,0:T(8,128)S(1)}, u32[]{:S(2)}, u32[]{:S(2)}) collective-permute-start(f32[3,16,1024]{2,1,0:T(8,128)S(1)} %get-tuple-element.32), channel_id=1, source_target_pairs={{0,2},{1,3},{2,0},{3,1},{4,6},{5,7},{6,4},{7,5},{8,10},{9,11},{10,... | collective-permute-start | bytes 589832 | tf_op jit(solution)/shard_map/ppermute | solution.py:143
  53.7 18.8 %collective-permute-start.6 = (f32[3,16,1024]{2,1,0:T(8,128)S(1)}, f32[3,16,1024]{2,1,0:T(8,128)S(1)}, u32[]{:S(2)}, u32[]{:S(2)}) collective-permute-start(f32[3,16,1024]{2,1,0:T(8,128)S(1)} %get-tuple-element.33), channel_id=1, source_target_pairs={{0,1},{1,2},{2,3},{3,0},{4,5},{5,6},{6,7},{7,4},{8,9},{9,10},{10,1... | collective-permute-start | bytes 589832 | tf_op jit(solution)/shard_map/ppermute | solution.py:143
  55.5 28.9 %all-to-all-start.2 = ((f32[64,2,512]{2,1,0:T(2,128)}), f32[64,2,512]{2,1,0:T(2,128)}, u32[]{:S(2)}, u32[]{:S(2)}) async-start(f32[64,2,512]{2,1,0:T(2,128)} %pad_maximum_fusion.4), calls=%async_computation.2 | async-start | bytes 524288 | tf_op jit(solution)/shard_map/all_to_all | solution.py:245
  72.5 9.6 %collective-permute-start.3 = (f32[2,3,16,1024]{3,2,1,0:T(8,128)}, f32[2,3,16,1024]{3,2,1,0:T(8,128)S(1)}, u32[]{:S(2)}, u32[]{:S(2)}) collective-permute-start(f32[2,3,16,1024]{3,2,1,0:T(8,128)} %get-tuple-element.20), channel_id=1, source_target_pairs={{0,1},{1,2},{2,3},{3,0},{4,5},{5,6},{6,7},{7,4},{8,9},{9,10},{10,1... | collective-permute-start | bytes 1179656 | tf_op jit(solution)/shard_map/ppermute | solution.py:143
  86.9 9.5 %all-to-all-start.3 = ((f32[3,64,128]{2,0,1:T(4,128)}), f32[3,64,128]{2,0,1:T(4,128)S(1)}, u32[]{:S(2)}, u32[]{:S(2)}) async-start(f32[3,64,128]{2,0,1:T(4,128)} %copy.188), calls=%async_computation.3 | async-start | bytes 262144 | tf_op jit(solution)/shard_map/all_to_all | solution.py:130
  102.9 6.3 %copy-start.1 = (f32[12,16,1024]{2,1,0:T(8,128)S(1)}, f32[12,16,1024]{2,1,0:T(8,128)}, u32[]{:S(2)}) copy-start(f32[12,16,1024]{2,1,0:T(8,128)} %get-tuple-element.12) | copy-start | bytes 2359300
  104.2 9.9 %collective-permute-start.11 = (f32[64,256]{1,0:T(8,128)S(1)}, f32[64,256]{1,0:T(8,128)S(1)}, u32[]{:S(2)}, u32[]{:S(2)}) collective-permute-start(f32[64,256]{1,0:T(8,128)S(1)} %bitcast.201), channel_id=1, source_target_pairs={{0,3},{1,0},{2,1},{3,2},{4,7},{5,4},{6,5},{7,6},{8,11},{9,8},{10,9... | collective-permute-start | bytes 196616 | tf_op jit(solution)/shard_map/ppermute | solution.py:169
  107.5 6.6 %collective-permute-start.10 = (f32[64,256]{1,0:T(8,128)S(1)}, f32[64,256]{1,0:T(8,128)S(1)}, u32[]{:S(2)}, u32[]{:S(2)}) collective-permute-start(f32[64,256]{1,0:T(8,128)S(1)} %bitcast.202), channel_id=1, source_target_pairs={{0,2},{1,3},{2,0},{3,1},{4,6},{5,7},{6,4},{7,5},{8,10},{9,11},{10,... | collective-permute-start | bytes 196616 | tf_op jit(solution)/shard_map/ppermute | solution.py:169
  108.3 6.1 %collective-permute-start.9 = (f32[64,256]{1,0:T(8,128)S(1)}, f32[64,256]{1,0:T(8,128)S(1)}, u32[]{:S(2)}, u32[]{:S(2)}) collective-permute-start(f32[64,256]{1,0:T(8,128)S(1)} %bitcast.203), channel_id=1, source_target_pairs={{0,1},{1,2},{2,3},{3,0},{4,5},{5,6},{6,7},{7,4},{8,9},{9,10},{10,1... | collective-permute-start | bytes 196616 | tf_op jit(solution)/shard_map/ppermute | solution.py:169
  110.4 9.4 %all-to-all-start.4 = ((f32[12,16,128]{2,1,0:T(8,128)}), f32[12,16,128]{2,1,0:T(8,128)S(1)}, u32[]{:S(2)}, u32[]{:S(2)}) async-start(f32[12,16,128]{2,1,0:T(8,128)} %convolution_multiply_fusion), calls=%async_computation.4 | async-start | bytes 196608 | tf_op jit(solution)/shard_map/all_to_all | solution.py:233
  121.3 25.0 %all-to-all-start.5 = ((f32[64,2,640]{2,1,0:T(2,128)}), f32[64,2,640]{2,1,0:T(2,128)S(1)}, u32[]{:S(2)}, u32[]{:S(2)}) async-start(f32[64,2,640]{2,1,0:T(2,128)} %copy.199), calls=%async_computation.5 | async-start | bytes 655360 | tf_op jit(solution)/shard_map/all_to_all | solution.py:245
  138.4 8.4 %copy-start.2 = (f32[192,1024]{1,0:T(8,128)S(1)}, f32[192,1024]{1,0:T(8,128)}, u32[]{:S(2)}) copy-start(f32[192,1024]{1,0:T(8,128)} %shard_map.116) | copy-start | bytes 2359300
  146.9 8.6 %collective-permute-start.14 = (f32[49,1024]{1,0:T(8,128)S(1)}, f32[49,1024]{1,0:T(8,128)S(1)}, u32[]{:S(2)}, u32[]{:S(2)}) collective-permute-start(f32[49,1024]{1,0:T(8,128)S(1)} %get-tuple-element.27), channel_id=1, source_target_pairs={{0,3},{1,0},{2,1},{3,2},{4,7},{5,4},{6,5},{7,6},{8,11},{9,8},{10,9... | collective-permute-start | bytes 602120 | tf_op jit(solution)/shard_map/ppermute | solution.py:157
  148.1 10.0 %collective-permute-start.13 = (f32[49,1024]{1,0:T(8,128)S(1)}, f32[49,1024]{1,0:T(8,128)S(1)}, u32[]{:S(2)}, u32[]{:S(2)}) collective-permute-start(f32[49,1024]{1,0:T(8,128)S(1)} %get-tuple-element.26), channel_id=1, source_target_pairs={{0,2},{1,3},{2,0},{3,1},{4,6},{5,7},{6,4},{7,5},{8,10},{9,11},{10,... | collective-permute-start | bytes 602120 | tf_op jit(solution)/shard_map/ppermute | solution.py:157
  149.6 12.4 %collective-permute-start.12 = (f32[49,1024]{1,0:T(8,128)S(1)}, f32[49,1024]{1,0:T(8,128)S(1)}, u32[]{:S(2)}, u32[]{:S(2)}) collective-permute-start(f32[49,1024]{1,0:T(8,128)S(1)} %get-tuple-element.25), channel_id=1, source_target_pairs={{0,1},{1,2},{2,3},{3,0},{4,5},{5,6},{6,7},{7,4},{8,9},{9,10},{10,1... | collective-permute-start | bytes 602120 | tf_op jit(solution)/shard_map/ppermute | solution.py:157

commit v8 on v6

--- a/solution.py
+++ b/solution.py
@@ -162,9 +162,9 @@
 
 
 def ring_sum(x, lev_index, lev_groups):
-    total = lax.dynamic_index_in_dim(x, lev_index, axis=x.ndim - 2, keepdims=False)
+    total = lax.dynamic_index_in_dim(x, lev_index, axis=0, keepdims=False)
     for shift in range(1, lev_groups):
-        piece = lax.dynamic_index_in_dim(x, (lev_index + shift) % lev_groups, axis=x.ndim - 2, keepdims=False)
+        piece = lax.dynamic_index_in_dim(x, (lev_index + shift) % lev_groups, axis=0, keepdims=False)
         ring = [(src, (src + shift) % lev_groups) for src in range(lev_groups)]
         total = total + lax.ppermute(piece, "lev", ring)
     return total
@@ -237,7 +237,8 @@
         if step_index == 0:
             sent = jnp.concatenate([sent, info], axis=2)
         if step_index == STEPS - 1:
-            quarter = ring_sum(grad_sum.reshape(blocks, lev_groups, cell_count // lev_groups), lev_index, lev_groups)
+            quarter = grad_sum.reshape(blocks, lev_groups, cell_count // lev_groups).transpose(1, 0, 2)
+            quarter = ring_sum(quarter, lev_index, lev_groups)
             tile_sent = jnp.dot(tile_pack, quarter, precision=HI).reshape(peer_count, cap, -1)
             sent = jnp.concatenate([sent, tile_sent], axis=2)
         got = lax.all_to_all(sent, "blk", split_axis=0, concat_axis=0, tiled=True)

time: 155 us -> 155 us (level)
  no operation moved by 1% of the time
where the time goes in v8:
time: 155 us; the launch traced here: 154 us
  starting transfers between devices  69.9 us (45%)
  waiting for transfers between devices  33 us (21%)
  Pallas kernels  17.6 us (11%)
  local copies, waits for them, and re-layouts  17.4 us (11%)
  matrix products  8.16 us (5%)
  other arithmetic  6.97 us (4%)
    all_to_all x2, starting transfers between devices, local(): got = lax.all_to_all(sent, 'blk', split_axis=0, concat_axis=0, tiled=True)  22.6 us
    all_to_all x2, waiting for transfers between devices, to_columns(): lax.all_to_all(x, 'lev', split_axis=x.ndim - 2, concat_axis=x.ndim - 3, t...  16.7 us
    ppermute x9, starting transfers between devices, ring_columns(): piece = lax.ppermute(piece, 'lev', ring)  15.1 us
    ppermute x6, starting transfers between devices, ring_exchange(): piece = lax.ppermute(piece, 'lev', ring)  11.1 us
    pallas_call x2, Pallas kernels, advect(): pl.pallas_call(functools.partial(stencil_kernel, side_len), grid=(rows //...  9.91 us
    ppermute x6, waiting for transfers between devices, ring_exchange(): piece = lax.ppermute(piece, 'lev', ring)  7.86 us
    all_to_all x2, starting transfers between devices, local(): lax.all_to_all(cycle_out, 'lev', split_axis=0, concat_axis=1, tiled=True)  7.49 us
    all_to_all x2, starting transfers between devices, to_columns(): lax.all_to_all(x, 'lev', split_axis=x.ndim - 2, concat_axis=x.ndim - 3, t...  7.35 us
  transfers between devices with their start and end apart: 24, of which 7 were waited for; matrix products, arithmetic and copies ran while one was open for 13% of the time, Pallas kernels for 6%

profile of v8, /device:TPU:8, one launch (start us, length us, event | category | flops | bytes accessed | tf_op | source)
XLA Modules:
  0.0 154.3 jit_solution(9924658588814867457)
XLA Ops:
  0.7 1.6 %collective-permute-start = (f32[3,1,1]{0,2,1:T(1,128)}, f32[3,1,1]{0,2,1:T(1,128)S(1)}, u32[]{:S(2)}, u32[]{:S(2)}) collective-permute-start(f32[3,1,1]{0,2,1:T(1,128)} %bitcast.213), channel_id=1, source_target_pairs={{0,1},{1,2},{2,3},{3,0},{4,5},{5,6},{6,7},{7,4},{8,9},{9,10},{10,1... | collective-permute-start | bytes 44 | tf_op jit(solution)/shard_map/ppermute | solution.py:143
  2.2 2.7 %collective-permute-start.1 = (f32[3,1,1]{0,2,1:T(1,128)}, f32[3,1,1]{0,2,1:T(1,128)S(1)}, u32[]{:S(2)}, u32[]{:S(2)}) collective-permute-start(f32[3,1,1]{0,2,1:T(1,128)} %bitcast.214), channel_id=1, source_target_pairs={{0,2},{1,3},{2,0},{3,1},{4,6},{5,7},{6,4},{7,5},{8,10},{9,11},{10,... | collective-permute-start | bytes 44 | tf_op jit(solution)/shard_map/ppermute | solution.py:143
  5.0 1.4 collective-permute-start.2
  6.4 1.6 %multiply_reduce_fusion = (f32[64,1024]{1,0:T(8,128)S(1)}, f32[1,64,3,1024]{3,1,2,0:T(8,128)S(1)}, f32[3,64,1024]{2,1,0:T(8,128)S(1)}) fusion(f32[64,3,1024]{2,0,1:T(8,128)} %param.12, f32[3]{0:T(128)} %param.20, f32[64,3,1024]{2,0,1:T(8,128)} %param.15), kind=kLoop, calls=%fused_computation.21 | loop fusion | flops 720896 | bytes 3407884 | tf_op jit(solution)/shard_map/reduce_sum | solution.py:201
  8.1 2.4 %copy.180 = f32[2,3,64,1024]{3,0,1,2:T(2,128)} copy(f32[2,3,64,1024]{3,2,1,0:T(8,128)S(1)} %maximum_bitcast_fusion) | data formatting | bytes 3145728 | tf_op jit(solution)/shard_map/transpose | solution.py:196
  10.6 3.7 %all-to-all-start = ((f32[2,3,64,1024]{3,0,1,2:T(2,128)}), f32[2,3,64,1024]{3,0,1,2:T(2,128)S(1)}, u32[]{:S(2)}, u32[]{:S(2)}) async-start(f32[2,3,64,1024]{3,0,1,2:T(2,128)} %copy.180), calls=%async_computation | async-start | bytes 3145728 | tf_op jit(solution)/shard_map/all_to_all | solution.py:130
  14.5 0.7 broadcast_in_dim_tile.4.st_ref
  17.7 16.7 %all-to-all-done = f32[2,3,64,1024]{3,0,1,2:T(2,128)S(1)} async-done(((f32[2,3,64,1024]{3,0,1,2:T(2,128)}), f32[2,3,64,1024]{3,0,1,2:T(2,128)S(1)}, u32[]{:S(2)}, u32[]{:S(2)}) %all-to-all-start) | async-done | bytes 1572896 | tf_op jit(solution)/shard_map/all_to_all | solution.py:130
  34.9 1.3 fusion.62
  36.2 3.7 %shard_map.113 = f32[12,16,1024]{2,1,0:T(8,128)} custom-call(f32[12,16,1024]{2,1,0:T(8,128)} %bitcast.187, f32[12,16,1024]{2,1,0:T(8,128)} %bitcast.172), custom_call_target="tpu_custom_call" | custom-call | tf_op jit(solution)/shard_map/pallas_call | solution.py:62
  39.9 0.9 dynamic-slice_bitcast_fusion.10
  41.4 2.1 %collective-permute-start.7 = (f32[3,16,1024]{2,1,0:T(8,128)}, f32[3,16,1024]{2,1,0:T(8,128)}, u32[]{:S(2)}, u32[]{:S(2)}) collective-permute-start(f32[3,16,1024]{2,1,0:T(8,128)} %get-tuple-element.31), channel_id=1, source_target_pairs={{0,2},{1,3},{2,0},{3,1},{4,6},{5,7},{6,4},{7,5},{8,10},{9,11},{10,... | collective-permute-start | bytes 589832 | tf_op jit(solution)/shard_map/ppermute | solution.py:143
  44.1 1.2 convolution_multiply_fusion.1
  45.3 4.2 %all-to-all-start.1 = ((f32[12,16,128]{2,1,0:T(8,128)}), f32[12,16,128]{2,1,0:T(8,128)S(1)}, u32[]{:S(2)}, u32[]{:S(2)}) async-start(f32[12,16,128]{2,1,0:T(8,128)} %convolution_multiply_fusion.1), calls=%async_computation.1 | async-start | bytes 196608 | tf_op jit(solution)/shard_map/all_to_all | solution.py:234
  49.5 1.1 dynamic-slice_bitcast_fusion.3
  50.5 2.0 %collective-permute-start.3 = (f32[2,3,16,1024]{3,2,1,0:T(8,128)}, f32[2,3,16,1024]{3,2,1,0:T(8,128)S(1)}, u32[]{:S(2)}, u32[]{:S(2)}) collective-permute-start(f32[2,3,16,1024]{3,2,1,0:T(8,128)} %get-tuple-element.19), channel_id=1, source_target_pairs={{0,1},{1,2},{2,3},{3,0},{4,5},{5,6},{6,7},{7,4},{8,9},{9,10},{10,1... | collective-permute-start | bytes 1179656 | tf_op jit(solution)/shard_map/ppermute | solution.py:143
  52.6 2.7 %collective-permute-start.4 = (f32[2,3,16,1024]{3,2,1,0:T(8,128)}, f32[2,3,16,1024]{3,2,1,0:T(8,128)S(1)}, u32[]{:S(2)}, u32[]{:S(2)}) collective-permute-start(f32[2,3,16,1024]{3,2,1,0:T(8,128)} %get-tuple-element.18), channel_id=1, source_target_pairs={{0,2},{1,3},{2,0},{3,1},{4,6},{5,7},{6,4},{7,5},{8,10},{9,11},{10,... | collective-permute-start | bytes 1179656 | tf_op jit(solution)/shard_map/ppermute | solution.py:143
  56.3 0.9 copy.191
  57.2 12.3 %all-to-all-start.2 = ((f32[64,2,512]{2,1,0:T(2,128)}), f32[64,2,512]{2,1,0:T(2,128)}, u32[]{:S(2)}, u32[]{:S(2)}) async-start(f32[64,2,512]{2,1,0:T(2,128)} %copy.191), calls=%async_computation.2 | async-start | bytes 524288 | tf_op jit(solution)/shard_map/all_to_all | solution.py:244
  69.5 1.4 collective-permute-start.5
  70.9 1.2 pad_maximum_fusion.1
  72.7 1.1 broadcast_select_fusion
  73.8 7.3 %collective-permute-done.5 = f32[2,3,16,1024]{3,2,1,0:T(8,128)S(1)} collective-permute-done((f32[2,3,16,1024]{3,2,1,0:T(8,128)}, f32[2,3,16,1024]{3,2,1,0:T(8,128)S(1)}, u32[]{:S(2)}, u32[]{:S(2)}) %collective-permute-start.5) | collective-permute-done | bytes 393248 | tf_op jit(solution)/shard_map/ppermute | solution.py:143
  82.3 1.1 reshape.226
  84.0 0.7 copy.194
  84.8 3.6 %all-to-all-start.3 = ((f32[3,64,128]{2,0,1:T(4,128)}), f32[3,64,128]{2,0,1:T(4,128)S(1)}, u32[]{:S(2)}, u32[]{:S(2)}) async-start(f32[3,64,128]{2,0,1:T(4,128)} %copy.194), calls=%async_computation.3 | async-start | bytes 262144 | tf_op jit(solution)/shard_map/all_to_all | solution.py:130
  88.4 1.3 fusion.61
  89.7 4.9 %shard_map.114 = f32[192,1024]{1,0:T(8,128)} custom-call(s32[192,1]{1,0:T(8,128)} %broadcast_in_dim_tile.4.st_ref, f32[192,1024]{1,0:T(8,128)} %bitcast.174, f32[192,1024]{1,0:T(8,128)} %bitcast.177, f32[192,1024]{1,0:T(8,128)} %bitcast.175), custom_call_target="tpu_custom_call" | custom-call | tf_op jit(solution)/shard_map/pallas_call | solution.py:104
  94.6 2.5 %convolution_add_fusion.1 = f32[192,1024]{1,0:T(8,128)} fusion(f32[192,1024]{1,0:T(8,128)} %shard_map.114, f32[192,128]{1,0:T(8,128)S(1)} %bitcast.197, s32[128]{0:T(128)S(1)} %pad_add_fusion), kind=kOutput, calls=%fused_computation.11 | convolution fusion | flops 302317568 | bytes 1671680 | tf_op jit(solution)/shard_map/dot_general | solution.py:262
  97.2 3.9 %shard_map.115 = (f32[12,16,1024]{2,1,0:T(8,128)}, f32[16,1024]{1,0:T(8,128)}) custom-call(f32[12]{0:T(128)} %reshape.291.ep_ref, f32[12,16,1024]{2,1,0:T(8,128)} %bitcast.182, f32[12,16,1024]{2,1,0:T(8,128)} %bitcast.181, f32[12,16,1024]{2,1,0:T(8,128)} %bitcast.173), custom_call_target="tpu_custom_call" | custom-call | tf_op jit(solution)/shard_map/pallas_call | solution.py:71
  101.1 0.9 add_dynamic-update-slice_fusion
  102.4 2.1 %collective-permute-start.12 = (f32[64,256]{1,0:T(8,128)S(1)}, f32[64,256]{1,0:T(8,128)S(1)}, u32[]{:S(2)}, u32[]{:S(2)}) collective-permute-start(f32[64,256]{1,0:T(8,128)S(1)} %bitcast.206), channel_id=1, source_target_pairs={{0,1},{1,2},{2,3},{3,0},{4,5},{5,6},{6,7},{7,4},{8,9},{9,10},{10,1... | collective-permute-start | bytes 196616 | tf_op jit(solution)/shard_map/ppermute | solution.py:169
  104.5 2.7 %collective-permute-start.13 = (f32[64,256]{1,0:T(8,128)S(1)}, f32[64,256]{1,0:T(8,128)S(1)}, u32[]{:S(2)}, u32[]{:S(2)}) collective-permute-start(f32[64,256]{1,0:T(8,128)S(1)} %bitcast.207), channel_id=1, source_target_pairs={{0,2},{1,3},{2,0},{3,1},{4,6},{5,7},{6,4},{7,5},{8,10},{9,11},{10,... | collective-permute-start | bytes 196616 | tf_op jit(solution)/shard_map/ppermute | solution.py:169
  107.2 1.5 collective-permute-start.14
  108.6 1.2 convolution_multiply_fusion
  109.8 3.3 %all-to-all-start.4 = ((f32[12,16,128]{2,1,0:T(8,128)}), f32[12,16,128]{2,1,0:T(8,128)S(1)}, u32[]{:S(2)}, u32[]{:S(2)}) async-start(f32[12,16,128]{2,1,0:T(8,128)} %convolution_multiply_fusion), calls=%async_computation.4 | async-start | bytes 196608 | tf_op jit(solution)/shard_map/all_to_all | solution.py:234
  113.2 5.0 %shard_map.116 = f32[192,1024]{1,0:T(8,128)} custom-call(s32[192,1]{1,0:T(8,128)} %broadcast_in_dim_tile.4.st_ref, f32[192,1024]{1,0:T(8,128)} %bitcast.186, f32[192,1024]{1,0:T(8,128)} %bitcast.178, f32[192,1024]{1,0:T(8,128)} %bitcast.176), custom_call_target="tpu_custom_call" | custom-call | tf_op jit(solution)/shard_map/pallas_call | solution.py:104
  119.4 1.0 copy.206
  120.4 10.3 %all-to-all-start.5 = ((f32[64,2,640]{2,1,0:T(2,128)}), f32[64,2,640]{2,1,0:T(2,128)S(1)}, u32[]{:S(2)}, u32[]{:S(2)}) async-start(f32[64,2,640]{2,1,0:T(2,128)} %copy.206), calls=%async_computation.5 | async-start | bytes 655360 | tf_op jit(solution)/shard_map/all_to_all | solution.py:244
  130.8 1.6 %collective-permute-start.9 = (f32[3,16,1024]{2,1,0:T(8,128)S(1)}, f32[3,16,1024]{2,1,0:T(8,128)S(1)}, u32[]{:S(2)}, u32[]{:S(2)}) collective-permute-start(f32[3,16,1024]{2,1,0:T(8,128)S(1)} %get-tuple-element.29), channel_id=1, source_target_pairs={{0,1},{1,2},{2,3},{3,0},{4,5},{5,6},{6,7},{7,4},{8,9},{9,10},{10,1... | collective-permute-start | bytes 589832 | tf_op jit(solution)/shard_map/ppermute | solution.py:157
  132.4 2.7 %collective-permute-start.10 = (f32[3,16,1024]{2,1,0:T(8,128)S(1)}, f32[3,16,1024]{2,1,0:T(8,128)S(1)}, u32[]{:S(2)}, u32[]{:S(2)}) collective-permute-start(f32[3,16,1024]{2,1,0:T(8,128)S(1)} %get-tuple-element.28), channel_id=1, source_target_pairs={{0,2},{1,3},{2,0},{3,1},{4,6},{5,7},{6,4},{7,5},{8,10},{9,11},{10,... | collective-permute-start | bytes 589832 | tf_op jit(solution)/shard_map/ppermute | solution.py:157
  135.1 1.5 collective-permute-start.11
  136.5 2.5 %collective-permute-done.9 = f32[3,16,1024]{2,1,0:T(8,128)S(1)} collective-permute-done((f32[3,16,1024]{2,1,0:T(8,128)S(1)}, f32[3,16,1024]{2,1,0:T(8,128)S(1)}, u32[]{:S(2)}, u32[]{:S(2)}) %collective-permute-start.9) | collective-permute-done | bytes 196640 | tf_op jit(solution)/shard_map/ppermute | solution.py:157
  139.0 5.2 %collective-permute-done.10 = f32[3,16,1024]{2,1,0:T(8,128)S(1)} collective-permute-done((f32[3,16,1024]{2,1,0:T(8,128)S(1)}, f32[3,16,1024]{2,1,0:T(8,128)S(1)}, u32[]{:S(2)}, u32[]{:S(2)}) %collective-permute-start.10) | collective-permute-done | bytes 196640 | tf_op jit(solution)/shard_map/ppermute | solution.py:157
  145.7 1.4 collective-permute-start.15
  147.1 2.4 %collective-permute-start.16 = (f32[4,256]{1,0:T(4,128)S(1)}, f32[4,256]{1,0:T(4,128)S(1)}, u32[]{:S(2)}, u32[]{:S(2)}) collective-permute-start(f32[4,256]{1,0:T(4,128)S(1)} %get-tuple-element.40), channel_id=1, source_target_pairs={{0,2},{1,3},{2,0},{3,1},{4,6},{5,7},{6,4},{7,5},{8,10},{9,11},{10,... | collective-permute-start | bytes 12296 | tf_op jit(solution)/shard_map/ppermute | solution.py:157
  149.5 1.6 %collective-permute-start.17 = (f32[4,256]{1,0:T(4,128)S(1)}, f32[4,256]{1,0:T(4,128)S(1)}, u32[]{:S(2)}, u32[]{:S(2)}) collective-permute-start(f32[4,256]{1,0:T(4,128)S(1)} %get-tuple-element.39), channel_id=1, source_target_pairs={{0,3},{1,0},{2,1},{3,2},{4,7},{5,4},{6,5},{7,6},{8,11},{9,8},{10,9... | collective-permute-start | bytes 12296 | tf_op jit(solution)/shard_map/ppermute | solution.py:157
  151.5 1.4 fusion
  (121 shorter events, 12.5 us)
Async XLA Ops:
  0.6 15.7 %copy-start = (f32[64,128]{1,0:T(8,128)S(1)}, f32[64,128]{1,0:T(8,128)}, u32[]{:S(2)}) copy-start(f32[64,128]{1,0:T(8,128)} %param.17) | copy-start | bytes 98308
  0.6 7.4 %copy-start.6 = (f32[64,3,1024]{2,0,1:T(8,128)S(1)}, f32[64,3,1024]{2,0,1:T(8,128)}, u32[]{:S(2)}) copy-start(f32[64,3,1024]{2,0,1:T(8,128)} %param.14) | copy-start | bytes 2359300
  0.7 15.7 %collective-permute-start = (f32[3,1,1]{0,2,1:T(1,128)}, f32[3,1,1]{0,2,1:T(1,128)S(1)}, u32[]{:S(2)}, u32[]{:S(2)}) collective-permute-start(f32[3,1,1]{0,2,1:T(1,128)} %bitcast.213), channel_id=1, source_target_pairs={{0,1},{1,2},{2,3},{3,0},{4,5},{5,6},{6,7},{7,4},{8,9},{9,10},{10,1... | collective-permute-start | bytes 44 | tf_op jit(solution)/shard_map/ppermute | solution.py:143
  2.2 14.2 %collective-permute-start.1 = (f32[3,1,1]{0,2,1:T(1,128)}, f32[3,1,1]{0,2,1:T(1,128)S(1)}, u32[]{:S(2)}, u32[]{:S(2)}) collective-permute-start(f32[3,1,1]{0,2,1:T(1,128)} %bitcast.214), channel_id=1, source_target_pairs={{0,2},{1,3},{2,0},{3,1},{4,6},{5,7},{6,4},{7,5},{8,10},{9,11},{10,... | collective-permute-start | bytes 44 | tf_op jit(solution)/shard_map/ppermute | solution.py:143
  5.0 11.4 %collective-permute-start.2 = (f32[3,1,1]{0,2,1:T(1,128)}, f32[3,1,1]{0,2,1:T(1,128)S(1)}, u32[]{:S(2)}, u32[]{:S(2)}) collective-permute-start(f32[3,1,1]{0,2,1:T(1,128)} %bitcast.215), channel_id=1, source_target_pairs={{0,3},{1,0},{2,1},{3,2},{4,7},{5,4},{6,5},{7,6},{8,11},{9,8},{10,9... | collective-permute-start | bytes 44 | tf_op jit(solution)/shard_map/ppermute | solution.py:143
  10.5 3.9 %copy-start.8 = (s32[64]{0:T(128)S(1)}, s32[64]{0:T(128)}, u32[]{:S(2)}) copy-start(s32[64]{0:T(128)} %param.16) | copy-start | bytes 772
  10.5 4.7 %copy-start.9 = (s32[64,1]{0,1:T(1,128)S(1)}, s32[64,1]{0,1:T(1,128)}, u32[]{:S(2)}) copy-start(s32[64,1]{0,1:T(1,128)} %param.18) | copy-start | bytes 772
  10.5 4.9 %copy-start.10 = (s32[64]{0:T(128)S(1)}, s32[64]{0:T(128)}, u32[]{:S(2)}) copy-start(s32[64]{0:T(128)} %param.21) | copy-start | bytes 772
  10.5 5.2 %copy-start.11 = (s32[64]{0:T(128)S(1)}, s32[64]{0:T(128)}, u32[]{:S(2)}) copy-start(s32[64]{0:T(128)} %param.19) | copy-start | bytes 772
  10.5 5.9 %copy-start.7 = (f32[3]{0:T(128)S(1)}, f32[3]{0:T(128)}, u32[]{:S(2)}) copy-start(f32[3]{0:T(128)} %param.20) | copy-start | bytes 40
  10.6 23.8 %all-to-all-start = ((f32[2,3,64,1024]{3,0,1,2:T(2,128)}), f32[2,3,64,1024]{3,0,1,2:T(2,128)S(1)}, u32[]{:S(2)}, u32[]{:S(2)}) async-start(f32[2,3,64,1024]{3,0,1,2:T(2,128)} %copy.180), calls=%async_computation | async-start | bytes 3145728 | tf_op jit(solution)/shard_map/all_to_all | solution.py:130
  39.9 4.2 %copy-start.1 = (f32[12,16,1024]{2,1,0:T(8,128)S(1)}, f32[12,16,1024]{2,1,0:T(8,128)}, u32[]{:S(2)}) copy-start(f32[12,16,1024]{2,1,0:T(8,128)} %shard_map.113) | copy-start | bytes 2359300
  39.9 9.6 %copy-start.4 = (f32[2,64,3,1024]{3,1,2,0:T(8,128)S(1)}, f32[2,64,3,1024]{3,1,2,0:T(8,128)}, u32[]{:S(2)}) copy-start(f32[2,64,3,1024]{3,1,2,0:T(8,128)} %param.13) | copy-start | bytes 4718596
  40.8 28.6 %collective-permute-start.6 = (f32[3,16,1024]{2,1,0:T(8,128)}, f32[3,16,1024]{2,1,0:T(8,128)}, u32[]{:S(2)}, u32[]{:S(2)}) collective-permute-start(f32[3,16,1024]{2,1,0:T(8,128)} %get-tuple-element.32), channel_id=1, source_target_pairs={{0,1},{1,2},{2,3},{3,0},{4,5},{5,6},{6,7},{7,4},{8,9},{9,10},{10,1... | collective-permute-start | bytes 589832 | tf_op jit(solution)/shard_map/ppermute | solution.py:143
  41.4 29.5 %collective-permute-start.7 = (f32[3,16,1024]{2,1,0:T(8,128)}, f32[3,16,1024]{2,1,0:T(8,128)}, u32[]{:S(2)}, u32[]{:S(2)}) collective-permute-start(f32[3,16,1024]{2,1,0:T(8,128)} %get-tuple-element.31), channel_id=1, source_target_pairs={{0,2},{1,3},{2,0},{3,1},{4,6},{5,7},{6,4},{7,5},{8,10},{9,11},{10,... | collective-permute-start | bytes 589832 | tf_op jit(solution)/shard_map/ppermute | solution.py:143
  43.5 27.5 %collective-permute-start.8 = (f32[3,16,1024]{2,1,0:T(8,128)}, f32[3,16,1024]{2,1,0:T(8,128)}, u32[]{:S(2)}, u32[]{:S(2)}) collective-permute-start(f32[3,16,1024]{2,1,0:T(8,128)} %get-tuple-element.33), channel_id=1, source_target_pairs={{0,3},{1,0},{2,1},{3,2},{4,7},{5,4},{6,5},{7,6},{8,11},{9,8},{10,9... | collective-permute-start | bytes 589832 | tf_op jit(solution)/shard_map/ppermute | solution.py:143
  45.3 10.5 %all-to-all-start.1 = ((f32[12,16,128]{2,1,0:T(8,128)}), f32[12,16,128]{2,1,0:T(8,128)S(1)}, u32[]{:S(2)}, u32[]{:S(2)}) async-start(f32[12,16,128]{2,1,0:T(8,128)} %convolution_multiply_fusion.1), calls=%async_computation.1 | async-start | bytes 196608 | tf_op jit(solution)/shard_map/all_to_all | solution.py:234
  50.5 20.4 %copy-start.5 = (f32[1,3,16,1024]{3,2,1,0:T(8,128)S(1)}, f32[1,3,16,1024]{3,2,1,0:T(8,128)}, u32[]{:S(2)}) copy-start(f32[1,3,16,1024]{3,2,1,0:T(8,128)} %get-tuple-element.30) | copy-start | bytes 589828
  50.5 23.2 %collective-permute-start.3 = (f32[2,3,16,1024]{3,2,1,0:T(8,128)}, f32[2,3,16,1024]{3,2,1,0:T(8,128)S(1)}, u32[]{:S(2)}, u32[]{:S(2)}) collective-permute-start(f32[2,3,16,1024]{3,2,1,0:T(8,128)} %get-tuple-element.19), channel_id=1, source_target_pairs={{0,1},{1,2},{2,3},{3,0},{4,5},{5,6},{6,7},{7,4},{8,9},{9,10},{10,1... | collective-permute-start | bytes 1179656 | tf_op jit(solution)/shard_map/ppermute | solution.py:143
  52.6 21.2 %collective-permute-start.4 = (f32[2,3,16,1024]{3,2,1,0:T(8,128)}, f32[2,3,16,1024]{3,2,1,0:T(8,128)S(1)}, u32[]{:S(2)}, u32[]{:S(2)}) collective-permute-start(f32[2,3,16,1024]{3,2,1,0:T(8,128)} %get-tuple-element.18), channel_id=1, source_target_pairs={{0,2},{1,3},{2,0},{3,1},{4,6},{5,7},{6,4},{7,5},{8,10},{9,11},{10,... | collective-permute-start | bytes 1179656 | tf_op jit(solution)/shard_map/ppermute | solution.py:143
  57.2 25.1 %all-to-all-start.2 = ((f32[64,2,512]{2,1,0:T(2,128)}), f32[64,2,512]{2,1,0:T(2,128)}, u32[]{:S(2)}, u32[]{:S(2)}) async-start(f32[64,2,512]{2,1,0:T(2,128)} %copy.191), calls=%async_computation.2 | async-start | bytes 524288 | tf_op jit(solution)/shard_map/all_to_all | solution.py:244
  69.5 11.6 %collective-permute-start.5 = (f32[2,3,16,1024]{3,2,1,0:T(8,128)}, f32[2,3,16,1024]{3,2,1,0:T(8,128)S(1)}, u32[]{:S(2)}, u32[]{:S(2)}) collective-permute-start(f32[2,3,16,1024]{3,2,1,0:T(8,128)} %get-tuple-element.20), channel_id=1, source_target_pairs={{0,3},{1,0},{2,1},{3,2},{4,7},{5,4},{6,5},{7,6},{8,11},{9,8},{10,9... | collective-permute-start | bytes 1179656 | tf_op jit(solution)/shard_map/ppermute | solution.py:143
  84.8 9.8 %all-to-all-start.3 = ((f32[3,64,128]{2,0,1:T(4,128)}), f32[3,64,128]{2,0,1:T(4,128)S(1)}, u32[]{:S(2)}, u32[]{:S(2)}) async-start(f32[3,64,128]{2,0,1:T(4,128)} %copy.194), calls=%async_computation.3 | async-start | bytes 262144 | tf_op jit(solution)/shard_map/all_to_all | solution.py:130
  101.1 7.6 %copy-start.3 = (f32[12,16,1024]{2,1,0:T(8,128)S(1)}, f32[12,16,1024]{2,1,0:T(8,128)}, u32[]{:S(2)}) copy-start(f32[12,16,1024]{2,1,0:T(8,128)} %get-tuple-element.11) | copy-start | bytes 2359300
  102.4 15.7 %collective-permute-start.12 = (f32[64,256]{1,0:T(8,128)S(1)}, f32[64,256]{1,0:T(8,128)S(1)}, u32[]{:S(2)}, u32[]{:S(2)}) collective-permute-start(f32[64,256]{1,0:T(8,128)S(1)} %bitcast.206), channel_id=1, source_target_pairs={{0,1},{1,2},{2,3},{3,0},{4,5},{5,6},{6,7},{7,4},{8,9},{9,10},{10,1... | collective-permute-start | bytes 196616 | tf_op jit(solution)/shard_map/ppermute | solution.py:169
  104.5 13.6 %collective-permute-start.13 = (f32[64,256]{1,0:T(8,128)S(1)}, f32[64,256]{1,0:T(8,128)S(1)}, u32[]{:S(2)}, u32[]{:S(2)}) collective-permute-start(f32[64,256]{1,0:T(8,128)S(1)} %bitcast.207), channel_id=1, source_target_pairs={{0,2},{1,3},{2,0},{3,1},{4,6},{5,7},{6,4},{7,5},{8,10},{9,11},{10,... | collective-permute-start | bytes 196616 | tf_op jit(solution)/shard_map/ppermute | solution.py:169
  107.2 10.9 %collective-permute-start.14 = (f32[64,256]{1,0:T(8,128)S(1)}, f32[64,256]{1,0:T(8,128)S(1)}, u32[]{:S(2)}, u32[]{:S(2)}) collective-permute-start(f32[64,256]{1,0:T(8,128)S(1)} %bitcast.208), channel_id=1, source_target_pairs={{0,3},{1,0},{2,1},{3,2},{4,7},{5,4},{6,5},{7,6},{8,11},{9,8},{10,9... | collective-permute-start | bytes 196616 | tf_op jit(solution)/shard_map/ppermute | solution.py:169
  109.8 9.1 %all-to-all-start.4 = ((f32[12,16,128]{2,1,0:T(8,128)}), f32[12,16,128]{2,1,0:T(8,128)S(1)}, u32[]{:S(2)}, u32[]{:S(2)}) async-start(f32[12,16,128]{2,1,0:T(8,128)} %convolution_multiply_fusion), calls=%async_computation.4 | async-start | bytes 196608 | tf_op jit(solution)/shard_map/all_to_all | solution.py:234
  118.4 12.3 %copy-start.2 = (f32[192,1024]{1,0:T(8,128)S(1)}, f32[192,1024]{1,0:T(8,128)}, u32[]{:S(2)}) copy-start(f32[192,1024]{1,0:T(8,128)} %shard_map.116) | copy-start | bytes 2359300
  120.4 24.8 %all-to-all-start.5 = ((f32[64,2,640]{2,1,0:T(2,128)}), f32[64,2,640]{2,1,0:T(2,128)S(1)}, u32[]{:S(2)}, u32[]{:S(2)}) async-start(f32[64,2,640]{2,1,0:T(2,128)} %copy.206), calls=%async_computation.5 | async-start | bytes 655360 | tf_op jit(solution)/shard_map/all_to_all | solution.py:244
  130.8 8.2 %collective-permute-start.9 = (f32[3,16,1024]{2,1,0:T(8,128)S(1)}, f32[3,16,1024]{2,1,0:T(8,128)S(1)}, u32[]{:S(2)}, u32[]{:S(2)}) collective-permute-start(f32[3,16,1024]{2,1,0:T(8,128)S(1)} %get-tuple-element.29), channel_id=1, source_target_pairs={{0,1},{1,2},{2,3},{3,0},{4,5},{5,6},{6,7},{7,4},{8,9},{9,10},{10,1... | collective-permute-start | bytes 589832 | tf_op jit(solution)/shard_map/ppermute | solution.py:157
  132.4 11.8 %collective-permute-start.10 = (f32[3,16,1024]{2,1,0:T(8,128)S(1)}, f32[3,16,1024]{2,1,0:T(8,128)S(1)}, u32[]{:S(2)}, u32[]{:S(2)}) collective-permute-start(f32[3,16,1024]{2,1,0:T(8,128)S(1)} %get-tuple-element.28), channel_id=1, source_target_pairs={{0,2},{1,3},{2,0},{3,1},{4,6},{5,7},{6,4},{7,5},{8,10},{9,11},{10,... | collective-permute-start | bytes 589832 | tf_op jit(solution)/shard_map/ppermute | solution.py:157
  135.1 9.1 %collective-permute-start.11 = (f32[3,16,1024]{2,1,0:T(8,128)S(1)}, f32[3,16,1024]{2,1,0:T(8,128)S(1)}, u32[]{:S(2)}, u32[]{:S(2)}) collective-permute-start(f32[3,16,1024]{2,1,0:T(8,128)S(1)} %get-tuple-element.27), channel_id=1, source_target_pairs={{0,3},{1,0},{2,1},{3,2},{4,7},{5,4},{6,5},{7,6},{8,11},{9,8},{10,9... | collective-permute-start | bytes 589832 | tf_op jit(solution)/shard_map/ppermute | solution.py:157
  145.7 7.2 %collective-permute-start.15 = (f32[4,256]{1,0:T(4,128)S(1)}, f32[4,256]{1,0:T(4,128)S(1)}, u32[]{:S(2)}, u32[]{:S(2)}) collective-permute-start(f32[4,256]{1,0:T(4,128)S(1)} %get-tuple-element.41), channel_id=1, source_target_pairs={{0,1},{1,2},{2,3},{3,0},{4,5},{5,6},{6,7},{7,4},{8,9},{9,10},{10,1... | collective-permute-start | bytes 12296 | tf_op jit(solution)/shard_map/ppermute | solution.py:157
  147.1 5.8 %collective-permute-start.16 = (f32[4,256]{1,0:T(4,128)S(1)}, f32[4,256]{1,0:T(4,128)S(1)}, u32[]{:S(2)}, u32[]{:S(2)}) collective-permute-start(f32[4,256]{1,0:T(4,128)S(1)} %get-tuple-element.40), channel_id=1, source_target_pairs={{0,2},{1,3},{2,0},{3,1},{4,6},{5,7},{6,4},{7,5},{8,10},{9,11},{10,... | collective-permute-start | bytes 12296 | tf_op jit(solution)/shard_map/ppermute | solution.py:157
  149.5 3.6 %collective-permute-start.17 = (f32[4,256]{1,0:T(4,128)S(1)}, f32[4,256]{1,0:T(4,128)S(1)}, u32[]{:S(2)}, u32[]{:S(2)}) collective-permute-start(f32[4,256]{1,0:T(4,128)S(1)} %get-tuple-element.39), channel_id=1, source_target_pairs={{0,3},{1,0},{2,1},{3,2},{4,7},{5,4},{6,5},{7,6},{8,11},{9,8},{10,9... | collective-permute-start | bytes 12296 | tf_op jit(solution)/shard_map/ppermute | solution.py:157
